TPU v7x, 32 devices: a whole 2x2x4 slice. The times are simulated.
32 devices in a mesh: seq: 16 (over z, y, core), mp: 2 (over x).
Axes of the slice: x: 2, y: 2, z: 4, core: 2. Of those that a mesh axis runs over, the one named last changes fastest.
Arguments:
- tokens: bfloat16 [4096, 2048], P('seq'), may hold values from -25 to 25
- lengths: int32 [32], replicated, may hold values from 1 to 1024, 4096 in all
- prefix_cache: bfloat16 [4, 2048, 512], P(None, 'seq'), may hold values from -1000 to 1000
- attn_gain: bfloat16 [2048], replicated, may hold values from 0.25 to 1.75
- w_query: bfloat16 [2048, 2048], P(None, 'mp'), may hold values from -0.25 to 0.25
- w_keyval: bfloat16 [2048, 512], replicated, may hold values from -0.125 to 0.125
- w_out: bfloat16 [2048, 2048], P('mp'), may hold values from -0.25 to 0.25
- final_gain: bfloat16 [2048], replicated, may hold values from 0.25 to 1.75
- w_head: bfloat16 [2048, 32000], P(None, ('seq', 'mp')), may hold values from -0.4375 to 0.4375
Outputs:
- hidden: bfloat16 [4096, 2048], P('seq', 'mp')
- suffix_cache: bfloat16 [4096, 512], P('seq')
- last_normed: bfloat16 [32, 2048], replicated
- greatest: float32 [32], replicated
Inputs may be any that keep to these rules, and one draw needn't show every extreme that they name: The lengths sum to 4096 and one of them equals 1024.
All inputs are finite; a program needn't handle non-finite values.
Results may differ from a plain program's by a relative error of at most 0.013.
Values may be sent and summed in bfloat16 or wider, within the bound.
No kernel may reach another device: no remote copies, remote signals or barrier semaphores. Data moves between devices by JAX's collectives and lax.ppermute only.
A program may use at most 64 MiB of HBM per device.

v0:
```python
import math

import jax
import jax.numpy as jnp
from jax import lax
from jax.sharding import PartitionSpec as P

QH = 32
KVH = 4
HD = 64
G = 4
RPG = 8
P_SIZE = 2048


epsilon = 1e-05


def passed_along(block, axis, distance):
    devices = range(lax.axis_size(axis))
    route = [((i - distance) % len(devices), i) for i in devices]
    return lax.ppermute(block, axis, route)


def rotate(source, places, head_count):
    half_dim = HD // 2
    row_count = source.shape[0]
    reshaped = source.reshape(row_count, head_count, HD)
    frequency = 10000.0 ** (-(jnp.arange(half_dim, dtype=jnp.float32) * 2.0 / HD))
    angles = places.astype(jnp.float32)[:, None] * frequency[None, :]
    cos_table = jnp.cos(angles)[:, None, :]
    sine_table = jnp.sin(angles)[:, None, :]
    leading = reshaped[..., :half_dim]
    second = reshaped[..., half_dim:]
    joined = jnp.concatenate(
        [leading * cos_table - second * sine_table, second * cos_table + leading * sine_table], -1
    )
    return joined.reshape(row_count, head_count * HD)


def attend(running, queries, kv_block, allowed):
    old_max, old_sum, numerator = running
    half_width = kv_block.shape[1] // 2
    kv_heads = queries.shape[1]
    key_rows = kv_block[:, :half_width].reshape(kv_block.shape[0], kv_heads, HD)
    val_rows = kv_block[:, half_width:].reshape(kv_block.shape[0], kv_heads, HD)
    scores = jnp.einsum("qgrd,ngd->grqn", queries, key_rows, preferred_element_type=jnp.float32) * (
        1.0 / math.sqrt(HD)
    )
    scores = jnp.where(allowed[None, None], scores, -jnp.inf)
    new_max = jnp.maximum(old_max, jnp.max(scores, -1))
    factor = jnp.exp(old_max - new_max)
    weights = jnp.exp(scores - new_max[..., None])
    new_sum = old_sum * factor + jnp.sum(weights, -1)
    numerator = numerator * factor[..., None] + jnp.einsum(
        "grqn,ngd->grqd", weights.astype(jnp.bfloat16), val_rows, preferred_element_type=jnp.float32
    )
    return (new_max, new_sum, numerator)


def suffix_allowed(source_dev, token_rows, request, position, request_end):
    key_place = source_dev * token_rows + jnp.arange(token_rows, dtype=jnp.int32)
    key_request = jnp.sum((key_place[:, None] >= request_end[None, :]).astype(jnp.int32), 1)
    return (
        (request[:, None] == key_request[None, :])
        & (key_place[None, :] <= position[:, None])
        & (source_dev >= 0)
    )


def prefix_allowed(group_of, row_count):
    key_group = (
        jnp.arange(G, dtype=jnp.int32)[:, None] + jnp.zeros((1, row_count), jnp.int32)
    ).reshape(-1)
    return group_of[:, None] == key_group[None, :]


def per_device(
    tokens, lengths, prefix_cache, attn_gain, w_query, w_keyval, w_out, final_gain, w_head
):
    token_rows = tokens.shape[0]
    model_width = tokens.shape[1]
    seq_devices = lax.axis_size("seq")
    seq_index = lax.axis_index("seq")
    mp_index = lax.axis_index("mp")
    part_width = model_width // lax.axis_size("mp")
    query_heads = w_query.shape[1] // HD
    group_size = QH // KVH
    kv_heads = max(1, query_heads // group_size)
    repeat_count = query_heads // kv_heads
    kv_first = mp_index * query_heads // group_size
    kv_width = KVH * HD
    request_count = lengths.shape[0]
    activations = tokens.astype(jnp.float32)
    normed = (
        activations
        * lax.rsqrt(jnp.mean(activations * activations, -1, keepdims=True) + epsilon)
        * attn_gain.astype(jnp.float32)
    ).astype(jnp.bfloat16)
    request_end = jnp.cumsum(lengths)
    starts = request_end - lengths
    position = seq_index * token_rows + jnp.arange(token_rows, dtype=jnp.int32)
    request = jnp.sum((position[:, None] >= request_end[None, :]).astype(jnp.int32), 1)
    request_table = request[:, None] == jnp.arange(request_count, dtype=jnp.int32)[None, :]
    offset = position - jnp.sum(jnp.where(request_table, starts[None, :], 0), 1)
    group_of = request // RPG
    query_full = jnp.dot(normed, w_query, preferred_element_type=jnp.float32)
    keyval = jnp.dot(normed, w_keyval, preferred_element_type=jnp.float32)
    queries = (
        rotate(query_full, P_SIZE + offset, query_heads)
        .astype(jnp.bfloat16)
        .reshape(token_rows, kv_heads, repeat_count, HD)
    )
    key_rows = rotate(keyval[:, :kv_width], P_SIZE + offset, KVH).astype(jnp.bfloat16)
    val_rows = keyval[:, kv_width:].astype(jnp.bfloat16)
    suffix_cache = jnp.concatenate([key_rows, val_rows], 1)
    own_suffix = jnp.concatenate(
        [
            lax.dynamic_slice_in_dim(key_rows, kv_first * HD, kv_heads * HD, 1),
            lax.dynamic_slice_in_dim(val_rows, kv_first * HD, kv_heads * HD, 1),
        ],
        1,
    )
    own_prefix = jnp.concatenate(
        [
            lax.dynamic_slice_in_dim(prefix_cache, kv_first * HD, kv_heads * HD, 2),
            lax.dynamic_slice_in_dim(prefix_cache, kv_width + kv_first * HD, kv_heads * HD, 2),
        ],
        2,
    )
    prefix_rows = own_prefix.shape[1]
    block_width = own_prefix.shape[2]
    running = (
        jnp.full((kv_heads, repeat_count, token_rows), -1e30, jnp.float32),
        jnp.zeros((kv_heads, repeat_count, token_rows), jnp.float32),
        jnp.zeros((kv_heads, repeat_count, token_rows, HD), jnp.float32),
    )
    prefix_mask = prefix_allowed(group_of, prefix_rows)
    running = attend(
        running, queries, own_prefix.reshape(G * prefix_rows, block_width), prefix_mask
    )
    running = attend(
        running,
        queries,
        own_suffix,
        suffix_allowed(seq_index, token_rows, request, position, request_end),
    )

    def cycle_hop(hop_count, loop_state):
        state_now, prefix_block, suffix_block = loop_state
        prefix_block, suffix_block = passed_along((prefix_block, suffix_block), "seq", 1)
        source_dev = (seq_index - hop_count) % seq_devices
        state_now = attend(
            state_now, queries, prefix_block.reshape(G * prefix_rows, block_width), prefix_mask
        )
        state_now = attend(
            state_now,
            queries,
            suffix_block,
            suffix_allowed(source_dev, token_rows, request, position, request_end),
        )
        return (state_now, prefix_block, suffix_block)

    running, unused_prefix, unused_suffix = lax.fori_loop(
        1, seq_devices, cycle_hop, (running, own_prefix, own_suffix)
    )
    final_max, final_sum, numerator = running
    context = numerator / final_sum[..., None]
    context = (
        jnp.transpose(context, (2, 0, 1, 3))
        .reshape(token_rows, query_heads * HD)
        .astype(jnp.bfloat16)
    )
    mixture = jnp.dot(context, w_out, preferred_element_type=jnp.float32)
    mixture = lax.psum_scatter(
        mixture.astype(jnp.bfloat16), "mp", scatter_dimension=1, tiled=True
    ).astype(jnp.float32)
    own_columns = lax.dynamic_slice_in_dim(activations, mp_index * part_width, part_width, 1)
    hidden = (own_columns + mixture).astype(jnp.bfloat16)
    local_last = request_end - 1 - seq_index * token_rows
    onehot = (local_last[:, None] == jnp.arange(token_rows, dtype=jnp.int32)[None, :]).astype(
        jnp.bfloat16
    )
    last_part = jnp.dot(onehot, hidden, preferred_element_type=jnp.float32)
    canvas = lax.dynamic_update_slice_in_dim(
        jnp.zeros((request_count, model_width), jnp.float32), last_part, mp_index * part_width, 1
    )
    last_rows = lax.psum(canvas, ("seq", "mp"))
    inv_rms = lax.rsqrt(jnp.mean(last_rows * last_rows, -1, keepdims=True) + epsilon)
    last_normed = (last_rows * final_gain.astype(jnp.float32) * inv_rms).astype(jnp.bfloat16)
    logits = jnp.dot(last_normed, w_head, preferred_element_type=jnp.float32)
    greatest = lax.pmax(jnp.max(logits, -1), ("seq", "mp"))
    return (hidden, suffix_cache, last_normed, greatest)


def solution(mesh):
    return jax.shard_map(
        per_device,
        mesh=mesh,
        in_specs=(
            P("seq", None),
            P(),
            P(None, "seq", None),
            P(),
            P(None, "mp"),
            P(),
            P("mp", None),
            P(),
            P(None, ("seq", "mp")),
        ),
        out_specs=(P("seq", "mp"), P("seq", None), P(), P()),
        check_vma=False,
    )
```

profile of v0, /device:TPU:0, one launch (start us, length us, event | category | flops | bytes accessed | tf_op | source)
XLA Modules:
  0.0 527.1 jit_solution(17378786312400722219)
XLA Ops:
  20.0 4.0 fusion.51
  33.5 2.3 fusion.47
  38.0 280.5 %while.24 = (s32[]{:T(128)}, f32[2,8,256]{2,1,0:T(8,128)S(1)}, f32[2,8,256]{2,1,0:T(8,128)S(1)}, f32[2,8,256,64]{2,3,1,0:T(8,128)}, bf16[4,128,256]{1,0,2:T(4,12...) while((s32[]{:T(128)}, f32[2,8,256]{2,1,0:T(8,128)S(1)}, ...), condition=%wide.region_14.15_spmd.clone, body=%wide.region_8.14_spmd.clone.sunk | while | flops 841392384 | bytes 52473384 | solution.py:164
  38.5 2.6 collective-permute-start.1
  41.6 4.6 collective-permute-done
  58.2 6.6 %collective-permute-done = bf16[256,256]{0,1:T(8,128)(2,1)S(1)} collective-permute-done((bf16[256,256]{0,1:T(8,128)(2,1)S(1)}, bf16[256,256]{0,1:T(8,128)(2,1)S(1)}, u32[]{:S(2)}, u32[]{:S(2)}) %collective-permute-start) | collective-permute-done | bytes 131104 | tf_op jit(solution)/shard_map/while/body/eval_jaxpr/ppermute | solution.py:22
  76.9 6.6 %collective-permute-done = bf16[256,256]{0,1:T(8,128)(2,1)S(1)} collective-permute-done((bf16[256,256]{0,1:T(8,128)(2,1)S(1)}, bf16[256,256]{0,1:T(8,128)(2,1)S(1)}, u32[]{:S(2)}, u32[]{:S(2)}) %collective-permute-start) | collective-permute-done | bytes 131104 | tf_op jit(solution)/shard_map/while/body/eval_jaxpr/ppermute | solution.py:22
  95.5 6.6 %collective-permute-done = bf16[256,256]{0,1:T(8,128)(2,1)S(1)} collective-permute-done((bf16[256,256]{0,1:T(8,128)(2,1)S(1)}, bf16[256,256]{0,1:T(8,128)(2,1)S(1)}, u32[]{:S(2)}, u32[]{:S(2)}) %collective-permute-start) | collective-permute-done | bytes 131104 | tf_op jit(solution)/shard_map/while/body/eval_jaxpr/ppermute | solution.py:22
  114.1 6.6 %collective-permute-done = bf16[256,256]{0,1:T(8,128)(2,1)S(1)} collective-permute-done((bf16[256,256]{0,1:T(8,128)(2,1)S(1)}, bf16[256,256]{0,1:T(8,128)(2,1)S(1)}, u32[]{:S(2)}, u32[]{:S(2)}) %collective-permute-start) | collective-permute-done | bytes 131104 | tf_op jit(solution)/shard_map/while/body/eval_jaxpr/ppermute | solution.py:22
  132.8 6.6 %collective-permute-done = bf16[256,256]{0,1:T(8,128)(2,1)S(1)} collective-permute-done((bf16[256,256]{0,1:T(8,128)(2,1)S(1)}, bf16[256,256]{0,1:T(8,128)(2,1)S(1)}, u32[]{:S(2)}, u32[]{:S(2)}) %collective-permute-start) | collective-permute-done | bytes 131104 | tf_op jit(solution)/shard_map/while/body/eval_jaxpr/ppermute | solution.py:22
  151.4 6.6 %collective-permute-done = bf16[256,256]{0,1:T(8,128)(2,1)S(1)} collective-permute-done((bf16[256,256]{0,1:T(8,128)(2,1)S(1)}, bf16[256,256]{0,1:T(8,128)(2,1)S(1)}, u32[]{:S(2)}, u32[]{:S(2)}) %collective-permute-start) | collective-permute-done | bytes 131104 | tf_op jit(solution)/shard_map/while/body/eval_jaxpr/ppermute | solution.py:22
  170.0 6.6 %collective-permute-done = bf16[256,256]{0,1:T(8,128)(2,1)S(1)} collective-permute-done((bf16[256,256]{0,1:T(8,128)(2,1)S(1)}, bf16[256,256]{0,1:T(8,128)(2,1)S(1)}, u32[]{:S(2)}, u32[]{:S(2)}) %collective-permute-start) | collective-permute-done | bytes 131104 | tf_op jit(solution)/shard_map/while/body/eval_jaxpr/ppermute | solution.py:22
  188.7 6.6 %collective-permute-done = bf16[256,256]{0,1:T(8,128)(2,1)S(1)} collective-permute-done((bf16[256,256]{0,1:T(8,128)(2,1)S(1)}, bf16[256,256]{0,1:T(8,128)(2,1)S(1)}, u32[]{:S(2)}, u32[]{:S(2)}) %collective-permute-start) | collective-permute-done | bytes 131104 | tf_op jit(solution)/shard_map/while/body/eval_jaxpr/ppermute | solution.py:22
  207.3 6.6 %collective-permute-done = bf16[256,256]{0,1:T(8,128)(2,1)S(1)} collective-permute-done((bf16[256,256]{0,1:T(8,128)(2,1)S(1)}, bf16[256,256]{0,1:T(8,128)(2,1)S(1)}, u32[]{:S(2)}, u32[]{:S(2)}) %collective-permute-start) | collective-permute-done | bytes 131104 | tf_op jit(solution)/shard_map/while/body/eval_jaxpr/ppermute | solution.py:22
  225.9 6.6 %collective-permute-done = bf16[256,256]{0,1:T(8,128)(2,1)S(1)} collective-permute-done((bf16[256,256]{0,1:T(8,128)(2,1)S(1)}, bf16[256,256]{0,1:T(8,128)(2,1)S(1)}, u32[]{:S(2)}, u32[]{:S(2)}) %collective-permute-start) | collective-permute-done | bytes 131104 | tf_op jit(solution)/shard_map/while/body/eval_jaxpr/ppermute | solution.py:22
  244.6 6.6 %collective-permute-done = bf16[256,256]{0,1:T(8,128)(2,1)S(1)} collective-permute-done((bf16[256,256]{0,1:T(8,128)(2,1)S(1)}, bf16[256,256]{0,1:T(8,128)(2,1)S(1)}, u32[]{:S(2)}, u32[]{:S(2)}) %collective-permute-start) | collective-permute-done | bytes 131104 | tf_op jit(solution)/shard_map/while/body/eval_jaxpr/ppermute | solution.py:22
  263.2 6.6 %collective-permute-done = bf16[256,256]{0,1:T(8,128)(2,1)S(1)} collective-permute-done((bf16[256,256]{0,1:T(8,128)(2,1)S(1)}, bf16[256,256]{0,1:T(8,128)(2,1)S(1)}, u32[]{:S(2)}, u32[]{:S(2)}) %collective-permute-start) | collective-permute-done | bytes 131104 | tf_op jit(solution)/shard_map/while/body/eval_jaxpr/ppermute | solution.py:22
  281.9 6.6 %collective-permute-done = bf16[256,256]{0,1:T(8,128)(2,1)S(1)} collective-permute-done((bf16[256,256]{0,1:T(8,128)(2,1)S(1)}, bf16[256,256]{0,1:T(8,128)(2,1)S(1)}, u32[]{:S(2)}, u32[]{:S(2)}) %collective-permute-start) | collective-permute-done | bytes 131104 | tf_op jit(solution)/shard_map/while/body/eval_jaxpr/ppermute | solution.py:22
  300.5 6.6 %collective-permute-done = bf16[256,256]{0,1:T(8,128)(2,1)S(1)} collective-permute-done((bf16[256,256]{0,1:T(8,128)(2,1)S(1)}, bf16[256,256]{0,1:T(8,128)(2,1)S(1)}, u32[]{:S(2)}, u32[]{:S(2)}) %collective-permute-start) | collective-permute-done | bytes 131104 | tf_op jit(solution)/shard_map/while/body/eval_jaxpr/ppermute | solution.py:22
  319.9 4.5 convolution_convert_fusion
  326.1 16.5 %reduce-scatter.2.cloned.1.call-done = bf16[256,1024]{1,0:T(8,128)(2,1)} async-done(((bf16[256,2048]{1,0:T(8,128)(2,1)}), bf16[256,1024]{1,0:T(8,128)(2,1)}) %reduce-scatter.2.cloned.1.call-update) | async-done | bytes 524304 | tf_op jit(solution)/shard_map/reduce_scatter | solution.py:175
  345.2 129.4 %all-reduce.2.cloned.1.call-done = f32[32,2048]{1,0:T(8,128)} async-done(((f32[32,2048]{1,0:T(8,128)}), f32[32,2048]{1,0:T(8,128)}) %all-reduce.2.cloned.1.call-update) | async-done | bytes 262160 | tf_op jit(solution)/shard_map/psum | solution.py:188
  476.7 3.6 convolution_reduce_fusion
  481.1 39.2 %pmax.7 = f32[32]{0:T(128)} all-reduce(f32[32]{0:T(128)S(1)} %convolution_reduce_fusion), channel_id=1, replica_groups=mesh['seq'=16,'mp'=2] {'seq','mp'}, use_global_device_ids=true, to_apply=%region_19.20 | all-reduce | flops 32 | bytes 256 | tf_op jit(solution)/shard_map/pmax | solution.py:192
  (483 shorter events, 211.0 us)
Async XLA Ops:
  7.2 335.4 %reduce-scatter.2.cloned.1.call-start = ((), (), s32[]{:S(2)}) async-start(), calls=%async_computation.1 | async-start | bytes 1572864 | tf_op jit(solution)/shard_map/reduce_scatter | solution.py:175
  38.0 8.1 %collective-permute-start = (bf16[256,256]{0,1:T(8,128)(2,1)S(1)}, bf16[256,256]{0,1:T(8,128)(2,1)S(1)}, u32[]{:S(2)}, u32[]{:S(2)}) collective-permute-start(bf16[256,256]{0,1:T(8,128)(2,1)S(1)} %get-tuple-element.555), channel_id=1, source_target_pairs={{30,0},{0,2},{2,4},{4,6},{6,8},{8,10},{10,12},{12,14},{14,16},{16,... | collective-permute-start | bytes 393224 | tf_op jit(solution)/shard_map/while/body/eval_jaxpr/ppermute | solution.py:22
  38.5 10.4 %collective-permute-start.1 = (bf16[4,128,256]{1,0,2:T(4,128)(2,1)S(1)}, bf16[4,128,256]{1,0,2:T(4,128)(2,1)S(1)}, u32[]{:S(2)}, u32[]{:S(2)}) collective-permute-start(bf16[4,128,256]{1,0,2:T(4,128)(2,1)S(1)} %get-tuple-element.554), channel_id=1, source_target_pairs={{30,0},{0,2},{2,4},{4,6},{6,8},{8,10},{10,12},{12,14},{14,16},{16,... | collective-permute-start | bytes 786440 | tf_op jit(solution)/shard_map/while/body/eval_jaxpr/ppermute | solution.py:22
  57.7 7.1 %collective-permute-start = (bf16[256,256]{0,1:T(8,128)(2,1)S(1)}, bf16[256,256]{0,1:T(8,128)(2,1)S(1)}, u32[]{:S(2)}, u32[]{:S(2)}) collective-permute-start(bf16[256,256]{0,1:T(8,128)(2,1)S(1)} %get-tuple-element.555), channel_id=1, source_target_pairs={{30,0},{0,2},{2,4},{4,6},{6,8},{8,10},{10,12},{12,14},{14,16},{16,... | collective-permute-start | bytes 393224 | tf_op jit(solution)/shard_map/while/body/eval_jaxpr/ppermute | solution.py:22
  57.7 9.9 %collective-permute-start.1 = (bf16[4,128,256]{1,0,2:T(4,128)(2,1)S(1)}, bf16[4,128,256]{1,0,2:T(4,128)(2,1)S(1)}, u32[]{:S(2)}, u32[]{:S(2)}) collective-permute-start(bf16[4,128,256]{1,0,2:T(4,128)(2,1)S(1)} %get-tuple-element.554), channel_id=1, source_target_pairs={{30,0},{0,2},{2,4},{4,6},{6,8},{8,10},{10,12},{12,14},{14,16},{16,... | collective-permute-start | bytes 786440 | tf_op jit(solution)/shard_map/while/body/eval_jaxpr/ppermute | solution.py:22
  76.3 7.1 %collective-permute-start = (bf16[256,256]{0,1:T(8,128)(2,1)S(1)}, bf16[256,256]{0,1:T(8,128)(2,1)S(1)}, u32[]{:S(2)}, u32[]{:S(2)}) collective-permute-start(bf16[256,256]{0,1:T(8,128)(2,1)S(1)} %get-tuple-element.555), channel_id=1, source_target_pairs={{30,0},{0,2},{2,4},{4,6},{6,8},{8,10},{10,12},{12,14},{14,16},{16,... | collective-permute-start | bytes 393224 | tf_op jit(solution)/shard_map/while/body/eval_jaxpr/ppermute | solution.py:22
  76.4 9.9 %collective-permute-start.1 = (bf16[4,128,256]{1,0,2:T(4,128)(2,1)S(1)}, bf16[4,128,256]{1,0,2:T(4,128)(2,1)S(1)}, u32[]{:S(2)}, u32[]{:S(2)}) collective-permute-start(bf16[4,128,256]{1,0,2:T(4,128)(2,1)S(1)} %get-tuple-element.554), channel_id=1, source_target_pairs={{30,0},{0,2},{2,4},{4,6},{6,8},{8,10},{10,12},{12,14},{14,16},{16,... | collective-permute-start | bytes 786440 | tf_op jit(solution)/shard_map/while/body/eval_jaxpr/ppermute | solution.py:22
  94.9 7.1 %collective-permute-start = (bf16[256,256]{0,1:T(8,128)(2,1)S(1)}, bf16[256,256]{0,1:T(8,128)(2,1)S(1)}, u32[]{:S(2)}, u32[]{:S(2)}) collective-permute-start(bf16[256,256]{0,1:T(8,128)(2,1)S(1)} %get-tuple-element.555), channel_id=1, source_target_pairs={{30,0},{0,2},{2,4},{4,6},{6,8},{8,10},{10,12},{12,14},{14,16},{16,... | collective-permute-start | bytes 393224 | tf_op jit(solution)/shard_map/while/body/eval_jaxpr/ppermute | solution.py:22
  95.0 9.9 %collective-permute-start.1 = (bf16[4,128,256]{1,0,2:T(4,128)(2,1)S(1)}, bf16[4,128,256]{1,0,2:T(4,128)(2,1)S(1)}, u32[]{:S(2)}, u32[]{:S(2)}) collective-permute-start(bf16[4,128,256]{1,0,2:T(4,128)(2,1)S(1)} %get-tuple-element.554), channel_id=1, source_target_pairs={{30,0},{0,2},{2,4},{4,6},{6,8},{8,10},{10,12},{12,14},{14,16},{16,... | collective-permute-start | bytes 786440 | tf_op jit(solution)/shard_map/while/body/eval_jaxpr/ppermute | solution.py:22
  113.6 7.1 %collective-permute-start = (bf16[256,256]{0,1:T(8,128)(2,1)S(1)}, bf16[256,256]{0,1:T(8,128)(2,1)S(1)}, u32[]{:S(2)}, u32[]{:S(2)}) collective-permute-start(bf16[256,256]{0,1:T(8,128)(2,1)S(1)} %get-tuple-element.555), channel_id=1, source_target_pairs={{30,0},{0,2},{2,4},{4,6},{6,8},{8,10},{10,12},{12,14},{14,16},{16,... | collective-permute-start | bytes 393224 | tf_op jit(solution)/shard_map/while/body/eval_jaxpr/ppermute | solution.py:22
  113.6 9.9 %collective-permute-start.1 = (bf16[4,128,256]{1,0,2:T(4,128)(2,1)S(1)}, bf16[4,128,256]{1,0,2:T(4,128)(2,1)S(1)}, u32[]{:S(2)}, u32[]{:S(2)}) collective-permute-start(bf16[4,128,256]{1,0,2:T(4,128)(2,1)S(1)} %get-tuple-element.554), channel_id=1, source_target_pairs={{30,0},{0,2},{2,4},{4,6},{6,8},{8,10},{10,12},{12,14},{14,16},{16,... | collective-permute-start | bytes 786440 | tf_op jit(solution)/shard_map/while/body/eval_jaxpr/ppermute | solution.py:22
  132.2 7.1 %collective-permute-start = (bf16[256,256]{0,1:T(8,128)(2,1)S(1)}, bf16[256,256]{0,1:T(8,128)(2,1)S(1)}, u32[]{:S(2)}, u32[]{:S(2)}) collective-permute-start(bf16[256,256]{0,1:T(8,128)(2,1)S(1)} %get-tuple-element.555), channel_id=1, source_target_pairs={{30,0},{0,2},{2,4},{4,6},{6,8},{8,10},{10,12},{12,14},{14,16},{16,... | collective-permute-start | bytes 393224 | tf_op jit(solution)/shard_map/while/body/eval_jaxpr/ppermute | solution.py:22
  132.3 9.9 %collective-permute-start.1 = (bf16[4,128,256]{1,0,2:T(4,128)(2,1)S(1)}, bf16[4,128,256]{1,0,2:T(4,128)(2,1)S(1)}, u32[]{:S(2)}, u32[]{:S(2)}) collective-permute-start(bf16[4,128,256]{1,0,2:T(4,128)(2,1)S(1)} %get-tuple-element.554), channel_id=1, source_target_pairs={{30,0},{0,2},{2,4},{4,6},{6,8},{8,10},{10,12},{12,14},{14,16},{16,... | collective-permute-start | bytes 786440 | tf_op jit(solution)/shard_map/while/body/eval_jaxpr/ppermute | solution.py:22
  150.8 7.1 %collective-permute-start = (bf16[256,256]{0,1:T(8,128)(2,1)S(1)}, bf16[256,256]{0,1:T(8,128)(2,1)S(1)}, u32[]{:S(2)}, u32[]{:S(2)}) collective-permute-start(bf16[256,256]{0,1:T(8,128)(2,1)S(1)} %get-tuple-element.555), channel_id=1, source_target_pairs={{30,0},{0,2},{2,4},{4,6},{6,8},{8,10},{10,12},{12,14},{14,16},{16,... | collective-permute-start | bytes 393224 | tf_op jit(solution)/shard_map/while/body/eval_jaxpr/ppermute | solution.py:22
  150.9 9.9 %collective-permute-start.1 = (bf16[4,128,256]{1,0,2:T(4,128)(2,1)S(1)}, bf16[4,128,256]{1,0,2:T(4,128)(2,1)S(1)}, u32[]{:S(2)}, u32[]{:S(2)}) collective-permute-start(bf16[4,128,256]{1,0,2:T(4,128)(2,1)S(1)} %get-tuple-element.554), channel_id=1, source_target_pairs={{30,0},{0,2},{2,4},{4,6},{6,8},{8,10},{10,12},{12,14},{14,16},{16,... | collective-permute-start | bytes 786440 | tf_op jit(solution)/shard_map/while/body/eval_jaxpr/ppermute | solution.py:22
  169.5 9.9 %collective-permute-start.1 = (bf16[4,128,256]{1,0,2:T(4,128)(2,1)S(1)}, bf16[4,128,256]{1,0,2:T(4,128)(2,1)S(1)}, u32[]{:S(2)}, u32[]{:S(2)}) collective-permute-start(bf16[4,128,256]{1,0,2:T(4,128)(2,1)S(1)} %get-tuple-element.554), channel_id=1, source_target_pairs={{30,0},{0,2},{2,4},{4,6},{6,8},{8,10},{10,12},{12,14},{14,16},{16,... | collective-permute-start | bytes 786440 | tf_op jit(solution)/shard_map/while/body/eval_jaxpr/ppermute | solution.py:22
  188.2 9.9 %collective-permute-start.1 = (bf16[4,128,256]{1,0,2:T(4,128)(2,1)S(1)}, bf16[4,128,256]{1,0,2:T(4,128)(2,1)S(1)}, u32[]{:S(2)}, u32[]{:S(2)}) collective-permute-start(bf16[4,128,256]{1,0,2:T(4,128)(2,1)S(1)} %get-tuple-element.554), channel_id=1, source_target_pairs={{30,0},{0,2},{2,4},{4,6},{6,8},{8,10},{10,12},{12,14},{14,16},{16,... | collective-permute-start | bytes 786440 | tf_op jit(solution)/shard_map/while/body/eval_jaxpr/ppermute | solution.py:22
  206.8 9.9 %collective-permute-start.1 = (bf16[4,128,256]{1,0,2:T(4,128)(2,1)S(1)}, bf16[4,128,256]{1,0,2:T(4,128)(2,1)S(1)}, u32[]{:S(2)}, u32[]{:S(2)}) collective-permute-start(bf16[4,128,256]{1,0,2:T(4,128)(2,1)S(1)} %get-tuple-element.554), channel_id=1, source_target_pairs={{30,0},{0,2},{2,4},{4,6},{6,8},{8,10},{10,12},{12,14},{14,16},{16,... | collective-permute-start | bytes 786440 | tf_op jit(solution)/shard_map/while/body/eval_jaxpr/ppermute | solution.py:22
  225.4 9.9 %collective-permute-start.1 = (bf16[4,128,256]{1,0,2:T(4,128)(2,1)S(1)}, bf16[4,128,256]{1,0,2:T(4,128)(2,1)S(1)}, u32[]{:S(2)}, u32[]{:S(2)}) collective-permute-start(bf16[4,128,256]{1,0,2:T(4,128)(2,1)S(1)} %get-tuple-element.554), channel_id=1, source_target_pairs={{30,0},{0,2},{2,4},{4,6},{6,8},{8,10},{10,12},{12,14},{14,16},{16,... | collective-permute-start | bytes 786440 | tf_op jit(solution)/shard_map/while/body/eval_jaxpr/ppermute | solution.py:22
  244.1 9.9 %collective-permute-start.1 = (bf16[4,128,256]{1,0,2:T(4,128)(2,1)S(1)}, bf16[4,128,256]{1,0,2:T(4,128)(2,1)S(1)}, u32[]{:S(2)}, u32[]{:S(2)}) collective-permute-start(bf16[4,128,256]{1,0,2:T(4,128)(2,1)S(1)} %get-tuple-element.554), channel_id=1, source_target_pairs={{30,0},{0,2},{2,4},{4,6},{6,8},{8,10},{10,12},{12,14},{14,16},{16,... | collective-permute-start | bytes 786440 | tf_op jit(solution)/shard_map/while/body/eval_jaxpr/ppermute | solution.py:22
  262.7 9.9 %collective-permute-start.1 = (bf16[4,128,256]{1,0,2:T(4,128)(2,1)S(1)}, bf16[4,128,256]{1,0,2:T(4,128)(2,1)S(1)}, u32[]{:S(2)}, u32[]{:S(2)}) collective-permute-start(bf16[4,128,256]{1,0,2:T(4,128)(2,1)S(1)} %get-tuple-element.554), channel_id=1, source_target_pairs={{30,0},{0,2},{2,4},{4,6},{6,8},{8,10},{10,12},{12,14},{14,16},{16,... | collective-permute-start | bytes 786440 | tf_op jit(solution)/shard_map/while/body/eval_jaxpr/ppermute | solution.py:22
  281.4 9.9 %collective-permute-start.1 = (bf16[4,128,256]{1,0,2:T(4,128)(2,1)S(1)}, bf16[4,128,256]{1,0,2:T(4,128)(2,1)S(1)}, u32[]{:S(2)}, u32[]{:S(2)}) collective-permute-start(bf16[4,128,256]{1,0,2:T(4,128)(2,1)S(1)} %get-tuple-element.554), channel_id=1, source_target_pairs={{30,0},{0,2},{2,4},{4,6},{6,8},{8,10},{10,12},{12,14},{14,16},{16,... | collective-permute-start | bytes 786440 | tf_op jit(solution)/shard_map/while/body/eval_jaxpr/ppermute | solution.py:22
  300.0 9.9 %collective-permute-start.1 = (bf16[4,128,256]{1,0,2:T(4,128)(2,1)S(1)}, bf16[4,128,256]{1,0,2:T(4,128)(2,1)S(1)}, u32[]{:S(2)}, u32[]{:S(2)}) collective-permute-start(bf16[4,128,256]{1,0,2:T(4,128)(2,1)S(1)} %get-tuple-element.554), channel_id=1, source_target_pairs={{30,0},{0,2},{2,4},{4,6},{6,8},{8,10},{10,12},{12,14},{14,16},{16,... | collective-permute-start | bytes 786440 | tf_op jit(solution)/shard_map/while/body/eval_jaxpr/ppermute | solution.py:22
  324.5 150.1 %all-reduce.2.cloned.1.call-start = ((), (), s32[]{:S(2)}) async-start(), calls=%async_computation.2 | async-start | bytes 524288 | tf_op jit(solution)/shard_map/psum | solution.py:188
  (56 other events, 733.8 us)
Sparse Core Ops, SparseCore 0:
  324.6 17.9 reduce-scatter.1
  349.6 124.9 all-reduce.1
where the time goes:
time: 528 us; the launch traced here: 527 us
  waiting for transfers between devices  272 us (52%)
  matrix products  117 us (22%)
  other arithmetic  60.6 us (11%)
  blocking collectives  39.2 us (7%)
  local copies, waits for them, and re-layouts  15.9 us (3%)
  between operations  14.7 us (3%)
    psum x1, waiting for transfers between devices, per_device(): last_rows = lax.psum(canvas, ('seq', 'mp'))  129 us
    ppermute x30, waiting for transfers between devices, passed_along(): return lax.ppermute(block, axis, route)  126 us
    dot_general x32, matrix products, attend(): jnp.einsum('grqn,ngd->grqd', weights.astype(jnp.bfloat16), val_rows, pref...  67.5 us
    reduce_sum x32, other arithmetic, attend(): new_sum = old_sum * factor + jnp.sum(weights, -1)  40.8 us
    pmax x1, blocking collectives, per_device(): greatest = lax.pmax(jnp.max(logits, -1), ('seq', 'mp'))  39.2 us
    dot_general x32, matrix products, attend(): jnp.einsum('qgrd,ngd->grqn', queries, key_rows, preferred_element_type=jn...  35.1 us
    reduce_scatter x1, waiting for transfers between devices, per_device(): lax.psum_scatter(mixture.astype(jnp.bfloat16), 'mp', scatter_dimension=1,...  16.5 us
  transfers between devices with their start and end apart: 32, of which 32 were waited for; matrix products, arithmetic and copies ran while one was open for 4% of the time, Pallas kernels for 0%

commit v1 on v0

--- a/solution.py
+++ b/solution.py
@@ -11,15 +11,11 @@
 G = 4
 RPG = 8
 P_SIZE = 2048
+MOST = 1024
+PREFIX_CHUNK = 512
 
 
 epsilon = 1e-05
-
-
-def passed_along(block, axis, distance):
-    devices = range(lax.axis_size(axis))
-    route = [((i - distance) % len(devices), i) for i in devices]
-    return lax.ppermute(block, axis, route)
 
 
 def rotate(source, places, head_count):
@@ -58,21 +54,10 @@
     return (new_max, new_sum, numerator)
 
 
-def suffix_allowed(source_dev, token_rows, request, position, request_end):
-    key_place = source_dev * token_rows + jnp.arange(token_rows, dtype=jnp.int32)
-    key_request = jnp.sum((key_place[:, None] >= request_end[None, :]).astype(jnp.int32), 1)
-    return (
-        (request[:, None] == key_request[None, :])
-        & (key_place[None, :] <= position[:, None])
-        & (source_dev >= 0)
-    )
-
-
-def prefix_allowed(group_of, row_count):
-    key_group = (
-        jnp.arange(G, dtype=jnp.int32)[:, None] + jnp.zeros((1, row_count), jnp.int32)
-    ).reshape(-1)
-    return group_of[:, None] == key_group[None, :]
+def shifted_back(block, axis, distance):
+    count = lax.axis_size(axis)
+    route = [(i, i + distance) for i in range(count - distance)]
+    return lax.ppermute(block, axis, route)
 
 
 def per_device(
@@ -91,6 +76,19 @@
     kv_first = mp_index * query_heads // group_size
     kv_width = KVH * HD
     request_count = lengths.shape[0]
+    back_blocks = min(seq_devices - 1, -(-(MOST - 1) // token_rows))
+
+    own_prefix = jnp.concatenate(
+        [
+            lax.dynamic_slice_in_dim(prefix_cache, kv_first * HD, kv_heads * HD, 2),
+            lax.dynamic_slice_in_dim(prefix_cache, kv_width + kv_first * HD, kv_heads * HD, 2),
+        ],
+        2,
+    )
+    prefix_rows = own_prefix.shape[1]
+    block_width = own_prefix.shape[2]
+    all_prefix = lax.all_gather(own_prefix, "seq", axis=0)
+
     activations = tokens.astype(jnp.float32)
     normed = (
         activations
@@ -104,13 +102,7 @@
     request_table = request[:, None] == jnp.arange(request_count, dtype=jnp.int32)[None, :]
     offset = position - jnp.sum(jnp.where(request_table, starts[None, :], 0), 1)
     group_of = request // RPG
-    query_full = jnp.dot(normed, w_query, preferred_element_type=jnp.float32)
     keyval = jnp.dot(normed, w_keyval, preferred_element_type=jnp.float32)
-    queries = (
-        rotate(query_full, P_SIZE + offset, query_heads)
-        .astype(jnp.bfloat16)
-        .reshape(token_rows, kv_heads, repeat_count, HD)
-    )
     key_rows = rotate(keyval[:, :kv_width], P_SIZE + offset, KVH).astype(jnp.bfloat16)
     val_rows = keyval[:, kv_width:].astype(jnp.bfloat16)
     suffix_cache = jnp.concatenate([key_rows, val_rows], 1)
@@ -121,49 +113,63 @@
         ],
         1,
     )
-    own_prefix = jnp.concatenate(
-        [
-            lax.dynamic_slice_in_dim(prefix_cache, kv_first * HD, kv_heads * HD, 2),
-            lax.dynamic_slice_in_dim(prefix_cache, kv_width + kv_first * HD, kv_heads * HD, 2),
-        ],
-        2,
-    )
-    prefix_rows = own_prefix.shape[1]
-    block_width = own_prefix.shape[2]
+    earlier = [own_suffix] + [
+        shifted_back(own_suffix, "seq", distance) for distance in range(1, back_blocks + 1)
+    ]
+    suffix_window = jnp.stack(earlier, 0)
+
+    query_full = jnp.dot(normed, w_query, preferred_element_type=jnp.float32)
+    queries = (
+        rotate(query_full, P_SIZE + offset, query_heads)
+        .astype(jnp.bfloat16)
+        .reshape(token_rows, kv_heads, repeat_count, HD)
+    )
+
     running = (
         jnp.full((kv_heads, repeat_count, token_rows), -1e30, jnp.float32),
         jnp.zeros((kv_heads, repeat_count, token_rows), jnp.float32),
         jnp.zeros((kv_heads, repeat_count, token_rows, HD), jnp.float32),
     )
-    prefix_mask = prefix_allowed(group_of, prefix_rows)
-    running = attend(
-        running, queries, own_prefix.reshape(G * prefix_rows, block_width), prefix_mask
-    )
-    running = attend(
-        running,
-        queries,
-        own_suffix,
-        suffix_allowed(seq_index, token_rows, request, position, request_end),
-    )
-
-    def cycle_hop(hop_count, loop_state):
-        state_now, prefix_block, suffix_block = loop_state
-        prefix_block, suffix_block = passed_along((prefix_block, suffix_block), "seq", 1)
-        source_dev = (seq_index - hop_count) % seq_devices
-        state_now = attend(
-            state_now, queries, prefix_block.reshape(G * prefix_rows, block_width), prefix_mask
+
+    sources_per_chunk = max(1, PREFIX_CHUNK // prefix_rows)
+    chunks_per_group = seq_devices // sources_per_chunk
+    first_group = group_of[0]
+    last_group = group_of[token_rows - 1]
+
+    def prefix_step(chunk, state_now):
+        group = chunk // chunks_per_group
+        part = chunk % chunks_per_group
+        block = lax.dynamic_slice(
+            all_prefix,
+            (part * sources_per_chunk, group, 0, 0),
+            (sources_per_chunk, 1, prefix_rows, block_width),
+        ).reshape(sources_per_chunk * prefix_rows, block_width)
+        allowed = jnp.broadcast_to(
+            (group_of == group)[:, None], (token_rows, sources_per_chunk * prefix_rows)
         )
-        state_now = attend(
-            state_now,
-            queries,
-            suffix_block,
-            suffix_allowed(source_dev, token_rows, request, position, request_end),
+        return attend(state_now, queries, block, allowed)
+
+    running = lax.fori_loop(
+        first_group * chunks_per_group, (last_group + 1) * chunks_per_group, prefix_step, running
+    )
+
+    first_block = starts[request[0]] // token_rows
+    back_needed = jnp.minimum(seq_index - first_block, back_blocks)
+
+    def suffix_step(distance, state_now):
+        source_dev = seq_index - distance
+        key_place = source_dev * token_rows + jnp.arange(token_rows, dtype=jnp.int32)
+        key_request = jnp.sum((key_place[:, None] >= request_end[None, :]).astype(jnp.int32), 1)
+        allowed = (
+            (request[:, None] == key_request[None, :])
+            & (key_place[None, :] <= position[:, None])
+            & (source_dev >= 0)
         )
-        return (state_now, prefix_block, suffix_block)
-
-    running, unused_prefix, unused_suffix = lax.fori_loop(
-        1, seq_devices, cycle_hop, (running, own_prefix, own_suffix)
-    )
+        block = lax.dynamic_index_in_dim(suffix_window, distance, 0, keepdims=False)
+        return attend(state_now, queries, block, allowed)
+
+    running = lax.fori_loop(0, back_needed + 1, suffix_step, running)
+
     final_max, final_sum, numerator = running
     context = numerator / final_sum[..., None]
     context = (
@@ -181,11 +187,9 @@
     onehot = (local_last[:, None] == jnp.arange(token_rows, dtype=jnp.int32)[None, :]).astype(
         jnp.bfloat16
     )
-    last_part = jnp.dot(onehot, hidden, preferred_element_type=jnp.float32)
-    canvas = lax.dynamic_update_slice_in_dim(
-        jnp.zeros((request_count, model_width), jnp.float32), last_part, mp_index * part_width, 1
-    )
-    last_rows = lax.psum(canvas, ("seq", "mp"))
+    last_part = jnp.dot(onehot, hidden, preferred_element_type=jnp.float32).astype(jnp.bfloat16)
+    last_part = lax.psum(last_part, "seq")
+    last_rows = lax.all_gather(last_part, "mp", axis=1, tiled=True).astype(jnp.float32)
     inv_rms = lax.rsqrt(jnp.mean(last_rows * last_rows, -1, keepdims=True) + epsilon)
     last_normed = (last_rows * final_gain.astype(jnp.float32) * inv_rms).astype(jnp.bfloat16)
     logits = jnp.dot(last_normed, w_head, preferred_element_type=jnp.float32)

time: 528 us -> 350 us (0.66)
  waiting for transfers between devices: 272 us -> 172 us
  matrix products: 117 us -> 48.3 us
  other arithmetic: 60.6 us -> 19.6 us
  local copies, waits for them, and re-layouts: 15.9 us -> 26.9 us
  starting transfers between devices: 4.83 us -> 15.5 us
  blocking collectives: 39.2 us -> 46.9 us
    ppermute x30 -> x4, waiting for transfers between devices: 126 us -> 0.01 us  [shifted_back(): return lax.ppermute(block, axis, route)]
    reduce_scatter x1, waiting for transfers between devices: 16.5 us -> 71.7 us  [per_device(): lax.psum_scatter(mixture.astype(jnp.bfloat16), 'mp', scatter_dimension=1,...]
    psum x1, waiting for transfers between devices: 129 us -> 86.5 us  [per_device(): last_part = lax.psum(last_part, 'seq')]
    dot_general x32 -> x5, matrix products: 67.5 us -> 27.2 us  [attend(): jnp.einsum('grqn,ngd->grqd', weights.astype(jnp.bfloat16), val_rows, pref...]
    reduce_sum x32 -> x5, other arithmetic: 40.8 us -> 7.48 us  [attend(): new_sum = old_sum * factor + jnp.sum(weights, -1)]
    dot_general x32 -> x5, matrix products: 35.1 us -> 5.99 us  [attend(): jnp.einsum('qgrd,ngd->grqn', queries, key_rows, preferred_element_type=jn...]
    all_gather x0 -> x1, waiting for transfers between devices: none -> 13.9 us  [per_device(): all_prefix = lax.all_gather(own_prefix, 'seq', axis=0)]
    ppermute x30 -> x4, starting transfers between devices: 4.76 us -> 15.3 us  [shifted_back(): return lax.ppermute(block, axis, route)]
  transfers between devices with their start and end apart: 32 -> 7, of which waited for: 32 -> 3; matrix products, arithmetic and copies ran while one was open for 4% -> 7% of each run, Pallas kernels for 0% -> 0%
where the time goes in v1:
time: 350 us; the launch traced here: 349 us
  waiting for transfers between devices  172 us (49%)
  matrix products  48.3 us (14%)
  blocking collectives  46.9 us (13%)
  local copies, waits for them, and re-layouts  26.9 us (8%)
  between operations  19.7 us (6%)
  other arithmetic  19.6 us (6%)
  starting transfers between devices  15.5 us (4%)
    psum x1, waiting for transfers between devices, per_device(): last_part = lax.psum(last_part, 'seq')  86.5 us
    reduce_scatter x1, waiting for transfers between devices, per_device(): lax.psum_scatter(mixture.astype(jnp.bfloat16), 'mp', scatter_dimension=1,...  71.7 us
    pmax x1, blocking collectives, per_device(): greatest = lax.pmax(jnp.max(logits, -1), ('seq', 'mp'))  41.7 us
    dot_general x5, matrix products, attend(): jnp.einsum('grqn,ngd->grqd', weights.astype(jnp.bfloat16), val_rows, pref...  27.2 us
    ppermute x4, starting transfers between devices, shifted_back(): return lax.ppermute(block, axis, route)  15.3 us
    all_gather x1, waiting for transfers between devices, per_device(): all_prefix = lax.all_gather(own_prefix, 'seq', axis=0)  13.9 us
    while x25, local copies, waits for them, and re-layouts  8.14 us
    reduce_sum x5, other arithmetic, attend(): new_sum = old_sum * factor + jnp.sum(weights, -1)  7.48 us
  transfers between devices with their start and end apart: 7, of which 3 were waited for; matrix products, arithmetic and copies ran while one was open for 7% of the time, Pallas kernels for 0%

profile of v1, /device:TPU:0, one launch (start us, length us, event | category | flops | bytes accessed | tf_op | source)
XLA Modules:
  0.0 349.3 jit_solution(14837220267693971893)
XLA Ops:
  11.6 2.0 fusion.24
  19.5 3.0 collective-permute-start
  22.5 4.4 %collective-permute-start.1 = (bf16[256,256]{1,0:T(8,128)(2,1)}, bf16[256,256]{1,0:T(8,128)(2,1)}, u32[]{:S(2)}, u32[]{:S(2)}) collective-permute-start(bf16[256,256]{1,0:T(8,128)(2,1)} %pad_maximum_fusion.4), channel_id=1, source_target_pairs={{0,4},{2,6},{4,8},{6,10},{8,12},{10,14},{12,16},{14,18},{16,20},{1... | collective-permute-start | bytes 393224 | tf_op jit(solution)/shard_map/ppermute | solution.py:60
  26.9 4.4 %collective-permute-start.2 = (bf16[256,256]{1,0:T(8,128)(2,1)}, bf16[256,256]{1,0:T(8,128)(2,1)}, u32[]{:S(2)}, u32[]{:S(2)}) collective-permute-start(bf16[256,256]{1,0:T(8,128)(2,1)} %pad_maximum_fusion.4), channel_id=1, source_target_pairs={{0,6},{2,8},{4,10},{6,12},{8,14},{10,16},{12,18},{14,20},{16,22},{... | collective-permute-start | bytes 393224 | tf_op jit(solution)/shard_map/ppermute | solution.py:60
  31.4 3.5 collective-permute-start.3
  35.5 4.0 %fusion.25 = f32[256,1024]{0,1:T(8,128)S(1)} fusion(bf16[2048,1024]{1,0:T(8,128)(2,1)} %param.17, f32[2048]{0:T(1024)S(1)} %convert_element_type.75, f32[256]{0:T(256)} %copy-done.17, bf16[256,2048]{1,0:T(8,128)(2,1)S(1)} %copy-done.4), kind=kOutput, calls=%fused_computation.46 | convolution fusion | flops 1075838976 | bytes 6300672 | tf_op jit(solution)/shard_map/dot_general | solution.py:121
  51.9 1.6 bitcast_dynamic-update-slice_fusion
  53.5 13.9 %all-gather.3.cloned.1.call-done = bf16[64,128,256]{2,1,0:T(8,128)(2,1)} async-done(((bf16[4,128,256]{2,1,0:T(8,128)(2,1)}), bf16[64,128,256]{2,1,0:T(8,128)(2,1)}) %all-gather.3.cloned.1.call-update) | async-done | bytes 4194320 | tf_op jit(solution)/shard_map/all_gather | solution.py:90
  68.6 49.2 %while.31 = (s32[]{:T(128)}, f32[2,8,256]{2,1,0:T(8,128)S(1)}, f32[2,8,256]{2,1,0:T(8,128)S(1)}, f32[2,8,256,64]{2,3,1,0:T(8,128)}, s32[]{:T(128)}, /*index=5*/s...) while((s32[]{:T(128)}, f32[2,8,256]{2,1,0:T(8,128)S(1)}, ...), condition=%wide.region_7.8_spmd, body=%wide.region_4.7_spmd.sunk | while | flops 560472320 | bytes 63441352 | solution.py:152
  71.0 1.7 fusion.66
  74.4 6.5 %fusion.67 = f32[2,8,256,64]{2,3,1,0:T(8,128)} fusion(bf16[512,2,64,1]{0,2,3,1:T(8,128)(2,1)S(1)} %bitcast.123, f32[2,512,256,8]{2,1,3,0:T(8,128)} %copy-done.1, f32[2,8,256]{2,1,0:T(8,128)S(1)} %max.14, pred[256]{0:T(512)(128)(4,1)S(1)} %broadcast_compare_fusion.2, f32[2,8,256,64]{2,3,1,0:T(8,128)} %get-tuple-element.501, ...), kind=kOutput, calls=%fused_computation.9.clone.1 | convolution fusion | flops 277348352 | bytes 10649856 | tf_op jit(solution)/shard_map/while/body/grqn,ngd->grqd/dot_general | solution.py:51
  83.3 1.7 fusion.66
  86.7 6.5 %fusion.67 = f32[2,8,256,64]{2,3,1,0:T(8,128)} fusion(bf16[512,2,64,1]{0,2,3,1:T(8,128)(2,1)S(1)} %bitcast.123, f32[2,512,256,8]{2,1,3,0:T(8,128)} %copy-done.1, f32[2,8,256]{2,1,0:T(8,128)S(1)} %max.14, pred[256]{0:T(512)(128)(4,1)S(1)} %broadcast_compare_fusion.2, f32[2,8,256,64]{2,3,1,0:T(8,128)} %get-tuple-element.501, ...), kind=kOutput, calls=%fused_computation.9.clone.1 | convolution fusion | flops 277348352 | bytes 10649856 | tf_op jit(solution)/shard_map/while/body/grqn,ngd->grqd/dot_general | solution.py:51
  95.6 1.7 fusion.66
  99.0 6.5 %fusion.67 = f32[2,8,256,64]{2,3,1,0:T(8,128)} fusion(bf16[512,2,64,1]{0,2,3,1:T(8,128)(2,1)S(1)} %bitcast.123, f32[2,512,256,8]{2,1,3,0:T(8,128)} %copy-done.1, f32[2,8,256]{2,1,0:T(8,128)S(1)} %max.14, pred[256]{0:T(512)(128)(4,1)S(1)} %broadcast_compare_fusion.2, f32[2,8,256,64]{2,3,1,0:T(8,128)} %get-tuple-element.501, ...), kind=kOutput, calls=%fused_computation.9.clone.1 | convolution fusion | flops 277348352 | bytes 10649856 | tf_op jit(solution)/shard_map/while/body/grqn,ngd->grqd/dot_general | solution.py:51
  108.0 1.7 fusion.66
  111.3 6.5 %fusion.67 = f32[2,8,256,64]{2,3,1,0:T(8,128)} fusion(bf16[512,2,64,1]{0,2,3,1:T(8,128)(2,1)S(1)} %bitcast.123, f32[2,512,256,8]{2,1,3,0:T(8,128)} %copy-done.1, f32[2,8,256]{2,1,0:T(8,128)S(1)} %max.14, pred[256]{0:T(512)(128)(4,1)S(1)} %broadcast_compare_fusion.2, f32[2,8,256,64]{2,3,1,0:T(8,128)} %get-tuple-element.501, ...), kind=kOutput, calls=%fused_computation.9.clone.1 | convolution fusion | flops 277348352 | bytes 10649856 | tf_op jit(solution)/shard_map/while/body/grqn,ngd->grqd/dot_general | solution.py:51
  117.8 5.3 %while.32 = (s32[]{:T(128)}, f32[2,8,256]{2,1,0:T(8,128)S(1)}, f32[2,8,256]{2,1,0:T(8,128)S(1)}, f32[2,8,256,64]{2,3,1,0:T(8,128)}, s32[]{:T(128)}, /*index=5*/s...) while((s32[]{:T(128)}, f32[2,8,256]{2,1,0:T(8,128)S(1)}, ...), condition=%wide.region_12.13_spmd.clone, body=%wide.region_8.12_spmd.clone.sunk | while | flops 280789248 | bytes 25043356 | solution.py:171
  124.4 4.6 %convolution_convert_fusion = bf16[256,2048]{1,0:T(8,128)(2,1)} fusion(bf16[256,1024]{0,1:T(8,128)(2,1)S(1)} %bitcast.126, bf16[1024,2048]{1,0:T(8,128)(2,1)} %param.19), kind=kOutput, calls=%fused_computation.33 | convolution fusion | flops 1074266112 | bytes 5767168 | tf_op jit(solution)/shard_map/dot_general | solution.py:180
  130.6 71.7 %reduce-scatter.2.cloned.1.call-done = bf16[256,1024]{1,0:T(8,128)(2,1)} async-done(((bf16[256,2048]{1,0:T(8,128)(2,1)}), bf16[256,1024]{1,0:T(8,128)(2,1)}) %reduce-scatter.2.cloned.1.call-update) | async-done | bytes 524304 | tf_op jit(solution)/shard_map/reduce_scatter | solution.py:181
  204.8 86.5 %all-reduce.2.cloned.1.call-done = bf16[32,1024]{1,0:T(8,128)(2,1)} async-done(((bf16[32,1024]{1,0:T(8,128)(2,1)}), bf16[32,1024]{1,0:T(8,128)(2,1)}) %all-reduce.2.cloned.1.call-update) | async-done | bytes 65552 | tf_op jit(solution)/shard_map/psum | solution.py:191
  291.3 5.2 %all_gather.11 = bf16[32,2048]{1,0:T(8,128)(2,1)S(1)} all-gather(bf16[32,1024]{1,0:T(8,128)(2,1)} %all-reduce.2.cloned.1.call-done), channel_id=1, replica_groups=mesh['seq'=16,'mp'=2] {'mp'}, dimensions={1}, use_global_device_ids=true | all-gather | bytes 196608 | tf_op jit(solution)/shard_map/all_gather | solution.py:192
  296.7 3.6 %convolution_reduce_fusion = f32[32]{0:T(128)S(1)} fusion(bf16[32,2048]{1,0:T(8,128)(2,1)S(1)} %fusion.27, bf16[2048,1000]{0,1:T(8,128)(2,1)} %param.21), kind=kOutput, calls=%fused_computation.37 | convolution fusion | flops 131103968 | bytes 4227200 | tf_op jit(solution)/shard_map/dot_general | solution.py:195
  301.1 41.7 %pmax.7 = f32[32]{0:T(128)} all-reduce(f32[32]{0:T(128)S(1)} %convolution_reduce_fusion), channel_id=1, replica_groups=mesh['seq'=16,'mp'=2] {'seq','mp'}, use_global_device_ids=true, to_apply=%region_17.18 | all-reduce | flops 32 | bytes 256 | tf_op jit(solution)/shard_map/pmax | solution.py:196
  (145 shorter events, 46.5 us)
Async XLA Ops:
  7.2 4.5 %copy-start = (bf16[2048,512]{1,0:T(8,128)(2,1)S(1)}, bf16[2048,512]{1,0:T(8,128)(2,1)}, u32[]{:S(2)}) copy-start(bf16[2048,512]{1,0:T(8,128)(2,1)} %param.18) | copy-start | bytes 6291460
  7.2 7.3 %copy-start.13 = (s32[32]{0:T(128)S(1)}, s32[32]{0:T(128)}, u32[]{:S(2)}) copy-start(s32[32]{0:T(128)} %param.14) | copy-start | bytes 388
  7.2 60.2 %all-gather.3.cloned.1.call-start = ((), (), s32[]{:S(2)}) async-start(), calls=%async_computation.3 | async-start | bytes 4456448 | tf_op jit(solution)/shard_map/all_gather | solution.py:90
  9.3 193.0 %reduce-scatter.2.cloned.1.call-start = ((), (), s32[]{:S(2)}) async-start(), calls=%async_computation.1 | async-start | bytes 1572864 | tf_op jit(solution)/shard_map/reduce_scatter | solution.py:181
  11.6 23.9 %copy-start.4 = (bf16[256,2048]{1,0:T(8,128)(2,1)S(1)}, bf16[256,2048]{1,0:T(8,128)(2,1)}, u32[]{:S(2)}) copy-start(bf16[256,2048]{1,0:T(8,128)(2,1)} %param.13) | copy-start | bytes 3145732
  11.6 2.9 copy-start.17
  18.7 20.9 %copy-start.9 = (f32[256,32]{0,1:T(8,128)S(1)}, f32[256,32]{0,1:T(8,128)}, u32[]{:S(2)}) copy-start(f32[256,32]{0,1:T(8,128)} %copy-done.8) | copy-start | bytes 98308
  18.7 20.9 %copy-start.11 = (f32[256,32]{0,1:T(8,128)S(1)}, f32[256,32]{0,1:T(8,128)}, u32[]{:S(2)}) copy-start(f32[256,32]{0,1:T(8,128)} %copy-done.10) | copy-start | bytes 98308
  19.5 27.7 %collective-permute-start = (bf16[256,256]{1,0:T(8,128)(2,1)}, bf16[256,256]{1,0:T(8,128)(2,1)}, u32[]{:S(2)}, u32[]{:S(2)}) collective-permute-start(bf16[256,256]{1,0:T(8,128)(2,1)} %pad_maximum_fusion.4), channel_id=1, source_target_pairs={{0,2},{2,4},{4,6},{6,8},{8,10},{10,12},{12,14},{14,16},{16,18},{18... | collective-permute-start | bytes 393224 | tf_op jit(solution)/shard_map/ppermute | solution.py:60
  22.5 26.3 %collective-permute-start.1 = (bf16[256,256]{1,0:T(8,128)(2,1)}, bf16[256,256]{1,0:T(8,128)(2,1)}, u32[]{:S(2)}, u32[]{:S(2)}) collective-permute-start(bf16[256,256]{1,0:T(8,128)(2,1)} %pad_maximum_fusion.4), channel_id=1, source_target_pairs={{0,4},{2,6},{4,8},{6,10},{8,12},{10,14},{12,16},{14,18},{16,20},{1... | collective-permute-start | bytes 393224 | tf_op jit(solution)/shard_map/ppermute | solution.py:60
  26.9 23.4 %collective-permute-start.2 = (bf16[256,256]{1,0:T(8,128)(2,1)}, bf16[256,256]{1,0:T(8,128)(2,1)}, u32[]{:S(2)}, u32[]{:S(2)}) collective-permute-start(bf16[256,256]{1,0:T(8,128)(2,1)} %pad_maximum_fusion.4), channel_id=1, source_target_pairs={{0,6},{2,8},{4,10},{6,12},{8,14},{10,16},{12,18},{14,20},{16,22},{... | collective-permute-start | bytes 393224 | tf_op jit(solution)/shard_map/ppermute | solution.py:60
  31.4 20.5 %collective-permute-start.3 = (bf16[256,256]{1,0:T(8,128)(2,1)}, bf16[256,256]{1,0:T(8,128)(2,1)}, u32[]{:S(2)}, u32[]{:S(2)}) collective-permute-start(bf16[256,256]{1,0:T(8,128)(2,1)} %pad_maximum_fusion.4), channel_id=1, source_target_pairs={{0,8},{2,10},{4,12},{6,14},{8,16},{10,18},{12,20},{14,22},{16,24},... | collective-permute-start | bytes 393224 | tf_op jit(solution)/shard_map/ppermute | solution.py:60
  35.5 7.2 %copy-start.15 = (s32[32]{0:T(128)S(1)}, s32[32]{0:T(128)}, u32[]{:S(2)}) copy-start(s32[32]{0:T(128)} %copy-done.14) | copy-start | bytes 388
  71.0 3.2 copy-start.1
  83.3 3.2 copy-start.1
  95.6 3.2 copy-start.1
  107.9 3.2 copy-start.1
  119.1 1.7 copy-start.2
  124.4 4.6 %copy-start.5 = (bf16[256,2048]{1,0:T(8,128)(2,1)S(1)}, bf16[256,2048]{1,0:T(8,128)(2,1)}, u32[]{:S(2)}) copy-start(bf16[256,2048]{1,0:T(8,128)(2,1)} %param.13) | copy-start | bytes 3145732
  129.0 74.9 %copy-start.16 = (s32[32]{0:T(128)S(1)}, s32[32]{0:T(128)}, u32[]{:S(2)}) copy-start(s32[32]{0:T(128)} %get-tuple-element.333) | copy-start | bytes 388
  129.0 75.8 %copy-start.12 = (bf16[2048]{0:T(1024)(128)(2,1)S(1)}, bf16[2048]{0:T(1024)(128)(2,1)}, u32[]{:S(2)}) copy-start(bf16[2048]{0:T(1024)(128)(2,1)} %param.20) | copy-start | bytes 12292
  129.0 162.3 %all-reduce.2.cloned.1.call-start = ((), (), s32[]{:S(2)}) async-start(), calls=%async_computation.2 | async-start | bytes 131072 | tf_op jit(solution)/shard_map/psum | solution.py:191
  203.9 138.9 %copy-start.6 = (bf16[256,1024]{1,0:T(8,128)(2,1)}, bf16[256,1024]{1,0:T(8,128)(2,1)S(1)}, u32[]{:S(2)}) copy-start(bf16[256,1024]{1,0:T(8,128)(2,1)S(1)} %add_convert_fusion) | copy-start | bytes 1572868
  296.7 46.1 %copy-start.7 = (bf16[32,2048]{1,0:T(8,128)(2,1)}, bf16[32,2048]{1,0:T(8,128)(2,1)S(1)}, u32[]{:S(2)}) copy-start(bf16[32,2048]{1,0:T(8,128)(2,1)S(1)} %fusion.27) | copy-start | bytes 393220
  (4 other events, 2.9 us)
Sparse Core Ops, SparseCore 0:
  10.8 56.5 all-gather.2
  129.1 73.1 reduce-scatter.1
  206.8 84.4 all-reduce.1

commit v2 on v1

--- a/solution.py
+++ b/solution.py
@@ -52,6 +52,18 @@
         "grqn,ngd->grqd", weights.astype(jnp.bfloat16), val_rows, preferred_element_type=jnp.float32
     )
     return (new_max, new_sum, numerator)
+
+
+def butterfly(block, axis, combine):
+    count = lax.axis_size(axis)
+    if count & (count - 1):
+        return None
+    step = 1
+    while step < count:
+        partner = lax.ppermute(block, axis, [(i, i ^ step) for i in range(count)])
+        block = combine(block, partner)
+        step *= 2
+    return block
 
 
 def shifted_back(block, axis, distance):
@@ -178,22 +190,34 @@
         .astype(jnp.bfloat16)
     )
     mixture = jnp.dot(context, w_out, preferred_element_type=jnp.float32)
-    mixture = lax.psum_scatter(
-        mixture.astype(jnp.bfloat16), "mp", scatter_dimension=1, tiled=True
-    ).astype(jnp.float32)
+    mp_devices = lax.axis_size("mp")
     own_columns = lax.dynamic_slice_in_dim(activations, mp_index * part_width, part_width, 1)
-    hidden = (own_columns + mixture).astype(jnp.bfloat16)
+    if mp_devices == 2:
+        kept = lax.dynamic_slice_in_dim(mixture, mp_index * part_width, part_width, 1)
+        sent = lax.dynamic_slice_in_dim(mixture, (1 - mp_index) * part_width, part_width, 1)
+        received = lax.ppermute(sent.astype(jnp.bfloat16), "mp", [(0, 1), (1, 0)])
+        hidden = (own_columns + (kept + received.astype(jnp.float32))).astype(jnp.bfloat16)
+    else:
+        mixture = lax.psum_scatter(
+            mixture.astype(jnp.bfloat16), "mp", scatter_dimension=1, tiled=True
+        ).astype(jnp.float32)
+        hidden = (own_columns + mixture).astype(jnp.bfloat16)
     local_last = request_end - 1 - seq_index * token_rows
     onehot = (local_last[:, None] == jnp.arange(token_rows, dtype=jnp.int32)[None, :]).astype(
         jnp.bfloat16
     )
     last_part = jnp.dot(onehot, hidden, preferred_element_type=jnp.float32).astype(jnp.bfloat16)
-    last_part = lax.psum(last_part, "seq")
-    last_rows = lax.all_gather(last_part, "mp", axis=1, tiled=True).astype(jnp.float32)
+    summed = butterfly(last_part, "seq", jnp.add)
+    if summed is None:
+        summed = lax.psum(last_part, "seq")
+    last_rows = lax.all_gather(summed, "mp", axis=1, tiled=True).astype(jnp.float32)
     inv_rms = lax.rsqrt(jnp.mean(last_rows * last_rows, -1, keepdims=True) + epsilon)
     last_normed = (last_rows * final_gain.astype(jnp.float32) * inv_rms).astype(jnp.bfloat16)
     logits = jnp.dot(last_normed, w_head, preferred_element_type=jnp.float32)
-    greatest = lax.pmax(jnp.max(logits, -1), ("seq", "mp"))
+    local_best = jnp.max(logits, -1)
+    best_seq = butterfly(local_best, "seq", jnp.maximum)
+    best_all = None if best_seq is None else butterfly(best_seq, "mp", jnp.maximum)
+    greatest = lax.pmax(local_best, ("seq", "mp")) if best_all is None else best_all
     return (hidden, suffix_cache, last_normed, greatest)
 
 

time: 350 us -> 252 us (0.72); the launches traced: 349 us -> 255 us
  waiting for transfers between devices: 172 us -> 43.3 us
  starting transfers between devices: 15.5 us -> 92.3 us
  blocking collectives: 46.9 us -> 4.94 us
  matrix products: 48.3 us -> 44.4 us
    psum x1 -> x0, waiting for transfers between devices: 86.5 us -> none  [per_device(): last_part = lax.psum(last_part, 'seq')]
    ppermute x0 -> x10, starting transfers between devices: none -> 77 us  [the longest x9 75.5 us: butterfly(): partner = lax.ppermute(block, axis, [(i, i ^ step) for i in range(count)])]
    reduce_scatter x1 -> x0, waiting for transfers between devices: 71.7 us -> none  [per_device(): lax.psum_scatter(mixture.astype(jnp.bfloat16), 'mp', scatter_dimension=1,...]
    pmax x1 -> x0, blocking collectives: 41.7 us -> none  [per_device(): greatest = lax.pmax(jnp.max(logits, -1), ('seq', 'mp'))]
    ppermute x0 -> x10, waiting for transfers between devices: none -> 29.3 us  [the longest x9 22.8 us: butterfly(): partner = lax.ppermute(block, axis, [(i, i ^ step) for i in range(count)])]
    unnamed x33 -> x37, local copies, waits for them, and re-layouts: 5.8 us -> 7.12 us
  transfers between devices with their start and end apart: 7 -> 15, of which waited for: 3 -> 11; matrix products, arithmetic and copies ran while one was open for 7% -> 9% of each run, Pallas kernels for 0% -> 0%
where the time goes in v2:
time: 252 us; the launch traced here: 255 us
  starting transfers between devices  92.3 us (37%)
  matrix products  44.4 us (18%)
  waiting for transfers between devices  43.3 us (17%)
  local copies, waits for them, and re-layouts  29.1 us (12%)
  other arithmetic  20.5 us (8%)
  between operations  20.2 us (8%)
  blocking collectives  4.94 us (2%)
    ppermute x9, starting transfers between devices, butterfly(): partner = lax.ppermute(block, axis, [(i, i ^ step) for i in range(count)])  75.5 us
    dot_general x5, matrix products, attend(): jnp.einsum('grqn,ngd->grqd', weights.astype(jnp.bfloat16), val_rows, pref...  27.2 us
    ppermute x9, waiting for transfers between devices, butterfly(): partner = lax.ppermute(block, axis, [(i, i ^ step) for i in range(count)])  22.8 us
    ppermute x4, starting transfers between devices, shifted_back(): return lax.ppermute(block, axis, route)  15.3 us
    all_gather x1, waiting for transfers between devices, per_device(): all_prefix = lax.all_gather(own_prefix, 'seq', axis=0)  14 us
    while x25, local copies, waits for them, and re-layouts  8.15 us
    reduce_sum x5, other arithmetic, attend(): new_sum = old_sum * factor + jnp.sum(weights, -1)  7.48 us
    unnamed x37, local copies, waits for them, and re-layouts  7.12 us
  transfers between devices with their start and end apart: 15, of which 11 were waited for; matrix products, arithmetic and copies ran while one was open for 9% of the time, Pallas kernels for 0%

profile of v2, /device:TPU:0, one launch (start us, length us, event | category | flops | bytes accessed | tf_op | source)
XLA Modules:
  0.0 255.1 jit_solution(12811339271903104042)
XLA Ops:
  11.6 2.0 fusion.24
  19.4 3.0 %collective-permute-start = (bf16[256,256]{1,0:T(8,128)(2,1)}, bf16[256,256]{1,0:T(8,128)(2,1)}, u32[]{:S(2)}, u32[]{:S(2)}) collective-permute-start(bf16[256,256]{1,0:T(8,128)(2,1)} %pad_maximum_fusion.4), channel_id=1, source_target_pairs={{0,2},{2,4},{4,6},{6,8},{8,10},{10,12},{12,14},{14,16},{16,18},{18... | collective-permute-start | bytes 393224 | tf_op jit(solution)/shard_map/ppermute | solution.py:72
  22.4 4.4 %collective-permute-start.1 = (bf16[256,256]{1,0:T(8,128)(2,1)}, bf16[256,256]{1,0:T(8,128)(2,1)}, u32[]{:S(2)}, u32[]{:S(2)}) collective-permute-start(bf16[256,256]{1,0:T(8,128)(2,1)} %pad_maximum_fusion.4), channel_id=1, source_target_pairs={{0,4},{2,6},{4,8},{6,10},{8,12},{10,14},{12,16},{14,18},{16,20},{1... | collective-permute-start | bytes 393224 | tf_op jit(solution)/shard_map/ppermute | solution.py:72
  26.8 4.4 %collective-permute-start.2 = (bf16[256,256]{1,0:T(8,128)(2,1)}, bf16[256,256]{1,0:T(8,128)(2,1)}, u32[]{:S(2)}, u32[]{:S(2)}) collective-permute-start(bf16[256,256]{1,0:T(8,128)(2,1)} %pad_maximum_fusion.4), channel_id=1, source_target_pairs={{0,6},{2,8},{4,10},{6,12},{8,14},{10,16},{12,18},{14,20},{16,22},{... | collective-permute-start | bytes 393224 | tf_op jit(solution)/shard_map/ppermute | solution.py:72
  31.2 3.5 %collective-permute-start.3 = (bf16[256,256]{1,0:T(8,128)(2,1)}, bf16[256,256]{1,0:T(8,128)(2,1)}, u32[]{:S(2)}, u32[]{:S(2)}) collective-permute-start(bf16[256,256]{1,0:T(8,128)(2,1)} %pad_maximum_fusion.4), channel_id=1, source_target_pairs={{0,8},{2,10},{4,12},{6,14},{8,16},{10,18},{12,20},{14,22},{16,24},... | collective-permute-start | bytes 393224 | tf_op jit(solution)/shard_map/ppermute | solution.py:72
  35.4 4.0 %fusion.25 = f32[256,1024]{0,1:T(8,128)S(1)} fusion(bf16[2048,1024]{1,0:T(8,128)(2,1)} %param.17, f32[2048]{0:T(1024)S(1)} %convert_element_type.75, f32[256]{0:T(256)} %copy-done.19, bf16[256,2048]{1,0:T(8,128)(2,1)S(1)} %copy-done.4), kind=kOutput, calls=%fused_computation.46 | convolution fusion | flops 1075838976 | bytes 6300672 | tf_op jit(solution)/shard_map/dot_general | solution.py:133
  53.4 14.0 %all-gather.3.cloned.1.call-done = bf16[64,128,256]{2,1,0:T(8,128)(2,1)} async-done(((bf16[4,128,256]{2,1,0:T(8,128)(2,1)}), bf16[64,128,256]{2,1,0:T(8,128)(2,1)}) %all-gather.3.cloned.1.call-update) | async-done | bytes 4194320 | tf_op jit(solution)/shard_map/all_gather | solution.py:102
  68.6 49.3 %while.31 = (s32[]{:T(128)}, f32[2,8,256]{2,1,0:T(8,128)S(1)}, f32[2,8,256]{2,1,0:T(8,128)S(1)}, f32[2,8,256,64]{2,3,1,0:T(8,128)}, s32[]{:T(128)}, /*index=5*/s...) while((s32[]{:T(128)}, f32[2,8,256]{2,1,0:T(8,128)S(1)}, ...), condition=%wide.region_7.8_spmd, body=%wide.region_4.7_spmd.sunk | while | flops 560472320 | bytes 63441352 | solution.py:164
  74.4 6.5 %fusion.68 = f32[2,8,256,64]{2,3,1,0:T(8,128)} fusion(bf16[512,2,64,1]{0,2,3,1:T(8,128)(2,1)S(1)} %bitcast.123, f32[2,512,256,8]{2,1,3,0:T(8,128)} %copy-done.1, f32[2,8,256]{2,1,0:T(8,128)S(1)} %max.32, pred[256]{0:T(512)(128)(4,1)S(1)} %broadcast_compare_fusion.2, f32[2,8,256,64]{2,3,1,0:T(8,128)} %get-tuple-element.501, ...), kind=kOutput, calls=%fused_computation.9.clone.1 | convolution fusion | flops 277348352 | bytes 10649856 | tf_op jit(solution)/shard_map/while/body/grqn,ngd->grqd/dot_general | solution.py:51
  86.7 6.5 %fusion.68 = f32[2,8,256,64]{2,3,1,0:T(8,128)} fusion(bf16[512,2,64,1]{0,2,3,1:T(8,128)(2,1)S(1)} %bitcast.123, f32[2,512,256,8]{2,1,3,0:T(8,128)} %copy-done.1, f32[2,8,256]{2,1,0:T(8,128)S(1)} %max.32, pred[256]{0:T(512)(128)(4,1)S(1)} %broadcast_compare_fusion.2, f32[2,8,256,64]{2,3,1,0:T(8,128)} %get-tuple-element.501, ...), kind=kOutput, calls=%fused_computation.9.clone.1 | convolution fusion | flops 277348352 | bytes 10649856 | tf_op jit(solution)/shard_map/while/body/grqn,ngd->grqd/dot_general | solution.py:51
  99.1 6.5 %fusion.68 = f32[2,8,256,64]{2,3,1,0:T(8,128)} fusion(bf16[512,2,64,1]{0,2,3,1:T(8,128)(2,1)S(1)} %bitcast.123, f32[2,512,256,8]{2,1,3,0:T(8,128)} %copy-done.1, f32[2,8,256]{2,1,0:T(8,128)S(1)} %max.32, pred[256]{0:T(512)(128)(4,1)S(1)} %broadcast_compare_fusion.2, f32[2,8,256,64]{2,3,1,0:T(8,128)} %get-tuple-element.501, ...), kind=kOutput, calls=%fused_computation.9.clone.1 | convolution fusion | flops 277348352 | bytes 10649856 | tf_op jit(solution)/shard_map/while/body/grqn,ngd->grqd/dot_general | solution.py:51
  111.4 6.5 %fusion.68 = f32[2,8,256,64]{2,3,1,0:T(8,128)} fusion(bf16[512,2,64,1]{0,2,3,1:T(8,128)(2,1)S(1)} %bitcast.123, f32[2,512,256,8]{2,1,3,0:T(8,128)} %copy-done.1, f32[2,8,256]{2,1,0:T(8,128)S(1)} %max.32, pred[256]{0:T(512)(128)(4,1)S(1)} %broadcast_compare_fusion.2, f32[2,8,256,64]{2,3,1,0:T(8,128)} %get-tuple-element.501, ...), kind=kOutput, calls=%fused_computation.9.clone.1 | convolution fusion | flops 277348352 | bytes 10649856 | tf_op jit(solution)/shard_map/while/body/grqn,ngd->grqd/dot_general | solution.py:51
  117.9 5.3 %while.32 = (s32[]{:T(128)}, f32[2,8,256]{2,1,0:T(8,128)S(1)}, f32[2,8,256]{2,1,0:T(8,128)S(1)}, f32[2,8,256,64]{2,3,1,0:T(8,128)}, s32[]{:T(128)}, /*index=5*/s...) while((s32[]{:T(128)}, f32[2,8,256]{2,1,0:T(8,128)S(1)}, ...), condition=%wide.region_12.13_spmd.clone, body=%wide.region_8.12_spmd.clone.sunk | while | flops 280789248 | bytes 25043356 | solution.py:183
  124.5 3.5 %fusion.33 = f32[256,2048]{1,0:T(8,128)S(1)} fusion(bf16[256,1024]{0,1:T(8,128)(2,1)S(1)} %bitcast.126, bf16[1024,2048]{1,0:T(8,128)(2,1)} %param.19), kind=kOutput, calls=%fused_computation.86 | convolution fusion | flops 1073741824 | bytes 6815744 | tf_op jit(solution)/shard_map/dot_general | solution.py:192
  133.3 6.5 %collective-permute-done.4 = bf16[256,1024]{1,0:T(8,128)(2,1)} collective-permute-done((bf16[256,1024]{1,0:T(8,128)(2,1)}, bf16[256,1024]{1,0:T(8,128)(2,1)}, u32[]{:S(2)}, u32[]{:S(2)}) %collective-permute-start.4) | collective-permute-done | bytes 524320 | tf_op jit(solution)/shard_map/ppermute | solution.py:198
  139.7 1.9 add_convert_fusion
  141.9 53.7 %collective-permute-start.5 = (bf16[32,1024]{1,0:T(8,128)(2,1)S(1)}, bf16[32,1024]{1,0:T(8,128)(2,1)S(1)}, u32[]{:S(2)}, u32[]{:S(2)}) collective-permute-start(bf16[32,1024]{1,0:T(8,128)(2,1)S(1)} %convolution_convert_fusion), channel_id=1, source_target_pairs={{0,2},{2,0},{4,6},{6,4},{8,10},{10,8},{12,14},{14,12},{16,18},{18,... | collective-permute-start | bytes 196616 | tf_op jit(solution)/shard_map/ppermute | solution.py:63
  196.6 4.3 %collective-permute-done.6 = bf16[32,1024]{1,0:T(8,128)(2,1)S(1)} collective-permute-done((bf16[32,1024]{1,0:T(8,128)(2,1)S(1)}, bf16[32,1024]{1,0:T(8,128)(2,1)S(1)}, u32[]{:S(2)}, u32[]{:S(2)}) %collective-permute-start.6) | collective-permute-done | bytes 65568 | tf_op jit(solution)/shard_map/ppermute | solution.py:63
  201.0 16.2 %collective-permute-start.7 = (bf16[32,1024]{1,0:T(8,128)(2,1)S(1)}, bf16[32,1024]{1,0:T(8,128)(2,1)S(1)}, u32[]{:S(2)}, u32[]{:S(2)}) collective-permute-start(bf16[32,1024]{1,0:T(8,128)(2,1)S(1)} %add.191), channel_id=1, source_target_pairs={{0,8},{2,10},{4,12},{6,14},{8,0},{10,2},{12,4},{14,6},{16,24},{18,... | collective-permute-start | bytes 196616 | tf_op jit(solution)/shard_map/ppermute | solution.py:63
  217.1 2.2 collective-permute-done.7
  219.5 5.1 %collective-permute-done.8 = bf16[32,1024]{1,0:T(8,128)(2,1)S(1)} collective-permute-done((bf16[32,1024]{1,0:T(8,128)(2,1)S(1)}, bf16[32,1024]{1,0:T(8,128)(2,1)S(1)}, u32[]{:S(2)}, u32[]{:S(2)}) %collective-permute-start.8) | collective-permute-done | bytes 65568 | tf_op jit(solution)/shard_map/ppermute | solution.py:63
  224.7 4.9 %all_gather.11 = bf16[32,2048]{1,0:T(8,128)(2,1)S(1)} all-gather(bf16[32,1024]{1,0:T(8,128)(2,1)S(1)} %add.193), channel_id=1, replica_groups=mesh['seq'=16,'mp'=2] {'mp'}, dimensions={1}, use_global_device_ids=true | all-gather | bytes 196608 | tf_op jit(solution)/shard_map/all_gather | solution.py:213
  236.0 2.2 collective-permute-start.11
  239.7 4.4 %collective-permute-done.12 = f32[32]{0:T(128)S(1)} collective-permute-done((f32[32]{0:T(128)S(1)}, f32[32]{0:T(128)S(1)}, u32[]{:S(2)}, u32[]{:S(2)}) %collective-permute-start.12) | collective-permute-done | bytes 160 | tf_op jit(solution)/shard_map/ppermute | solution.py:63
  (172 shorter events, 68.0 us)
Async XLA Ops:
  7.2 60.3 %all-gather.3.cloned.1.call-start = ((), (), s32[]{:S(2)}) async-start(), calls=%async_computation | async-start | bytes 4456448 | tf_op jit(solution)/shard_map/all_gather | solution.py:102
  11.5 23.8 %copy-start.4 = (bf16[256,2048]{1,0:T(8,128)(2,1)S(1)}, bf16[256,2048]{1,0:T(8,128)(2,1)}, u32[]{:S(2)}) copy-start(bf16[256,2048]{1,0:T(8,128)(2,1)} %param.13) | copy-start | bytes 3145732
  18.6 20.8 %copy-start.11 = (f32[256,32]{0,1:T(8,128)S(1)}, f32[256,32]{0,1:T(8,128)}, u32[]{:S(2)}) copy-start(f32[256,32]{0,1:T(8,128)} %copy-done.10) | copy-start | bytes 98308
  18.6 20.8 %copy-start.13 = (f32[256,32]{0,1:T(8,128)S(1)}, f32[256,32]{0,1:T(8,128)}, u32[]{:S(2)}) copy-start(f32[256,32]{0,1:T(8,128)} %copy-done.12) | copy-start | bytes 98308
  19.4 27.8 %collective-permute-start = (bf16[256,256]{1,0:T(8,128)(2,1)}, bf16[256,256]{1,0:T(8,128)(2,1)}, u32[]{:S(2)}, u32[]{:S(2)}) collective-permute-start(bf16[256,256]{1,0:T(8,128)(2,1)} %pad_maximum_fusion.4), channel_id=1, source_target_pairs={{0,2},{2,4},{4,6},{6,8},{8,10},{10,12},{12,14},{14,16},{16,18},{18... | collective-permute-start | bytes 393224 | tf_op jit(solution)/shard_map/ppermute | solution.py:72
  22.4 26.3 %collective-permute-start.1 = (bf16[256,256]{1,0:T(8,128)(2,1)}, bf16[256,256]{1,0:T(8,128)(2,1)}, u32[]{:S(2)}, u32[]{:S(2)}) collective-permute-start(bf16[256,256]{1,0:T(8,128)(2,1)} %pad_maximum_fusion.4), channel_id=1, source_target_pairs={{0,4},{2,6},{4,8},{6,10},{8,12},{10,14},{12,16},{14,18},{16,20},{1... | collective-permute-start | bytes 393224 | tf_op jit(solution)/shard_map/ppermute | solution.py:72
  26.8 23.5 %collective-permute-start.2 = (bf16[256,256]{1,0:T(8,128)(2,1)}, bf16[256,256]{1,0:T(8,128)(2,1)}, u32[]{:S(2)}, u32[]{:S(2)}) collective-permute-start(bf16[256,256]{1,0:T(8,128)(2,1)} %pad_maximum_fusion.4), channel_id=1, source_target_pairs={{0,6},{2,8},{4,10},{6,12},{8,14},{10,16},{12,18},{14,20},{16,22},{... | collective-permute-start | bytes 393224 | tf_op jit(solution)/shard_map/ppermute | solution.py:72
  31.2 20.6 %collective-permute-start.3 = (bf16[256,256]{1,0:T(8,128)(2,1)}, bf16[256,256]{1,0:T(8,128)(2,1)}, u32[]{:S(2)}, u32[]{:S(2)}) collective-permute-start(bf16[256,256]{1,0:T(8,128)(2,1)} %pad_maximum_fusion.4), channel_id=1, source_target_pairs={{0,8},{2,10},{4,12},{6,14},{8,16},{10,18},{12,20},{14,22},{16,24},... | collective-permute-start | bytes 393224 | tf_op jit(solution)/shard_map/ppermute | solution.py:72
  124.5 7.2 %copy-start.5 = (bf16[256,2048]{1,0:T(8,128)(2,1)S(1)}, bf16[256,2048]{1,0:T(8,128)(2,1)}, u32[]{:S(2)}) copy-start(bf16[256,2048]{1,0:T(8,128)(2,1)} %param.13) | copy-start | bytes 3145732
  129.4 12.3 %copy-start.18 = (s32[32]{0:T(128)S(1)}, s32[32]{0:T(128)}, u32[]{:S(2)}) copy-start(s32[32]{0:T(128)} %get-tuple-element.333) | copy-start | bytes 388
  129.4 90.1 %copy-start.14 = (bf16[2048]{0:T(1024)(128)(2,1)S(1)}, bf16[2048]{0:T(1024)(128)(2,1)}, u32[]{:S(2)}) copy-start(bf16[2048]{0:T(1024)(128)(2,1)} %param.20) | copy-start | bytes 12292
  130.2 9.5 %collective-permute-start.4 = (bf16[256,1024]{1,0:T(8,128)(2,1)}, bf16[256,1024]{1,0:T(8,128)(2,1)}, u32[]{:S(2)}, u32[]{:S(2)}) collective-permute-start(bf16[256,1024]{1,0:T(8,128)(2,1)} %dynamic-slice_convert_fusion), channel_id=1, source_target_pairs={{0,1},{1,0},{2,3},{3,2},{4,5},{5,4},{6,7},{7,6},{8,9},{9,8},{10,11... | collective-permute-start | bytes 1572872 | tf_op jit(solution)/shard_map/ppermute | solution.py:198
  133.3 96.6 %copy-start.6 = (bf16[2048,1000]{0,1:T(8,128)(2,1)S(1)}, bf16[2048,1000]{0,1:T(8,128)(2,1)}, u32[]{:S(2)}) copy-start(bf16[2048,1000]{0,1:T(8,128)(2,1)} %param.21) | copy-start | bytes 12288004
  141.7 106.5 %copy-start.7 = (bf16[256,1024]{1,0:T(8,128)(2,1)}, bf16[256,1024]{1,0:T(8,128)(2,1)S(1)}, u32[]{:S(2)}) copy-start(bf16[256,1024]{1,0:T(8,128)(2,1)S(1)} %add_convert_fusion) | copy-start | bytes 1572868
  141.9 54.6 %collective-permute-start.5 = (bf16[32,1024]{1,0:T(8,128)(2,1)S(1)}, bf16[32,1024]{1,0:T(8,128)(2,1)S(1)}, u32[]{:S(2)}, u32[]{:S(2)}) collective-permute-start(bf16[32,1024]{1,0:T(8,128)(2,1)S(1)} %convolution_convert_fusion), channel_id=1, source_target_pairs={{0,2},{2,0},{4,6},{6,4},{8,10},{10,8},{12,14},{14,12},{16,18},{18,... | collective-permute-start | bytes 196616 | tf_op jit(solution)/shard_map/ppermute | solution.py:63
  196.5 4.4 %collective-permute-start.6 = (bf16[32,1024]{1,0:T(8,128)(2,1)S(1)}, bf16[32,1024]{1,0:T(8,128)(2,1)S(1)}, u32[]{:S(2)}, u32[]{:S(2)}) collective-permute-start(bf16[32,1024]{1,0:T(8,128)(2,1)S(1)} %add.190), channel_id=1, source_target_pairs={{0,4},{2,6},{4,0},{6,2},{8,12},{10,14},{12,8},{14,10},{16,20},{18,... | collective-permute-start | bytes 196616 | tf_op jit(solution)/shard_map/ppermute | solution.py:63
  201.0 18.4 %collective-permute-start.7 = (bf16[32,1024]{1,0:T(8,128)(2,1)S(1)}, bf16[32,1024]{1,0:T(8,128)(2,1)S(1)}, u32[]{:S(2)}, u32[]{:S(2)}) collective-permute-start(bf16[32,1024]{1,0:T(8,128)(2,1)S(1)} %add.191), channel_id=1, source_target_pairs={{0,8},{2,10},{4,12},{6,14},{8,0},{10,2},{12,4},{14,6},{16,24},{18,... | collective-permute-start | bytes 196616 | tf_op jit(solution)/shard_map/ppermute | solution.py:63
  219.4 5.2 %collective-permute-start.8 = (bf16[32,1024]{1,0:T(8,128)(2,1)S(1)}, bf16[32,1024]{1,0:T(8,128)(2,1)S(1)}, u32[]{:S(2)}, u32[]{:S(2)}) collective-permute-start(bf16[32,1024]{1,0:T(8,128)(2,1)S(1)} %add.192), channel_id=1, source_target_pairs={{0,16},{2,18},{4,20},{6,22},{8,24},{10,26},{12,28},{14,30},{16,0},... | collective-permute-start | bytes 196616 | tf_op jit(solution)/shard_map/ppermute | solution.py:63
  229.9 18.4 %copy-start.9 = (bf16[32,2048]{1,0:T(8,128)(2,1)}, bf16[32,2048]{1,0:T(8,128)(2,1)S(1)}, u32[]{:S(2)}) copy-start(bf16[32,2048]{1,0:T(8,128)(2,1)S(1)} %fusion.27) | copy-start | bytes 393220
  231.3 1.2 collective-permute-start.9
  232.4 3.5 %collective-permute-start.10 = (f32[32]{0:T(128)S(1)}, f32[32]{0:T(128)S(1)}, u32[]{:S(2)}, u32[]{:S(2)}) collective-permute-start(f32[32]{0:T(128)S(1)} %max.24), channel_id=1, source_target_pairs={{0,4},{2,6},{4,0},{6,2},{8,12},{10,14},{12,8},{14,10},{16,20},{18,... | collective-permute-start | bytes 392 | tf_op jit(solution)/shard_map/ppermute | solution.py:63
  236.0 3.7 %collective-permute-start.11 = (f32[32]{0:T(128)S(1)}, f32[32]{0:T(128)S(1)}, u32[]{:S(2)}, u32[]{:S(2)}) collective-permute-start(f32[32]{0:T(128)S(1)} %max.25), channel_id=1, source_target_pairs={{0,8},{2,10},{4,12},{6,14},{8,0},{10,2},{12,4},{14,6},{16,24},{18,... | collective-permute-start | bytes 392 | tf_op jit(solution)/shard_map/ppermute | solution.py:63
  239.7 4.4 %collective-permute-start.12 = (f32[32]{0:T(128)S(1)}, f32[32]{0:T(128)S(1)}, u32[]{:S(2)}, u32[]{:S(2)}) collective-permute-start(f32[32]{0:T(128)S(1)} %max.26), channel_id=1, source_target_pairs={{0,16},{2,18},{4,20},{6,22},{8,24},{10,26},{12,28},{14,30},{16,0},... | collective-permute-start | bytes 392 | tf_op jit(solution)/shard_map/ppermute | solution.py:63
  244.2 3.5 %collective-permute-start.13 = (f32[32]{0:T(128)S(1)}, f32[32]{0:T(128)S(1)}, u32[]{:S(2)}, u32[]{:S(2)}) collective-permute-start(f32[32]{0:T(128)S(1)} %max.27), channel_id=1, source_target_pairs={{0,1},{1,0},{2,3},{3,2},{4,5},{5,4},{6,7},{7,6},{8,9},{9,8},{10,11... | collective-permute-start | bytes 392 | tf_op jit(solution)/shard_map/ppermute | solution.py:63
  (14 other events, 40.6 us)
Sparse Core Ops, SparseCore 0:
  10.8 56.6 all-gather.2

commit v3 on v2

--- a/solution.py
+++ b/solution.py
@@ -1,8 +1,11 @@
+import functools
 import math
 
 import jax
 import jax.numpy as jnp
 from jax import lax
+from jax.experimental import pallas as pl
+from jax.experimental.pallas import tpu as pltpu
 from jax.sharding import PartitionSpec as P
 
 QH = 32
@@ -13,6 +16,8 @@
 P_SIZE = 2048
 MOST = 1024
 PREFIX_CHUNK = 512
+SUFFIX_CHUNK = 256
+TILE_TOKENS = 128
 
 
 epsilon = 1e-05
@@ -52,6 +57,61 @@
         "grqn,ngd->grqd", weights.astype(jnp.bfloat16), val_rows, preferred_element_type=jnp.float32
     )
     return (new_max, new_sum, numerator)
+
+
+def attention_kernel(
+    table, q_ref, rg_ref, rr_ref, rp_ref, pk_ref, pv_ref, sk_ref, sv_ref, kr_ref, kp_ref,
+    o_ref, m_ref, l_ref, acc_ref, *, kv_heads, prefix_chunk, suffix_chunk, chunks_per_group
+):
+    tile = pl.program_id(0)
+    p_lo = table[4 * tile]
+    p_hi = table[4 * tile + 1]
+    s_lo = table[4 * tile + 2]
+    s_hi = table[4 * tile + 3]
+    row_group = rg_ref[...]
+    row_request = rr_ref[...]
+    row_place = rp_ref[...]
+    for head in range(kv_heads):
+        query = q_ref[head]
+        m_ref[...] = jnp.full(m_ref.shape, -1e30, jnp.float32)
+        l_ref[...] = jnp.zeros(l_ref.shape, jnp.float32)
+        acc_ref[...] = jnp.zeros(acc_ref.shape, jnp.float32)
+
+        def update(key, value, allowed):
+            scores = lax.dot_general(
+                query, key, (((1,), (1,)), ((), ())), preferred_element_type=jnp.float32
+            ) * (1.0 / math.sqrt(HD))
+            scores = jnp.where(allowed, scores, -jnp.inf)
+            old_max = m_ref[...]
+            new_max = jnp.maximum(old_max, jnp.max(scores, axis=1, keepdims=True))
+            factor = jnp.exp(old_max - new_max)
+            weights = jnp.exp(scores - new_max)
+            l_ref[...] = l_ref[...] * factor + jnp.sum(weights, axis=1, keepdims=True)
+            acc_ref[...] = acc_ref[...] * factor + jnp.dot(
+                weights.astype(jnp.bfloat16), value, preferred_element_type=jnp.float32
+            )
+            m_ref[...] = new_max
+
+        def prefix_step(chunk, carry):
+            start = pl.multiple_of(chunk * prefix_chunk, prefix_chunk)
+            key = pk_ref[head, pl.ds(start, prefix_chunk), :]
+            value = pv_ref[head, pl.ds(start, prefix_chunk), :]
+            update(key, value, row_group == chunk // chunks_per_group)
+            return carry
+
+        lax.fori_loop(p_lo, p_hi, prefix_step, 0)
+
+        def suffix_step(chunk, carry):
+            start = pl.multiple_of(chunk * suffix_chunk, suffix_chunk)
+            key = sk_ref[head, pl.ds(start, suffix_chunk), :]
+            value = sv_ref[head, pl.ds(start, suffix_chunk), :]
+            key_request = kr_ref[pl.ds(chunk, 1), :]
+            key_place = kp_ref[pl.ds(chunk, 1), :]
+            update(key, value, (row_request == key_request) & (key_place <= row_place))
+            return carry
+
+        lax.fori_loop(s_lo, s_hi, suffix_step, 0)
+        o_ref[head] = (acc_ref[...] / l_ref[...]).astype(o_ref.dtype)
 
 
 def butterfly(block, axis, combine):
@@ -128,7 +188,6 @@
     earlier = [own_suffix] + [
         shifted_back(own_suffix, "seq", distance) for distance in range(1, back_blocks + 1)
     ]
-    suffix_window = jnp.stack(earlier, 0)
 
     query_full = jnp.dot(normed, w_query, preferred_element_type=jnp.float32)
     queries = (
@@ -137,58 +196,94 @@
         .reshape(token_rows, kv_heads, repeat_count, HD)
     )
 
-    running = (
-        jnp.full((kv_heads, repeat_count, token_rows), -1e30, jnp.float32),
-        jnp.zeros((kv_heads, repeat_count, token_rows), jnp.float32),
-        jnp.zeros((kv_heads, repeat_count, token_rows, HD), jnp.float32),
-    )
-
-    sources_per_chunk = max(1, PREFIX_CHUNK // prefix_rows)
-    chunks_per_group = seq_devices // sources_per_chunk
-    first_group = group_of[0]
-    last_group = group_of[token_rows - 1]
-
-    def prefix_step(chunk, state_now):
-        group = chunk // chunks_per_group
-        part = chunk % chunks_per_group
-        block = lax.dynamic_slice(
-            all_prefix,
-            (part * sources_per_chunk, group, 0, 0),
-            (sources_per_chunk, 1, prefix_rows, block_width),
-        ).reshape(sources_per_chunk * prefix_rows, block_width)
-        allowed = jnp.broadcast_to(
-            (group_of == group)[:, None], (token_rows, sources_per_chunk * prefix_rows)
-        )
-        return attend(state_now, queries, block, allowed)
-
-    running = lax.fori_loop(
-        first_group * chunks_per_group, (last_group + 1) * chunks_per_group, prefix_step, running
-    )
-
-    first_block = starts[request[0]] // token_rows
-    back_needed = jnp.minimum(seq_index - first_block, back_blocks)
-
-    def suffix_step(distance, state_now):
-        source_dev = seq_index - distance
-        key_place = source_dev * token_rows + jnp.arange(token_rows, dtype=jnp.int32)
-        key_request = jnp.sum((key_place[:, None] >= request_end[None, :]).astype(jnp.int32), 1)
-        allowed = (
-            (request[:, None] == key_request[None, :])
-            & (key_place[None, :] <= position[:, None])
-            & (source_dev >= 0)
-        )
-        block = lax.dynamic_index_in_dim(suffix_window, distance, 0, keepdims=False)
-        return attend(state_now, queries, block, allowed)
-
-    running = lax.fori_loop(0, back_needed + 1, suffix_step, running)
-
-    final_max, final_sum, numerator = running
-    context = numerator / final_sum[..., None]
-    context = (
-        jnp.transpose(context, (2, 0, 1, 3))
-        .reshape(token_rows, query_heads * HD)
-        .astype(jnp.bfloat16)
-    )
+    window_blocks = back_blocks + 1
+    window_rows = window_blocks * token_rows
+    window_start = (seq_index - back_blocks) * token_rows
+    suffix_window = jnp.concatenate(earlier[::-1], 0)
+    suffix_keys = jnp.transpose(
+        suffix_window[:, : kv_heads * HD].reshape(window_rows, kv_heads, HD), (1, 0, 2)
+    )
+    suffix_values = jnp.transpose(
+        suffix_window[:, kv_heads * HD :].reshape(window_rows, kv_heads, HD), (1, 0, 2)
+    )
+    prefix_total = seq_devices * prefix_rows
+    prefix_flat = jnp.transpose(all_prefix, (1, 0, 2, 3)).reshape(G * prefix_total, block_width)
+    prefix_keys = jnp.transpose(
+        prefix_flat[:, : kv_heads * HD].reshape(G * prefix_total, kv_heads, HD), (1, 0, 2)
+    )
+    prefix_values = jnp.transpose(
+        prefix_flat[:, kv_heads * HD :].reshape(G * prefix_total, kv_heads, HD), (1, 0, 2)
+    )
+    suffix_chunk = min(SUFFIX_CHUNK, token_rows)
+    prefix_chunk = min(PREFIX_CHUNK, prefix_total)
+    chunks_per_group = prefix_total // prefix_chunk
+    suffix_chunks = window_rows // suffix_chunk
+    key_place = window_start + jnp.arange(window_rows, dtype=jnp.int32)
+    key_request = jnp.sum((key_place[:, None] >= request_end[None, :]).astype(jnp.int32), 1)
+    key_request = jnp.where(key_place >= 0, key_request, -1)
+    key_request = key_request.reshape(suffix_chunks, suffix_chunk)
+    key_place = key_place.reshape(suffix_chunks, suffix_chunk)
+
+    tile_tokens = min(TILE_TOKENS, token_rows)
+    tile_count = token_rows // tile_tokens
+    tile_rows = tile_tokens * repeat_count
+    first_token = jnp.arange(tile_count, dtype=jnp.int32) * tile_tokens
+    last_token = first_token + tile_tokens - 1
+    p_lo = group_of[first_token] * chunks_per_group
+    p_hi = (group_of[last_token] + 1) * chunks_per_group
+    s_lo = jnp.maximum((starts[request[first_token]] - window_start) // suffix_chunk, 0)
+    s_hi = jnp.minimum((position[last_token] - window_start) // suffix_chunk + 1, suffix_chunks)
+    table = jnp.stack([p_lo, p_hi, s_lo, s_hi], 1).reshape(-1).astype(jnp.int32)
+
+    query_rows = jnp.transpose(queries, (1, 0, 2, 3)).reshape(
+        kv_heads, token_rows * repeat_count, HD
+    )
+    row_group = jnp.repeat(group_of, repeat_count)[:, None]
+    row_request = jnp.repeat(request, repeat_count)[:, None]
+    row_place = jnp.repeat(position, repeat_count)[:, None]
+
+    def whole(shape):
+        return pl.BlockSpec(shape, lambda tile, table: (0,) * len(shape))
+
+    row_spec = pl.BlockSpec((tile_rows, 1), lambda tile, table: (tile, 0))
+    context = pl.pallas_call(
+        functools.partial(
+            attention_kernel,
+            kv_heads=kv_heads,
+            prefix_chunk=prefix_chunk,
+            suffix_chunk=suffix_chunk,
+            chunks_per_group=chunks_per_group,
+        ),
+        grid_spec=pltpu.PrefetchScalarGridSpec(
+            num_scalar_prefetch=1,
+            grid=(tile_count,),
+            in_specs=[
+                pl.BlockSpec((kv_heads, tile_rows, HD), lambda tile, table: (0, tile, 0)),
+                row_spec,
+                row_spec,
+                row_spec,
+                whole(prefix_keys.shape),
+                whole(prefix_values.shape),
+                whole(suffix_keys.shape),
+                whole(suffix_values.shape),
+                whole(key_request.shape),
+                whole(key_place.shape),
+            ],
+            out_specs=pl.BlockSpec((kv_heads, tile_rows, HD), lambda tile, table: (0, tile, 0)),
+            scratch_shapes=[
+                pltpu.VMEM((tile_rows, 1), jnp.float32),
+                pltpu.VMEM((tile_rows, 1), jnp.float32),
+                pltpu.VMEM((tile_rows, HD), jnp.float32),
+            ],
+        ),
+        out_shape=jax.ShapeDtypeStruct((kv_heads, token_rows * repeat_count, HD), jnp.bfloat16),
+    )(
+        table, query_rows, row_group, row_request, row_place, prefix_keys, prefix_values,
+        suffix_keys, suffix_values, key_request, key_place,
+    )
+    context = jnp.transpose(
+        context.reshape(kv_heads, token_rows, repeat_count, HD), (1, 0, 2, 3)
+    ).reshape(token_rows, query_heads * HD)
     mixture = jnp.dot(context, w_out, preferred_element_type=jnp.float32)
     mp_devices = lax.axis_size("mp")
     own_columns = lax.dynamic_slice_in_dim(activations, mp_index * part_width, part_width, 1)

time: 252 us -> 215 us (0.85)
  starting transfers between devices: 92.3 us -> 48.9 us
  Pallas kernels: 0 us -> 39.4 us
  matrix products: 44.4 us -> 10 us
  local copies, waits for them, and re-layouts: 29.1 us -> 56.5 us
  waiting for transfers between devices: 43.3 us -> 25 us
  between operations: 20.2 us -> 14.5 us
  other arithmetic: 20.5 us -> 17.4 us
    ppermute x9, starting transfers between devices: 75.5 us -> 32.4 us  [butterfly(): partner = lax.ppermute(block, axis, [(i, i ^ step) for i in range(count)])]
    pallas_call x0 -> x1, Pallas kernels: none -> 39.4 us  [per_device(): pl.pallas_call(functools.partial(attention_kernel, kv_heads=kv_heads, pre...]
    dot_general x10 -> x0, matrix products: 33.2 us -> none  [the longest x5 27.2 us: attend(): jnp.einsum('grqn,ngd->grqd', weights.astype(jnp.bfloat16), val_rows, pref...]
    reshape x0 -> x6, local copies, waits for them, and re-layouts: none -> 16.8 us  [the longest x1 4.85 us: per_device(): prefix_flat[:, kv_heads * HD:].reshape(G * prefix_total, kv_heads, HD)]
    all_gather x1, waiting for transfers between devices: 14 us -> 0.04 us  [per_device(): all_prefix = lax.all_gather(own_prefix, 'seq', axis=0)]
    slice x7 -> x6, local copies, waits for them, and re-layouts: 1.25 us -> 14 us  [the longest x2 6.35 us: per_device(): prefix_flat[:, kv_heads * HD:].reshape(G * prefix_total, kv_heads, HD)]
    while x25 -> x0, local copies, waits for them, and re-layouts: 8.15 us -> none
    reduce_sum x6 -> x1, other arithmetic: 7.57 us -> 0.77 us  [per_device(): jnp.sum((key_place[:, None] >= request_end[None, :]).astype(jnp.int32), 1)]
  transfers between devices with their start and end apart: 15 -> 15, of which waited for: 11 -> 10; matrix products, arithmetic and copies ran while one was open for 9% -> 21% of each run, Pallas kernels for 0% -> 0%
where the time goes in v3:
time: 215 us; the launch traced here: 217 us
  local copies, waits for them, and re-layouts  56.5 us (26%)
  starting transfers between devices  48.9 us (23%)
  Pallas kernels  39.4 us (18%)
  waiting for transfers between devices  25 us (12%)
  other arithmetic  17.4 us (8%)
  between operations  14.5 us (7%)
  matrix products  10 us (5%)
  blocking collectives  4.94 us (2%)
    pallas_call x1, Pallas kernels, per_device(): pl.pallas_call(functools.partial(attention_kernel, kv_heads=kv_heads, pre...  39.4 us
    ppermute x9, starting transfers between devices, butterfly(): partner = lax.ppermute(block, axis, [(i, i ^ step) for i in range(count)])  32.4 us
    ppermute x9, waiting for transfers between devices, butterfly(): partner = lax.ppermute(block, axis, [(i, i ^ step) for i in range(count)])  18.6 us
    ppermute x4, starting transfers between devices, shifted_back(): return lax.ppermute(block, axis, route)  14.9 us
    ppermute x1, waiting for transfers between devices, per_device(): received = lax.ppermute(sent.astype(jnp.bfloat16), 'mp', [(0, 1), (1, 0)])  6.38 us
    slice x2, local copies, waits for them, and re-layouts, per_device(): prefix_flat[:, kv_heads * HD:].reshape(G * prefix_total, kv_heads, HD)  6.35 us
    unnamed x44, local copies, waits for them, and re-layouts  6.21 us
    all_gather x1, blocking collectives, per_device(): lax.all_gather(summed, 'mp', axis=1, tiled=True).astype(jnp.float32)  4.94 us
  transfers between devices with their start and end apart: 15, of which 10 were waited for; matrix products, arithmetic and copies ran while one was open for 21% of the time, Pallas kernels for 0%

profile of v3, /device:TPU:0, one launch (start us, length us, event | category | flops | bytes accessed | tf_op | source)
XLA Modules:
  0.0 216.7 jit_solution(7161681405586415389)
XLA Ops:
  17.8 5.6 %collective-permute-start = (bf16[256,256]{1,0:T(8,128)(2,1)}, bf16[256,256]{1,0:T(8,128)(2,1)}, u32[]{:S(2)}, u32[]{:S(2)}) collective-permute-start(bf16[256,256]{1,0:T(8,128)(2,1)} %pad_maximum_fusion.4), channel_id=1, source_target_pairs={{0,8},{2,10},{4,12},{6,14},{8,16},{10,18},{12,20},{14,22},{16,24},... | collective-permute-start | bytes 393224 | tf_op jit(solution)/shard_map/ppermute | solution.py:132
  23.4 3.2 %collective-permute-start.1 = (bf16[256,256]{1,0:T(8,128)(2,1)}, bf16[256,256]{1,0:T(8,128)(2,1)}, u32[]{:S(2)}, u32[]{:S(2)}) collective-permute-start(bf16[256,256]{1,0:T(8,128)(2,1)} %pad_maximum_fusion.4), channel_id=1, source_target_pairs={{0,6},{2,8},{4,10},{6,12},{8,14},{10,16},{12,18},{14,20},{16,22},{... | collective-permute-start | bytes 393224 | tf_op jit(solution)/shard_map/ppermute | solution.py:132
  26.6 3.5 %collective-permute-start.2 = (bf16[256,256]{1,0:T(8,128)(2,1)}, bf16[256,256]{1,0:T(8,128)(2,1)}, u32[]{:S(2)}, u32[]{:S(2)}) collective-permute-start(bf16[256,256]{1,0:T(8,128)(2,1)} %pad_maximum_fusion.4), channel_id=1, source_target_pairs={{0,4},{2,6},{4,8},{6,10},{8,12},{10,14},{12,16},{14,18},{16,20},{1... | collective-permute-start | bytes 393224 | tf_op jit(solution)/shard_map/ppermute | solution.py:132
  30.1 2.6 %collective-permute-start.3 = (bf16[256,256]{1,0:T(8,128)(2,1)}, bf16[256,256]{1,0:T(8,128)(2,1)}, u32[]{:S(2)}, u32[]{:S(2)}) collective-permute-start(bf16[256,256]{1,0:T(8,128)(2,1)} %pad_maximum_fusion.4), channel_id=1, source_target_pairs={{0,2},{2,4},{4,6},{6,8},{8,10},{10,12},{12,14},{14,16},{16,18},{18... | collective-permute-start | bytes 393224 | tf_op jit(solution)/shard_map/ppermute | solution.py:132
  44.9 4.0 %fusion.1 = f32[256,1024]{0,1:T(8,128)S(1)} fusion(bf16[2048,1024]{1,0:T(8,128)(2,1)} %param.13, f32[2048]{0:T(1024)} %copy-done.14, f32[256]{0:T(256)} %copy-done.19, bf16[256,2048]{1,0:T(8,128)(2,1)S(1)} %copy-done.1), kind=kOutput, calls=%fused_computation.17 | convolution fusion | flops 1075838976 | bytes 6300672 | tf_op jit(solution)/shard_map/dot_general | solution.py:192
  50.0 2.5 %copy.77 = bf16[2,256,8,64]{3,2,1,0:T(8,128)(2,1)} copy(bf16[2,256,8,64]{1,3,2,0:T(8,128)(2,1)} %bitcast.73) | data formatting | bytes 1048576 | tf_op jit(solution)/shard_map/transpose | solution.py:238
  68.9 2.5 %copy.78 = bf16[4,16,128,256]{3,2,1,0:T(8,128)(2,1)S(1)} copy(bf16[4,16,128,256]{3,2,0,1:T(8,128)(2,1)} %bitcast.70) | data formatting | bytes 8388608 | tf_op jit(solution)/shard_map/transpose | solution.py:210
  71.4 2.2 %fusion.10 = (bf16[8192,128]{1,0:T(8,128)(2,1)}, bf16[8192,128]{1,0:T(8,128)(2,1)}) fusion(bf16[8192,256]{1,0:T(8,128)(2,1)S(1)} %bitcast.63), kind=kLoop, calls=%fused_computation.83 | loop fusion | bytes 8388608 | tf_op jit(solution)/shard_map/slice | solution.py:215
  73.6 4.1 %copy.79 = bf16[8192,128]{0,1:T(8,128)(2,1)} copy(bf16[8192,128]{1,0:T(8,128)(2,1)} %get-tuple-element.5) | data formatting | bytes 4194304 | tf_op jit(solution)/shard_map/slice | solution.py:212
  77.7 4.8 %copy.80 = bf16[8192,2,64]{2,0,1:T(8,128)(2,1)} copy(bf16[8192,2,64]{0,2,1:T(8,128)(2,1)} %bitcast.66) | data formatting | bytes 4194304 | tf_op jit(solution)/shard_map/reshape | solution.py:212
  82.5 4.1 %copy.81 = bf16[8192,128]{0,1:T(8,128)(2,1)} copy(bf16[8192,128]{1,0:T(8,128)(2,1)} %get-tuple-element.4) | data formatting | bytes 4194304 | tf_op jit(solution)/shard_map/slice | solution.py:215
  86.6 4.9 %copy.82 = bf16[8192,2,64]{2,0,1:T(8,128)(2,1)} copy(bf16[8192,2,64]{0,2,1:T(8,128)(2,1)} %bitcast.67) | data formatting | bytes 4194304 | tf_op jit(solution)/shard_map/reshape | solution.py:215
  91.4 39.4 %shard_map.120 = bf16[2,2048,64]{2,1,0:T(8,128)(2,1)} custom-call(s32[8]{0:T(128)} %reshape.346.table, bf16[2,2048,64]{2,1,0:T(8,128)(2,1)} %bitcast.68, s32[2048,1]{1,0:T(8,128)} %broadcast_in_dim_reshape.12.rg_ref, s32[2048,1]{1,0:T(8,128)} %broadcast_in_dim_reshape.13.rr_ref, s32[2048,1]{1,0:T(8,128)} %broadcast_in_dim_reshape.14.rp_ref, ...), custom_call_target="tpu_custom_call" | custom-call | tf_op jit(solution)/shard_map/pallas_call | solution.py:249
  130.9 2.5 %copy.92 = bf16[2,256,8,64]{1,3,2,0:T(8,128)(2,1)} copy(bf16[2,256,8,64]{3,2,1,0:T(8,128)(2,1)} %bitcast.69) | data formatting | bytes 1048576 | tf_op jit(solution)/shard_map/reshape | solution.py:285
  133.4 3.6 %fusion.12 = f32[256,2048]{1,0:T(8,128)S(1)} fusion(bf16[256,1024]{0,1:T(8,128)(2,1)} %bitcast.78, bf16[1024,2048]{1,0:T(8,128)(2,1)} %param.15), kind=kOutput, calls=%fused_computation.85 | convolution fusion | flops 1073741824 | bytes 6815744 | tf_op jit(solution)/shard_map/dot_general | solution.py:287
  142.3 6.4 %collective-permute-done.4 = bf16[256,1024]{1,0:T(8,128)(2,1)} collective-permute-done((bf16[256,1024]{1,0:T(8,128)(2,1)}, bf16[256,1024]{1,0:T(8,128)(2,1)}, u32[]{:S(2)}, u32[]{:S(2)}) %collective-permute-start.4) | collective-permute-done | bytes 524320 | tf_op jit(solution)/shard_map/ppermute | solution.py:293
  150.9 15.0 %collective-permute-start.5 = (bf16[32,1024]{1,0:T(8,128)(2,1)S(1)}, bf16[32,1024]{1,0:T(8,128)(2,1)S(1)}, u32[]{:S(2)}, u32[]{:S(2)}) collective-permute-start(bf16[32,1024]{1,0:T(8,128)(2,1)S(1)} %convolution_convert_fusion), channel_id=1, source_target_pairs={{0,2},{2,0},{4,6},{6,4},{8,10},{10,8},{12,14},{14,12},{16,18},{18,... | collective-permute-start | bytes 196616 | tf_op jit(solution)/shard_map/ppermute | solution.py:123
  166.9 4.3 %collective-permute-done.6 = bf16[32,1024]{1,0:T(8,128)(2,1)S(1)} collective-permute-done((bf16[32,1024]{1,0:T(8,128)(2,1)S(1)}, bf16[32,1024]{1,0:T(8,128)(2,1)S(1)}, u32[]{:S(2)}, u32[]{:S(2)}) %collective-permute-start.6) | collective-permute-done | bytes 65568 | tf_op jit(solution)/shard_map/ppermute | solution.py:123
  171.3 2.7 %collective-permute-start.7 = (bf16[32,1024]{1,0:T(8,128)(2,1)S(1)}, bf16[32,1024]{1,0:T(8,128)(2,1)S(1)}, u32[]{:S(2)}, u32[]{:S(2)}) collective-permute-start(bf16[32,1024]{1,0:T(8,128)(2,1)S(1)} %add.227), channel_id=1, source_target_pairs={{0,8},{2,10},{4,12},{6,14},{8,0},{10,2},{12,4},{14,6},{16,24},{18,... | collective-permute-start | bytes 196616 | tf_op jit(solution)/shard_map/ppermute | solution.py:123
  174.0 2.2 %collective-permute-done.7 = bf16[32,1024]{1,0:T(8,128)(2,1)S(1)} collective-permute-done((bf16[32,1024]{1,0:T(8,128)(2,1)S(1)}, bf16[32,1024]{1,0:T(8,128)(2,1)S(1)}, u32[]{:S(2)}, u32[]{:S(2)}) %collective-permute-start.7) | collective-permute-done | bytes 65568 | tf_op jit(solution)/shard_map/ppermute | solution.py:123
  176.3 7.8 %collective-permute-start.8 = (bf16[32,1024]{1,0:T(8,128)(2,1)S(1)}, bf16[32,1024]{1,0:T(8,128)(2,1)S(1)}, u32[]{:S(2)}, u32[]{:S(2)}) collective-permute-start(bf16[32,1024]{1,0:T(8,128)(2,1)S(1)} %add.228), channel_id=1, source_target_pairs={{0,16},{2,18},{4,20},{6,22},{8,24},{10,26},{12,28},{14,30},{16,0},... | collective-permute-start | bytes 196616 | tf_op jit(solution)/shard_map/ppermute | solution.py:123
  186.3 4.9 %all_gather.11 = bf16[32,2048]{1,0:T(8,128)(2,1)S(1)} all-gather(bf16[32,1024]{1,0:T(8,128)(2,1)S(1)} %add.229), channel_id=1, replica_groups=mesh['seq'=16,'mp'=2] {'mp'}, dimensions={1}, use_global_device_ids=true | all-gather | bytes 196608 | tf_op jit(solution)/shard_map/all_gather | solution.py:308
  194.3 3.4 %collective-permute-done.10 = f32[32]{0:T(128)S(1)} collective-permute-done((f32[32]{0:T(128)S(1)}, f32[32]{0:T(128)S(1)}, u32[]{:S(2)}, u32[]{:S(2)}) %collective-permute-start.10) | collective-permute-done | bytes 160 | tf_op jit(solution)/shard_map/ppermute | solution.py:123
  201.3 3.1 %collective-permute-start.12 = (f32[32]{0:T(128)S(1)}, f32[32]{0:T(128)S(1)}, u32[]{:S(2)}, u32[]{:S(2)}) collective-permute-start(f32[32]{0:T(128)S(1)} %max.28), channel_id=1, source_target_pairs={{0,16},{2,18},{4,20},{6,22},{8,24},{10,26},{12,28},{14,30},{16,0},... | collective-permute-start | bytes 392 | tf_op jit(solution)/shard_map/ppermute | solution.py:123
  (142 shorter events, 62.8 us)
Async XLA Ops:
  7.2 61.7 %all-gather.3.cloned.1.call-start = ((), (), s32[]{:S(2)}) async-start(), calls=%async_computation | async-start | bytes 4456448 | tf_op jit(solution)/shard_map/all_gather | solution.py:162
  12.0 28.2 %copy-start.5 = (bf16[256,256]{1,0:T(8,128)(2,1)}, bf16[256,256]{1,0:T(8,128)(2,1)S(1)}, u32[]{:S(2)}) copy-start(bf16[256,256]{1,0:T(8,128)(2,1)S(1)} %slice.70) | copy-start | bytes 393220
  17.0 31.9 %copy-start.7 = (bf16[256,256]{1,0:T(8,128)(2,1)}, bf16[256,256]{1,0:T(8,128)(2,1)S(1)}, u32[]{:S(2)}) copy-start(bf16[256,256]{1,0:T(8,128)(2,1)S(1)} %copy.84) | copy-start | bytes 393220
  17.8 39.6 %collective-permute-start = (bf16[256,256]{1,0:T(8,128)(2,1)}, bf16[256,256]{1,0:T(8,128)(2,1)}, u32[]{:S(2)}, u32[]{:S(2)}) collective-permute-start(bf16[256,256]{1,0:T(8,128)(2,1)} %pad_maximum_fusion.4), channel_id=1, source_target_pairs={{0,8},{2,10},{4,12},{6,14},{8,16},{10,18},{12,20},{14,22},{16,24},... | collective-permute-start | bytes 393224 | tf_op jit(solution)/shard_map/ppermute | solution.py:132
  23.4 35.0 %collective-permute-start.1 = (bf16[256,256]{1,0:T(8,128)(2,1)}, bf16[256,256]{1,0:T(8,128)(2,1)}, u32[]{:S(2)}, u32[]{:S(2)}) collective-permute-start(bf16[256,256]{1,0:T(8,128)(2,1)} %pad_maximum_fusion.4), channel_id=1, source_target_pairs={{0,6},{2,8},{4,10},{6,12},{8,14},{10,16},{12,18},{14,20},{16,22},{... | collective-permute-start | bytes 393224 | tf_op jit(solution)/shard_map/ppermute | solution.py:132
  26.6 32.7 %collective-permute-start.2 = (bf16[256,256]{1,0:T(8,128)(2,1)}, bf16[256,256]{1,0:T(8,128)(2,1)}, u32[]{:S(2)}, u32[]{:S(2)}) collective-permute-start(bf16[256,256]{1,0:T(8,128)(2,1)} %pad_maximum_fusion.4), channel_id=1, source_target_pairs={{0,4},{2,6},{4,8},{6,10},{8,12},{10,14},{12,16},{14,18},{16,20},{1... | collective-permute-start | bytes 393224 | tf_op jit(solution)/shard_map/ppermute | solution.py:132
  30.1 30.2 %collective-permute-start.3 = (bf16[256,256]{1,0:T(8,128)(2,1)}, bf16[256,256]{1,0:T(8,128)(2,1)}, u32[]{:S(2)}, u32[]{:S(2)}) collective-permute-start(bf16[256,256]{1,0:T(8,128)(2,1)} %pad_maximum_fusion.4), channel_id=1, source_target_pairs={{0,2},{2,4},{4,6},{6,8},{8,10},{10,12},{12,14},{14,16},{16,18},{18... | collective-permute-start | bytes 393224 | tf_op jit(solution)/shard_map/ppermute | solution.py:132
  44.9 4.1 %copy-start.13 = (f32[256,32]{0,1:T(8,128)S(1)}, f32[256,32]{0,1:T(8,128)}, u32[]{:S(2)}) copy-start(f32[256,32]{0,1:T(8,128)} %copy-done.12) | copy-start | bytes 98308
  139.2 9.5 %collective-permute-start.4 = (bf16[256,1024]{1,0:T(8,128)(2,1)}, bf16[256,1024]{1,0:T(8,128)(2,1)}, u32[]{:S(2)}, u32[]{:S(2)}) collective-permute-start(bf16[256,1024]{1,0:T(8,128)(2,1)} %dynamic-slice_convert_fusion), channel_id=1, source_target_pairs={{0,1},{1,0},{2,3},{3,2},{4,5},{5,4},{6,7},{7,6},{8,9},{9,8},{10,11... | collective-permute-start | bytes 1572872 | tf_op jit(solution)/shard_map/ppermute | solution.py:293
  142.3 8.4 %copy-start.18 = (s32[32]{0:T(128)S(1)}, s32[32]{0:T(128)}, u32[]{:S(2)}) copy-start(s32[32]{0:T(128)} %get-tuple-element.16) | copy-start | bytes 388
  142.3 41.8 %copy-start.16 = (bf16[2048]{0:T(1024)(128)(2,1)S(1)}, bf16[2048]{0:T(1024)(128)(2,1)}, u32[]{:S(2)}) copy-start(bf16[2048]{0:T(1024)(128)(2,1)} %param.16) | copy-start | bytes 12292
  142.3 49.2 %copy-start.2 = (bf16[2048,1000]{0,1:T(8,128)(2,1)S(1)}, bf16[2048,1000]{0,1:T(8,128)(2,1)}, u32[]{:S(2)}) copy-start(bf16[2048,1000]{0,1:T(8,128)(2,1)} %param.17) | copy-start | bytes 12288004
  150.6 42.3 %copy-start.3 = (bf16[256,1024]{1,0:T(8,128)(2,1)}, bf16[256,1024]{1,0:T(8,128)(2,1)S(1)}, u32[]{:S(2)}) copy-start(bf16[256,1024]{1,0:T(8,128)(2,1)S(1)} %add_convert_fusion) | copy-start | bytes 1572868
  150.9 15.9 %collective-permute-start.5 = (bf16[32,1024]{1,0:T(8,128)(2,1)S(1)}, bf16[32,1024]{1,0:T(8,128)(2,1)S(1)}, u32[]{:S(2)}, u32[]{:S(2)}) collective-permute-start(bf16[32,1024]{1,0:T(8,128)(2,1)S(1)} %convolution_convert_fusion), channel_id=1, source_target_pairs={{0,2},{2,0},{4,6},{6,4},{8,10},{10,8},{12,14},{14,12},{16,18},{18,... | collective-permute-start | bytes 196616 | tf_op jit(solution)/shard_map/ppermute | solution.py:123
  166.9 4.4 %collective-permute-start.6 = (bf16[32,1024]{1,0:T(8,128)(2,1)S(1)}, bf16[32,1024]{1,0:T(8,128)(2,1)S(1)}, u32[]{:S(2)}, u32[]{:S(2)}) collective-permute-start(bf16[32,1024]{1,0:T(8,128)(2,1)S(1)} %add.226), channel_id=1, source_target_pairs={{0,4},{2,6},{4,0},{6,2},{8,12},{10,14},{12,8},{14,10},{16,20},{18,... | collective-permute-start | bytes 196616 | tf_op jit(solution)/shard_map/ppermute | solution.py:123
  171.3 5.0 %collective-permute-start.7 = (bf16[32,1024]{1,0:T(8,128)(2,1)S(1)}, bf16[32,1024]{1,0:T(8,128)(2,1)S(1)}, u32[]{:S(2)}, u32[]{:S(2)}) collective-permute-start(bf16[32,1024]{1,0:T(8,128)(2,1)S(1)} %add.227), channel_id=1, source_target_pairs={{0,8},{2,10},{4,12},{6,14},{8,0},{10,2},{12,4},{14,6},{16,24},{18,... | collective-permute-start | bytes 196616 | tf_op jit(solution)/shard_map/ppermute | solution.py:123
  176.3 10.0 %collective-permute-start.8 = (bf16[32,1024]{1,0:T(8,128)(2,1)S(1)}, bf16[32,1024]{1,0:T(8,128)(2,1)S(1)}, u32[]{:S(2)}, u32[]{:S(2)}) collective-permute-start(bf16[32,1024]{1,0:T(8,128)(2,1)S(1)} %add.228), channel_id=1, source_target_pairs={{0,16},{2,18},{4,20},{6,22},{8,24},{10,26},{12,28},{14,30},{16,0},... | collective-permute-start | bytes 196616 | tf_op jit(solution)/shard_map/ppermute | solution.py:123
  191.6 15.8 %copy-start.6 = (bf16[256,256]{1,0:T(8,128)(2,1)S(1)}, bf16[256,256]{1,0:T(8,128)(2,1)}, u32[]{:S(2)}) copy-start(bf16[256,256]{1,0:T(8,128)(2,1)} %copy-done.5) | copy-start | bytes 393220
  191.6 15.8 %copy-start.8 = (bf16[256,256]{1,0:T(8,128)(2,1)S(1)}, bf16[256,256]{1,0:T(8,128)(2,1)}, u32[]{:S(2)}) copy-start(bf16[256,256]{1,0:T(8,128)(2,1)} %copy-done.7) | copy-start | bytes 393220
  193.0 1.2 collective-permute-start.9
  194.2 3.5 %collective-permute-start.10 = (f32[32]{0:T(128)S(1)}, f32[32]{0:T(128)S(1)}, u32[]{:S(2)}, u32[]{:S(2)}) collective-permute-start(f32[32]{0:T(128)S(1)} %max.26), channel_id=1, source_target_pairs={{0,4},{2,6},{4,0},{6,2},{8,12},{10,14},{12,8},{14,10},{16,20},{18,... | collective-permute-start | bytes 392 | tf_op jit(solution)/shard_map/ppermute | solution.py:123
  197.7 3.5 %collective-permute-start.11 = (f32[32]{0:T(128)S(1)}, f32[32]{0:T(128)S(1)}, u32[]{:S(2)}, u32[]{:S(2)}) collective-permute-start(f32[32]{0:T(128)S(1)} %max.27), channel_id=1, source_target_pairs={{0,8},{2,10},{4,12},{6,14},{8,0},{10,2},{12,4},{14,6},{16,24},{18,... | collective-permute-start | bytes 392 | tf_op jit(solution)/shard_map/ppermute | solution.py:123
  201.3 4.6 %collective-permute-start.12 = (f32[32]{0:T(128)S(1)}, f32[32]{0:T(128)S(1)}, u32[]{:S(2)}, u32[]{:S(2)}) collective-permute-start(f32[32]{0:T(128)S(1)} %max.28), channel_id=1, source_target_pairs={{0,16},{2,18},{4,20},{6,22},{8,24},{10,26},{12,28},{14,30},{16,0},... | collective-permute-start | bytes 392 | tf_op jit(solution)/shard_map/ppermute | solution.py:123
  205.8 3.5 %collective-permute-start.13 = (f32[32]{0:T(128)S(1)}, f32[32]{0:T(128)S(1)}, u32[]{:S(2)}, u32[]{:S(2)}) collective-permute-start(f32[32]{0:T(128)S(1)} %max.29), channel_id=1, source_target_pairs={{0,1},{1,0},{2,3},{3,2},{4,5},{5,4},{6,7},{7,6},{8,9},{9,8},{10,11... | collective-permute-start | bytes 392 | tf_op jit(solution)/shard_map/ppermute | solution.py:123
  (11 other events, 18.2 us)
Sparse Core Ops, SparseCore 0:
  10.8 58.0 all-gather.2

commit v4 on v3

--- a/solution.py
+++ b/solution.py
@@ -150,6 +150,7 @@
     request_count = lengths.shape[0]
     back_blocks = min(seq_devices - 1, -(-(MOST - 1) // token_rows))
 
+    prefix_rows = prefix_cache.shape[1]
     own_prefix = jnp.concatenate(
         [
             lax.dynamic_slice_in_dim(prefix_cache, kv_first * HD, kv_heads * HD, 2),
@@ -157,9 +158,10 @@
         ],
         2,
     )
-    prefix_rows = own_prefix.shape[1]
-    block_width = own_prefix.shape[2]
-    all_prefix = lax.all_gather(own_prefix, "seq", axis=0)
+    own_prefix = jnp.transpose(own_prefix.reshape(G, prefix_rows, 2 * kv_heads, HD), (2, 0, 1, 3))
+    all_prefix = lax.all_gather(own_prefix, "seq", axis=2, tiled=True)
+    prefix_total = seq_devices * prefix_rows
+    all_prefix = all_prefix.reshape(2 * kv_heads, G * prefix_total, HD)
 
     activations = tokens.astype(jnp.float32)
     normed = (
@@ -185,6 +187,7 @@
         ],
         1,
     )
+    own_suffix = jnp.transpose(own_suffix.reshape(token_rows, 2 * kv_heads, HD), (1, 0, 2))
     earlier = [own_suffix] + [
         shifted_back(own_suffix, "seq", distance) for distance in range(1, back_blocks + 1)
     ]
@@ -199,21 +202,7 @@
     window_blocks = back_blocks + 1
     window_rows = window_blocks * token_rows
     window_start = (seq_index - back_blocks) * token_rows
-    suffix_window = jnp.concatenate(earlier[::-1], 0)
-    suffix_keys = jnp.transpose(
-        suffix_window[:, : kv_heads * HD].reshape(window_rows, kv_heads, HD), (1, 0, 2)
-    )
-    suffix_values = jnp.transpose(
-        suffix_window[:, kv_heads * HD :].reshape(window_rows, kv_heads, HD), (1, 0, 2)
-    )
-    prefix_total = seq_devices * prefix_rows
-    prefix_flat = jnp.transpose(all_prefix, (1, 0, 2, 3)).reshape(G * prefix_total, block_width)
-    prefix_keys = jnp.transpose(
-        prefix_flat[:, : kv_heads * HD].reshape(G * prefix_total, kv_heads, HD), (1, 0, 2)
-    )
-    prefix_values = jnp.transpose(
-        prefix_flat[:, kv_heads * HD :].reshape(G * prefix_total, kv_heads, HD), (1, 0, 2)
-    )
+    suffix_window = jnp.concatenate(earlier[::-1], 1)
     suffix_chunk = min(SUFFIX_CHUNK, token_rows)
     prefix_chunk = min(PREFIX_CHUNK, prefix_total)
     chunks_per_group = prefix_total // prefix_chunk
@@ -244,6 +233,9 @@
 
     def whole(shape):
         return pl.BlockSpec(shape, lambda tile, table: (0,) * len(shape))
+
+    def half(shape, index):
+        return pl.BlockSpec((kv_heads,) + shape[1:], lambda tile, table: (index, 0, 0))
 
     row_spec = pl.BlockSpec((tile_rows, 1), lambda tile, table: (tile, 0))
     context = pl.pallas_call(
@@ -262,10 +254,10 @@
                 row_spec,
                 row_spec,
                 row_spec,
-                whole(prefix_keys.shape),
-                whole(prefix_values.shape),
-                whole(suffix_keys.shape),
-                whole(suffix_values.shape),
+                half(all_prefix.shape, 0),
+                half(all_prefix.shape, 1),
+                half(suffix_window.shape, 0),
+                half(suffix_window.shape, 1),
                 whole(key_request.shape),
                 whole(key_place.shape),
             ],
@@ -278,8 +270,8 @@
         ),
         out_shape=jax.ShapeDtypeStruct((kv_heads, token_rows * repeat_count, HD), jnp.bfloat16),
     )(
-        table, query_rows, row_group, row_request, row_place, prefix_keys, prefix_values,
-        suffix_keys, suffix_values, key_request, key_place,
+        table, query_rows, row_group, row_request, row_place, all_prefix, all_prefix,
+        suffix_window, suffix_window, key_request, key_place,
     )
     context = jnp.transpose(
         context.reshape(kv_heads, token_rows, repeat_count, HD), (1, 0, 2, 3)

time: 215 us -> 208 us (0.967); the launches traced: 217 us -> 205 us
  waiting for transfers between devices: 25 us -> 49.8 us
  local copies, waits for them, and re-layouts: 56.5 us -> 33.7 us
  starting transfers between devices: 48.9 us -> 39.2 us
  other arithmetic: 17.4 us -> 12.1 us
    all_gather x1, waiting for transfers between devices: 0.04 us -> 20.3 us  [per_device(): all_prefix = lax.all_gather(own_prefix, 'seq', axis=2, tiled=True)]
    slice x6 -> x0, local copies, waits for them, and re-layouts: 14 us -> none  [the longest x2 6.35 us: per_device(): prefix_flat[:, kv_heads * HD:].reshape(G * prefix_total, kv_heads, HD)]
    reshape x4 -> x1, local copies, waits for them, and re-layouts: 13.7 us -> 0.84 us  [per_device(): own_suffix.reshape(token_rows, 2 * kv_heads, HD)]
    ppermute x9, starting transfers between devices: 32.4 us -> 22.7 us  [butterfly(): partner = lax.ppermute(block, axis, [(i, i ^ step) for i in range(count)])]
    all_gather x0 -> x1, local copies, waits for them, and re-layouts: none -> 8.42 us  [per_device(): all_prefix = lax.all_gather(own_prefix, 'seq', axis=2, tiled=True)]
    transpose x1 -> x0, local copies, waits for them, and re-layouts: 2.46 us -> none  [per_device(): jnp.transpose(all_prefix, (1, 0, 2, 3))]
    ppermute x9, waiting for transfers between devices: 18.6 us -> 21 us  [butterfly(): partner = lax.ppermute(block, axis, [(i, i ^ step) for i in range(count)])]
    unnamed x44 -> x42, local copies, waits for them, and re-layouts: 6.21 us -> 4.83 us
  transfers between devices with their start and end apart: 15 -> 15, of which waited for: 10 -> 11; matrix products, arithmetic and copies ran while one was open for 21% -> 15% of each run, Pallas kernels for 0% -> 0%
where the time goes in v4:
time: 208 us; the launch traced here: 205 us
  waiting for transfers between devices  49.8 us (24%)
  Pallas kernels  39.4 us (19%)
  starting transfers between devices  39.2 us (19%)
  local copies, waits for them, and re-layouts  33.7 us (16%)
  between operations  14.5 us (7%)
  other arithmetic  12.1 us (6%)
  matrix products  11.4 us (5%)
  blocking collectives  4.94 us (2%)
    pallas_call x1, Pallas kernels, per_device(): pl.pallas_call(functools.partial(attention_kernel, kv_heads=kv_heads, pre...  39.4 us
    ppermute x9, starting transfers between devices, butterfly(): partner = lax.ppermute(block, axis, [(i, i ^ step) for i in range(count)])  22.7 us
    ppermute x9, waiting for transfers between devices, butterfly(): partner = lax.ppermute(block, axis, [(i, i ^ step) for i in range(count)])  21 us
    all_gather x1, waiting for transfers between devices, per_device(): all_prefix = lax.all_gather(own_prefix, 'seq', axis=2, tiled=True)  20.3 us
    ppermute x4, starting transfers between devices, shifted_back(): return lax.ppermute(block, axis, route)  15 us
    ppermute x1, waiting for transfers between devices, per_device(): received = lax.ppermute(sent.astype(jnp.bfloat16), 'mp', [(0, 1), (1, 0)])  8.47 us
    all_gather x1, local copies, waits for them, and re-layouts, per_device(): all_prefix = lax.all_gather(own_prefix, 'seq', axis=2, tiled=True)  8.42 us
    dot_general x1, matrix products, per_device(): mixture = jnp.dot(context, w_out, preferred_element_type=jnp.float32)  5.05 us
  transfers between devices with their start and end apart: 15, of which 11 were waited for; matrix products, arithmetic and copies ran while one was open for 15% of the time, Pallas kernels for 0%

profile of v4, /device:TPU:0, one launch (start us, length us, event | category | flops | bytes accessed | tf_op | source)
XLA Modules:
  0.0 205.1 jit_solution(91095693653283440)
XLA Ops:
  19.7 5.6 %collective-permute-start = (bf16[4,256,64]{2,1,0:T(8,128)(2,1)}, bf16[4,256,64]{2,1,0:T(8,128)(2,1)}, u32[]{:S(2)}, u32[]{:S(2)}) collective-permute-start(bf16[4,256,64]{2,1,0:T(8,128)(2,1)} %bitcast.19), channel_id=1, source_target_pairs={{0,8},{2,10},{4,12},{6,14},{8,16},{10,18},{12,20},{14,22},{16,24},... | collective-permute-start | bytes 393224 | tf_op jit(solution)/shard_map/ppermute | solution.py:132
  25.4 3.3 %collective-permute-start.1 = (bf16[4,256,64]{2,1,0:T(8,128)(2,1)}, bf16[4,256,64]{2,1,0:T(8,128)(2,1)}, u32[]{:S(2)}, u32[]{:S(2)}) collective-permute-start(bf16[4,256,64]{2,1,0:T(8,128)(2,1)} %bitcast.19), channel_id=1, source_target_pairs={{0,6},{2,8},{4,10},{6,12},{8,14},{10,16},{12,18},{14,20},{16,22},{... | collective-permute-start | bytes 393224 | tf_op jit(solution)/shard_map/ppermute | solution.py:132
  28.7 3.4 %collective-permute-start.2 = (bf16[4,256,64]{2,1,0:T(8,128)(2,1)}, bf16[4,256,64]{2,1,0:T(8,128)(2,1)}, u32[]{:S(2)}, u32[]{:S(2)}) collective-permute-start(bf16[4,256,64]{2,1,0:T(8,128)(2,1)} %bitcast.19), channel_id=1, source_target_pairs={{0,4},{2,6},{4,8},{6,10},{8,12},{10,14},{12,16},{14,18},{16,20},{1... | collective-permute-start | bytes 393224 | tf_op jit(solution)/shard_map/ppermute | solution.py:132
  32.1 2.6 %collective-permute-start.3 = (bf16[4,256,64]{2,1,0:T(8,128)(2,1)}, bf16[4,256,64]{2,1,0:T(8,128)(2,1)}, u32[]{:S(2)}, u32[]{:S(2)}) collective-permute-start(bf16[4,256,64]{2,1,0:T(8,128)(2,1)} %bitcast.19), channel_id=1, source_target_pairs={{0,2},{2,4},{4,6},{6,8},{8,10},{10,12},{12,14},{14,16},{16,18},{18... | collective-permute-start | bytes 393224 | tf_op jit(solution)/shard_map/ppermute | solution.py:132
  39.4 4.0 %fusion.1 = f32[256,1024]{0,1:T(8,128)S(1)} fusion(bf16[2048,1024]{1,0:T(8,128)(2,1)} %param.13, f32[2048]{0:T(1024)} %copy-done.13, f32[256]{0:T(256)} %copy-done.17, bf16[256,2048]{1,0:T(8,128)(2,1)S(1)} %copy-done.2), kind=kOutput, calls=%fused_computation.17 | convolution fusion | flops 1075838976 | bytes 6300672 | tf_op jit(solution)/shard_map/dot_general | solution.py:195
  55.1 20.3 %all-gather.2.cloned.1.call-done = bf16[4,4,2048,64]{2,3,0,1:T(8,128)(2,1)} async-done(((bf16[4,4,128,64]{2,3,0,1:T(8,128)(2,1)}), bf16[4,4,2048,64]{2,3,0,1:T(8,128)(2,1)}) %all-gather.2.cloned.1.call-update) | async-done | bytes 4194320 | tf_op jit(solution)/shard_map/all_gather | solution.py:162
  75.4 8.4 %copy.38 = bf16[4,4,2048,64]{3,2,1,0:T(8,128)(2,1)} copy(bf16[4,4,2048,64]{2,3,0,1:T(8,128)(2,1)} %all-gather.2.cloned.1.call-done) | data formatting | bytes 8388608 | tf_op jit(solution)/shard_map/all_gather | solution.py:162
  83.8 39.4 %shard_map.120 = bf16[2,2048,64]{2,1,0:T(8,128)(2,1)} custom-call(s32[8]{0:T(128)} %reshape.340.table, bf16[2,2048,64]{2,1,0:T(8,128)(2,1)} %bitcast.60, s32[2048,1]{1,0:T(8,128)} %broadcast_in_dim_reshape.12.rg_ref, s32[2048,1]{1,0:T(8,128)} %broadcast_in_dim_reshape.13.rr_ref, s32[2048,1]{1,0:T(8,128)} %broadcast_in_dim_reshape.14.rp_ref, ...), custom_call_target="tpu_custom_call" | custom-call | tf_op jit(solution)/shard_map/pallas_call | solution.py:241
  123.2 2.5 %copy.46 = bf16[2,256,8,64]{1,3,2,0:T(8,128)(2,1)} copy(bf16[2,256,8,64]{3,2,1,0:T(8,128)(2,1)} %bitcast.61) | data formatting | bytes 1048576 | tf_op jit(solution)/shard_map/reshape | solution.py:277
  125.7 5.0 %fusion.10 = f32[256,2048]{1,0:T(8,128)} fusion(bf16[256,1024]{0,1:T(8,128)(2,1)} %bitcast.66, bf16[1024,2048]{1,0:T(8,128)(2,1)} %param.15), kind=kOutput, calls=%fused_computation.83 | convolution fusion | flops 1073741824 | bytes 6815744 | tf_op jit(solution)/shard_map/dot_general | solution.py:279
  130.8 2.1 %dynamic-slice_convert_fusion = bf16[256,1024]{1,0:T(8,128)(2,1)} fusion(f32[256,2048]{1,0:T(8,128)} %fusion.10, s32[]{:T(128)S(6)} %select_n.107), kind=kLoop, calls=%fused_computation.10 | loop fusion | bytes 1048580 | tf_op jit(solution)/shard_map/convert_element_type | solution.py:285
  134.3 1.6 convert_element_type.55
  135.9 8.5 %collective-permute-done.4 = bf16[256,1024]{1,0:T(8,128)(2,1)} collective-permute-done((bf16[256,1024]{1,0:T(8,128)(2,1)}, bf16[256,1024]{1,0:T(8,128)(2,1)}, u32[]{:S(2)}, u32[]{:S(2)}) %collective-permute-start.4) | collective-permute-done | bytes 524320 | tf_op jit(solution)/shard_map/ppermute | solution.py:285
  144.4 1.9 add_convert_fusion
  146.6 3.5 %collective-permute-start.5 = (bf16[32,1024]{1,0:T(8,128)(2,1)S(1)}, bf16[32,1024]{1,0:T(8,128)(2,1)S(1)}, u32[]{:S(2)}, u32[]{:S(2)}) collective-permute-start(bf16[32,1024]{1,0:T(8,128)(2,1)S(1)} %convolution_convert_fusion), channel_id=1, source_target_pairs={{0,2},{2,0},{4,6},{6,4},{8,10},{10,8},{12,14},{14,12},{16,18},{18,... | collective-permute-start | bytes 196616 | tf_op jit(solution)/shard_map/ppermute | solution.py:123
  151.0 8.3 %collective-permute-start.6 = (bf16[32,1024]{1,0:T(8,128)(2,1)S(1)}, bf16[32,1024]{1,0:T(8,128)(2,1)S(1)}, u32[]{:S(2)}, u32[]{:S(2)}) collective-permute-start(bf16[32,1024]{1,0:T(8,128)(2,1)S(1)} %add.226), channel_id=1, source_target_pairs={{0,4},{2,6},{4,0},{6,2},{8,12},{10,14},{12,8},{14,10},{16,20},{18,... | collective-permute-start | bytes 196616 | tf_op jit(solution)/shard_map/ppermute | solution.py:123
  159.3 2.6 %collective-permute-done.6 = bf16[32,1024]{1,0:T(8,128)(2,1)S(1)} collective-permute-done((bf16[32,1024]{1,0:T(8,128)(2,1)S(1)}, bf16[32,1024]{1,0:T(8,128)(2,1)S(1)}, u32[]{:S(2)}, u32[]{:S(2)}) %collective-permute-start.6) | collective-permute-done | bytes 65568 | tf_op jit(solution)/shard_map/ppermute | solution.py:123
  162.0 4.3 %collective-permute-done.7 = bf16[32,1024]{1,0:T(8,128)(2,1)S(1)} collective-permute-done((bf16[32,1024]{1,0:T(8,128)(2,1)S(1)}, bf16[32,1024]{1,0:T(8,128)(2,1)S(1)}, u32[]{:S(2)}, u32[]{:S(2)}) %collective-permute-start.7) | collective-permute-done | bytes 65568 | tf_op jit(solution)/shard_map/ppermute | solution.py:123
  166.3 6.3 %collective-permute-start.8 = (bf16[32,1024]{1,0:T(8,128)(2,1)S(1)}, bf16[32,1024]{1,0:T(8,128)(2,1)S(1)}, u32[]{:S(2)}, u32[]{:S(2)}) collective-permute-start(bf16[32,1024]{1,0:T(8,128)(2,1)S(1)} %add.228), channel_id=1, source_target_pairs={{0,16},{2,18},{4,20},{6,22},{8,24},{10,26},{12,28},{14,30},{16,0},... | collective-permute-start | bytes 196616 | tf_op jit(solution)/shard_map/ppermute | solution.py:123
  172.6 2.2 %collective-permute-done.8 = bf16[32,1024]{1,0:T(8,128)(2,1)S(1)} collective-permute-done((bf16[32,1024]{1,0:T(8,128)(2,1)S(1)}, bf16[32,1024]{1,0:T(8,128)(2,1)S(1)}, u32[]{:S(2)}, u32[]{:S(2)}) %collective-permute-start.8) | collective-permute-done | bytes 65568 | tf_op jit(solution)/shard_map/ppermute | solution.py:123
  174.9 4.9 %all_gather.7 = bf16[32,2048]{1,0:T(8,128)(2,1)S(1)} all-gather(bf16[32,1024]{1,0:T(8,128)(2,1)S(1)} %add.229), channel_id=1, replica_groups=mesh['seq'=16,'mp'=2] {'mp'}, dimensions={1}, use_global_device_ids=true | all-gather | bytes 196608 | tf_op jit(solution)/shard_map/all_gather | solution.py:300
  182.7 3.5 %collective-permute-done.10 = f32[32]{0:T(128)S(1)} collective-permute-done((f32[32]{0:T(128)S(1)}, f32[32]{0:T(128)S(1)}, u32[]{:S(2)}, u32[]{:S(2)}) %collective-permute-start.10) | collective-permute-done | bytes 160 | tf_op jit(solution)/shard_map/ppermute | solution.py:123
  186.2 3.5 %collective-permute-done.11 = f32[32]{0:T(128)S(1)} collective-permute-done((f32[32]{0:T(128)S(1)}, f32[32]{0:T(128)S(1)}, u32[]{:S(2)}, u32[]{:S(2)}) %collective-permute-start.11) | collective-permute-done | bytes 160 | tf_op jit(solution)/shard_map/ppermute | solution.py:123
  189.8 2.9 %collective-permute-start.12 = (f32[32]{0:T(128)S(1)}, f32[32]{0:T(128)S(1)}, u32[]{:S(2)}, u32[]{:S(2)}) collective-permute-start(f32[32]{0:T(128)S(1)} %max.28), channel_id=1, source_target_pairs={{0,16},{2,18},{4,20},{6,22},{8,24},{10,26},{12,28},{14,30},{16,0},... | collective-permute-start | bytes 392 | tf_op jit(solution)/shard_map/ppermute | solution.py:123
  (132 shorter events, 39.6 us)
Async XLA Ops:
  7.2 68.2 %all-gather.2.cloned.1.call-start = ((), (), s32[]{:S(2)}) async-start(), calls=%async_computation | async-start | bytes 4456448 | tf_op jit(solution)/shard_map/all_gather | solution.py:162
  17.1 26.4 %copy-start.6 = (bf16[256,256]{1,0:T(8,128)(2,1)}, bf16[256,256]{1,0:T(8,128)(2,1)S(1)}, u32[]{:S(2)}) copy-start(bf16[256,256]{1,0:T(8,128)(2,1)S(1)} %copy.40) | copy-start | bytes 393220
  19.7 30.3 %collective-permute-start = (bf16[4,256,64]{2,1,0:T(8,128)(2,1)}, bf16[4,256,64]{2,1,0:T(8,128)(2,1)}, u32[]{:S(2)}, u32[]{:S(2)}) collective-permute-start(bf16[4,256,64]{2,1,0:T(8,128)(2,1)} %bitcast.19), channel_id=1, source_target_pairs={{0,8},{2,10},{4,12},{6,14},{8,16},{10,18},{12,20},{14,22},{16,24},... | collective-permute-start | bytes 393224 | tf_op jit(solution)/shard_map/ppermute | solution.py:132
  25.4 25.6 %collective-permute-start.1 = (bf16[4,256,64]{2,1,0:T(8,128)(2,1)}, bf16[4,256,64]{2,1,0:T(8,128)(2,1)}, u32[]{:S(2)}, u32[]{:S(2)}) collective-permute-start(bf16[4,256,64]{2,1,0:T(8,128)(2,1)} %bitcast.19), channel_id=1, source_target_pairs={{0,6},{2,8},{4,10},{6,12},{8,14},{10,16},{12,18},{14,20},{16,22},{... | collective-permute-start | bytes 393224 | tf_op jit(solution)/shard_map/ppermute | solution.py:132
  28.7 23.3 %collective-permute-start.2 = (bf16[4,256,64]{2,1,0:T(8,128)(2,1)}, bf16[4,256,64]{2,1,0:T(8,128)(2,1)}, u32[]{:S(2)}, u32[]{:S(2)}) collective-permute-start(bf16[4,256,64]{2,1,0:T(8,128)(2,1)} %bitcast.19), channel_id=1, source_target_pairs={{0,4},{2,6},{4,8},{6,10},{8,12},{10,14},{12,16},{14,18},{16,20},{1... | collective-permute-start | bytes 393224 | tf_op jit(solution)/shard_map/ppermute | solution.py:132
  32.1 20.9 %collective-permute-start.3 = (bf16[4,256,64]{2,1,0:T(8,128)(2,1)}, bf16[4,256,64]{2,1,0:T(8,128)(2,1)}, u32[]{:S(2)}, u32[]{:S(2)}) collective-permute-start(bf16[4,256,64]{2,1,0:T(8,128)(2,1)} %bitcast.19), channel_id=1, source_target_pairs={{0,2},{2,4},{4,6},{6,8},{8,10},{10,12},{12,14},{14,16},{16,18},{18... | collective-permute-start | bytes 393224 | tf_op jit(solution)/shard_map/ppermute | solution.py:132
  39.4 4.1 %copy-start.12 = (f32[256,32]{0,1:T(8,128)S(1)}, f32[256,32]{0,1:T(8,128)}, u32[]{:S(2)}) copy-start(f32[256,32]{0,1:T(8,128)} %copy-done.11) | copy-start | bytes 98308
  55.1 28.8 %copy-start.1 = (bf16[4,1280,64]{2,1,0:T(8,128)(2,1)}, bf16[4,1280,64]{2,1,0:T(8,128)(2,1)S(1)}, u32[]{:S(2)}) copy-start(bf16[4,1280,64]{2,1,0:T(8,128)(2,1)S(1)} %constant_dynamic-update-slice_fusion.sk_ref.sv_ref) | copy-start | bytes 1966084
  125.7 8.6 %copy-start.3 = (bf16[256,2048]{1,0:T(8,128)(2,1)S(1)}, bf16[256,2048]{1,0:T(8,128)(2,1)}, u32[]{:S(2)}) copy-start(bf16[256,2048]{1,0:T(8,128)(2,1)} %param.9) | copy-start | bytes 3145732
  132.9 11.5 %collective-permute-start.4 = (bf16[256,1024]{1,0:T(8,128)(2,1)}, bf16[256,1024]{1,0:T(8,128)(2,1)}, u32[]{:S(2)}, u32[]{:S(2)}) collective-permute-start(bf16[256,1024]{1,0:T(8,128)(2,1)} %dynamic-slice_convert_fusion), channel_id=1, source_target_pairs={{0,1},{1,0},{2,3},{3,2},{4,5},{5,4},{6,7},{7,6},{8,9},{9,8},{10,11... | collective-permute-start | bytes 1572872 | tf_op jit(solution)/shard_map/ppermute | solution.py:285
  135.9 10.4 %copy-start.16 = (s32[32]{0:T(128)S(1)}, s32[32]{0:T(128)}, u32[]{:S(2)}) copy-start(s32[32]{0:T(128)} %get-tuple-element.12) | copy-start | bytes 388
  135.9 36.7 %copy-start.14 = (bf16[2048]{0:T(1024)(128)(2,1)S(1)}, bf16[2048]{0:T(1024)(128)(2,1)}, u32[]{:S(2)}) copy-start(bf16[2048]{0:T(1024)(128)(2,1)} %param.16) | copy-start | bytes 12292
  135.9 44.2 %copy-start.4 = (bf16[2048,1000]{0,1:T(8,128)(2,1)S(1)}, bf16[2048,1000]{0,1:T(8,128)(2,1)}, u32[]{:S(2)}) copy-start(bf16[2048,1000]{0,1:T(8,128)(2,1)} %param.17) | copy-start | bytes 12288004
  146.3 35.1 %copy-start.5 = (bf16[256,1024]{1,0:T(8,128)(2,1)}, bf16[256,1024]{1,0:T(8,128)(2,1)S(1)}, u32[]{:S(2)}) copy-start(bf16[256,1024]{1,0:T(8,128)(2,1)S(1)} %add_convert_fusion) | copy-start | bytes 1572868
  146.6 4.4 %collective-permute-start.5 = (bf16[32,1024]{1,0:T(8,128)(2,1)S(1)}, bf16[32,1024]{1,0:T(8,128)(2,1)S(1)}, u32[]{:S(2)}, u32[]{:S(2)}) collective-permute-start(bf16[32,1024]{1,0:T(8,128)(2,1)S(1)} %convolution_convert_fusion), channel_id=1, source_target_pairs={{0,2},{2,0},{4,6},{6,4},{8,10},{10,8},{12,14},{14,12},{16,18},{18,... | collective-permute-start | bytes 196616 | tf_op jit(solution)/shard_map/ppermute | solution.py:123
  151.0 10.9 %collective-permute-start.6 = (bf16[32,1024]{1,0:T(8,128)(2,1)S(1)}, bf16[32,1024]{1,0:T(8,128)(2,1)S(1)}, u32[]{:S(2)}, u32[]{:S(2)}) collective-permute-start(bf16[32,1024]{1,0:T(8,128)(2,1)S(1)} %add.226), channel_id=1, source_target_pairs={{0,4},{2,6},{4,0},{6,2},{8,12},{10,14},{12,8},{14,10},{16,20},{18,... | collective-permute-start | bytes 196616 | tf_op jit(solution)/shard_map/ppermute | solution.py:123
  161.9 4.3 %collective-permute-start.7 = (bf16[32,1024]{1,0:T(8,128)(2,1)S(1)}, bf16[32,1024]{1,0:T(8,128)(2,1)S(1)}, u32[]{:S(2)}, u32[]{:S(2)}) collective-permute-start(bf16[32,1024]{1,0:T(8,128)(2,1)S(1)} %add.227), channel_id=1, source_target_pairs={{0,8},{2,10},{4,12},{6,14},{8,0},{10,2},{12,4},{14,6},{16,24},{18,... | collective-permute-start | bytes 196616 | tf_op jit(solution)/shard_map/ppermute | solution.py:123
  166.3 8.6 %collective-permute-start.8 = (bf16[32,1024]{1,0:T(8,128)(2,1)S(1)}, bf16[32,1024]{1,0:T(8,128)(2,1)S(1)}, u32[]{:S(2)}, u32[]{:S(2)}) collective-permute-start(bf16[32,1024]{1,0:T(8,128)(2,1)S(1)} %add.228), channel_id=1, source_target_pairs={{0,16},{2,18},{4,20},{6,22},{8,24},{10,26},{12,28},{14,30},{16,0},... | collective-permute-start | bytes 196616 | tf_op jit(solution)/shard_map/ppermute | solution.py:123
  180.1 15.7 %copy-start.7 = (bf16[256,256]{1,0:T(8,128)(2,1)S(1)}, bf16[256,256]{1,0:T(8,128)(2,1)}, u32[]{:S(2)}) copy-start(bf16[256,256]{1,0:T(8,128)(2,1)} %copy-done.6) | copy-start | bytes 393220
  181.5 1.2 collective-permute-start.9
  182.7 3.5 %collective-permute-start.10 = (f32[32]{0:T(128)S(1)}, f32[32]{0:T(128)S(1)}, u32[]{:S(2)}, u32[]{:S(2)}) collective-permute-start(f32[32]{0:T(128)S(1)} %max.26), channel_id=1, source_target_pairs={{0,4},{2,6},{4,0},{6,2},{8,12},{10,14},{12,8},{14,10},{16,20},{18,... | collective-permute-start | bytes 392 | tf_op jit(solution)/shard_map/ppermute | solution.py:123
  186.2 3.5 %collective-permute-start.11 = (f32[32]{0:T(128)S(1)}, f32[32]{0:T(128)S(1)}, u32[]{:S(2)}, u32[]{:S(2)}) collective-permute-start(f32[32]{0:T(128)S(1)} %max.27), channel_id=1, source_target_pairs={{0,8},{2,10},{4,12},{6,14},{8,0},{10,2},{12,4},{14,6},{16,24},{18,... | collective-permute-start | bytes 392 | tf_op jit(solution)/shard_map/ppermute | solution.py:123
  189.8 4.4 %collective-permute-start.12 = (f32[32]{0:T(128)S(1)}, f32[32]{0:T(128)S(1)}, u32[]{:S(2)}, u32[]{:S(2)}) collective-permute-start(f32[32]{0:T(128)S(1)} %max.28), channel_id=1, source_target_pairs={{0,16},{2,18},{4,20},{6,22},{8,24},{10,26},{12,28},{14,30},{16,0},... | collective-permute-start | bytes 392 | tf_op jit(solution)/shard_map/ppermute | solution.py:123
  194.2 3.5 %collective-permute-start.13 = (f32[32]{0:T(128)S(1)}, f32[32]{0:T(128)S(1)}, u32[]{:S(2)}, u32[]{:S(2)}) collective-permute-start(f32[32]{0:T(128)S(1)} %max.29), channel_id=1, source_target_pairs={{0,1},{1,0},{2,3},{3,2},{4,5},{5,4},{6,7},{7,6},{8,9},{9,8},{10,11... | collective-permute-start | bytes 392 | tf_op jit(solution)/shard_map/ppermute | solution.py:123
  (9 other events, 16.8 us)
Sparse Core Ops, SparseCore 0:
  10.8 64.6 all-gather.1

commit v5 on v4

--- a/solution.py
+++ b/solution.py
@@ -276,6 +276,15 @@
     context = jnp.transpose(
         context.reshape(kv_heads, token_rows, repeat_count, HD), (1, 0, 2, 3)
     ).reshape(token_rows, query_heads * HD)
+    local_last = request_end - 1 - seq_index * token_rows
+    onehot = (local_last[:, None] == jnp.arange(token_rows, dtype=jnp.int32)[None, :]).astype(
+        jnp.bfloat16
+    )
+    context_last = jnp.dot(onehot, context, preferred_element_type=jnp.float32)
+    tokens_last = jnp.dot(onehot, tokens, preferred_element_type=jnp.float32)
+    last_part = jnp.dot(
+        context_last.astype(jnp.bfloat16), w_out, preferred_element_type=jnp.float32
+    ) + jnp.where(mp_index == 0, tokens_last, 0.0)
     mixture = jnp.dot(context, w_out, preferred_element_type=jnp.float32)
     mp_devices = lax.axis_size("mp")
     own_columns = lax.dynamic_slice_in_dim(activations, mp_index * part_width, part_width, 1)
@@ -289,15 +298,11 @@
             mixture.astype(jnp.bfloat16), "mp", scatter_dimension=1, tiled=True
         ).astype(jnp.float32)
         hidden = (own_columns + mixture).astype(jnp.bfloat16)
-    local_last = request_end - 1 - seq_index * token_rows
-    onehot = (local_last[:, None] == jnp.arange(token_rows, dtype=jnp.int32)[None, :]).astype(
-        jnp.bfloat16
-    )
-    last_part = jnp.dot(onehot, hidden, preferred_element_type=jnp.float32).astype(jnp.bfloat16)
-    summed = butterfly(last_part, "seq", jnp.add)
-    if summed is None:
-        summed = lax.psum(last_part, "seq")
-    last_rows = lax.all_gather(summed, "mp", axis=1, tiled=True).astype(jnp.float32)
+    last_rows = butterfly(last_part, "seq", jnp.add)
+    last_rows = lax.psum(last_part, "seq") if last_rows is None else last_rows
+    summed = butterfly(last_rows, "mp", jnp.add)
+    last_rows = lax.psum(last_rows, "mp") if summed is None else summed
+    last_rows = last_rows.astype(jnp.bfloat16).astype(jnp.float32)
     inv_rms = lax.rsqrt(jnp.mean(last_rows * last_rows, -1, keepdims=True) + epsilon)
     last_normed = (last_rows * final_gain.astype(jnp.float32) * inv_rms).astype(jnp.bfloat16)
     logits = jnp.dot(last_normed, w_head, preferred_element_type=jnp.float32)

time: 208 us -> 221 us (1.062); the launches traced: 205 us -> 226 us
  starting transfers between devices: 39.2 us -> 54.9 us
  local copies, waits for them, and re-layouts: 33.7 us -> 48.4 us
  waiting for transfers between devices: 49.8 us -> 35.1 us
  other arithmetic: 12.1 us -> 19.6 us
  blocking collectives: 4.94 us -> 0 us
    all_gather x1, waiting for transfers between devices: 20.3 us -> 0.13 us  [per_device(): all_prefix = lax.all_gather(own_prefix, 'seq', axis=2, tiled=True)]
    ppermute x9 -> x10, starting transfers between devices: 22.7 us -> 39.3 us  [butterfly(): partner = lax.ppermute(block, axis, [(i, i ^ step) for i in range(count)])]
    ppermute x9 -> x10, waiting for transfers between devices: 21 us -> 35 us  [butterfly(): partner = lax.ppermute(block, axis, [(i, i ^ step) for i in range(count)])]
    ppermute x1, waiting for transfers between devices: 8.47 us -> 0.01 us  [per_device(): received = lax.ppermute(sent.astype(jnp.bfloat16), 'mp', [(0, 1), (1, 0)])]
    all_gather x1 -> x0, blocking collectives: 4.94 us -> none  [per_device(): lax.all_gather(summed, 'mp', axis=1, tiled=True).astype(jnp.float32)]
    unnamed x42, local copies, waits for them, and re-layouts: 4.83 us -> 9.6 us
    dot_general x1 -> x2, matrix products: 0.22 us -> 3.67 us  [the longest x1 3.34 us: per_device(): jnp.dot(context_last.astype(jnp.bfloat16), w_out, preferred_element_type=...]
  transfers between devices with their start and end apart: 15 -> 16, of which waited for: 11 -> 10; matrix products, arithmetic and copies ran while one was open for 15% -> 27% of each run, Pallas kernels for 0% -> 0%
where the time goes in v5:
time: 221 us; the launch traced here: 226 us
  starting transfers between devices  54.9 us (25%)
  local copies, waits for them, and re-layouts  48.4 us (22%)
  Pallas kernels  39.5 us (18%)
  waiting for transfers between devices  35.1 us (16%)
  other arithmetic  19.6 us (9%)
  between operations  14.4 us (7%)
  matrix products  13.6 us (6%)
    pallas_call x1, Pallas kernels, per_device(): pl.pallas_call(functools.partial(attention_kernel, kv_heads=kv_heads, pre...  39.5 us
    ppermute x10, starting transfers between devices, butterfly(): partner = lax.ppermute(block, axis, [(i, i ^ step) for i in range(count)])  39.3 us
    ppermute x10, waiting for transfers between devices, butterfly(): partner = lax.ppermute(block, axis, [(i, i ^ step) for i in range(count)])  35 us
    ppermute x4, starting transfers between devices, shifted_back(): return lax.ppermute(block, axis, route)  15 us
    unnamed x42, local copies, waits for them, and re-layouts  9.6 us
    all_gather x1, local copies, waits for them, and re-layouts, per_device(): all_prefix = lax.all_gather(own_prefix, 'seq', axis=2, tiled=True)  8.44 us
  transfers between devices with their start and end apart: 16, of which 10 were waited for; matrix products, arithmetic and copies ran while one was open for 27% of the time, Pallas kernels for 0%

profile of v5, /device:TPU:0, one launch (start us, length us, event | category | flops | bytes accessed | tf_op | source)
XLA Modules:
  0.0 225.6 jit_solution(1894239316546071087)
XLA Ops:
  18.0 5.6 %collective-permute-start = (bf16[4,256,64]{2,1,0:T(8,128)(2,1)S(1)}, bf16[4,256,64]{2,1,0:T(8,128)(2,1)}, u32[]{:S(2)}, u32[]{:S(2)}) collective-permute-start(bf16[4,256,64]{2,1,0:T(8,128)(2,1)S(1)} %bitcast.70), channel_id=1, source_target_pairs={{0,8},{2,10},{4,12},{6,14},{8,16},{10,18},{12,20},{14,22},{16,24},... | collective-permute-start | bytes 393224 | tf_op jit(solution)/shard_map/ppermute | solution.py:132
  23.6 3.3 %collective-permute-start.1 = (bf16[4,256,64]{2,1,0:T(8,128)(2,1)S(1)}, bf16[4,256,64]{2,1,0:T(8,128)(2,1)}, u32[]{:S(2)}, u32[]{:S(2)}) collective-permute-start(bf16[4,256,64]{2,1,0:T(8,128)(2,1)S(1)} %bitcast.71), channel_id=1, source_target_pairs={{0,6},{2,8},{4,10},{6,12},{8,14},{10,16},{12,18},{14,20},{16,22},{... | collective-permute-start | bytes 393224 | tf_op jit(solution)/shard_map/ppermute | solution.py:132
  26.9 3.4 %collective-permute-start.2 = (bf16[4,256,64]{2,1,0:T(8,128)(2,1)S(1)}, bf16[4,256,64]{2,1,0:T(8,128)(2,1)}, u32[]{:S(2)}, u32[]{:S(2)}) collective-permute-start(bf16[4,256,64]{2,1,0:T(8,128)(2,1)S(1)} %bitcast.72), channel_id=1, source_target_pairs={{0,4},{2,6},{4,8},{6,10},{8,12},{10,14},{12,16},{14,18},{16,20},{1... | collective-permute-start | bytes 393224 | tf_op jit(solution)/shard_map/ppermute | solution.py:132
  30.3 2.6 %collective-permute-start.3 = (bf16[4,256,64]{2,1,0:T(8,128)(2,1)S(1)}, bf16[4,256,64]{2,1,0:T(8,128)(2,1)}, u32[]{:S(2)}, u32[]{:S(2)}) collective-permute-start(bf16[4,256,64]{2,1,0:T(8,128)(2,1)S(1)} %bitcast.73), channel_id=1, source_target_pairs={{0,2},{2,4},{4,6},{6,8},{8,10},{10,12},{12,14},{14,16},{16,18},{18... | collective-permute-start | bytes 393224 | tf_op jit(solution)/shard_map/ppermute | solution.py:132
  49.3 4.0 %fusion.3 = f32[256,1024]{0,1:T(8,128)S(1)} fusion(bf16[2048,1024]{1,0:T(8,128)(2,1)} %param.13, f32[2048]{0:T(1024)} %copy-done.12, f32[256]{0:T(256)} %copy-done.17, bf16[256,2048]{1,0:T(8,128)(2,1)S(1)} %copy-done.1), kind=kOutput, calls=%fused_computation.20 | convolution fusion | flops 1075838976 | bytes 6300672 | tf_op jit(solution)/shard_map/dot_general | solution.py:195
  54.4 2.5 %copy.35 = bf16[2,256,8,64]{3,2,1,0:T(8,128)(2,1)} copy(bf16[2,256,8,64]{1,3,2,0:T(8,128)(2,1)} %bitcast.66) | data formatting | bytes 1048576 | tf_op jit(solution)/shard_map/transpose | solution.py:227
  59.6 2.2 broadcast_in_dim_reshape.12.rg_ref
  62.6 2.2 broadcast_in_dim_reshape.13.rr_ref
  65.5 2.2 broadcast_in_dim_reshape.14.rp_ref
  75.4 8.4 %copy.38 = bf16[4,4,2048,64]{3,2,1,0:T(8,128)(2,1)} copy(bf16[4,4,2048,64]{2,3,0,1:T(8,128)(2,1)} %all-gather.2.cloned.1.call-done) | data formatting | bytes 8388608 | tf_op jit(solution)/shard_map/all_gather | solution.py:162
  83.8 39.5 %shard_map.120 = bf16[2,2048,64]{2,1,0:T(8,128)(2,1)} custom-call(s32[8]{0:T(128)} %reshape.340.table, bf16[2,2048,64]{2,1,0:T(8,128)(2,1)} %bitcast.62, s32[2048,1]{1,0:T(8,128)} %broadcast_in_dim_reshape.12.rg_ref, s32[2048,1]{1,0:T(8,128)} %broadcast_in_dim_reshape.13.rr_ref, s32[2048,1]{1,0:T(8,128)} %broadcast_in_dim_reshape.14.rp_ref, ...), custom_call_target="tpu_custom_call" | custom-call | tf_op jit(solution)/shard_map/pallas_call | solution.py:241
  123.4 2.5 %copy.46 = bf16[2,256,8,64]{1,3,2,0:T(8,128)(2,1)} copy(bf16[2,256,8,64]{3,2,1,0:T(8,128)(2,1)} %bitcast.63) | data formatting | bytes 1048576 | tf_op jit(solution)/shard_map/reshape | solution.py:277
  125.9 3.3 %fusion.1 = f32[32,2048]{1,0:T(8,128)S(1)} fusion(bf16[1024,2048]{1,0:T(8,128)(2,1)} %param.15, bf16[256,1024]{0,1:T(8,128)(2,1)} %bitcast.64, s32[32]{0:T(128)S(1)} %copy-done.14), kind=kOutput, calls=%fused_computation.11 | convolution fusion | flops 151035904 | bytes 4980864 | tf_op jit(solution)/shard_map/dot_general | solution.py:285
  129.6 2.5 %collective-permute-start.5 = (f32[32,2048]{1,0:T(8,128)S(1)}, f32[32,2048]{1,0:T(8,128)S(1)}, u32[]{:S(2)}, u32[]{:S(2)}) collective-permute-start(f32[32,2048]{1,0:T(8,128)S(1)} %fusion), channel_id=1, source_target_pairs={{0,2},{2,0},{4,6},{6,4},{8,10},{10,8},{12,14},{14,12},{16,18},{18,... | collective-permute-start | bytes 786440 | tf_op jit(solution)/shard_map/ppermute | solution.py:123
  133.2 14.5 %collective-permute-start.6 = (f32[32,2048]{1,0:T(8,128)S(1)}, f32[32,2048]{1,0:T(8,128)S(1)}, u32[]{:S(2)}, u32[]{:S(2)}) collective-permute-start(f32[32,2048]{1,0:T(8,128)S(1)} %add.233), channel_id=1, source_target_pairs={{0,4},{2,6},{4,0},{6,2},{8,12},{10,14},{12,8},{14,10},{16,20},{18,... | collective-permute-start | bytes 786440 | tf_op jit(solution)/shard_map/ppermute | solution.py:123
  147.7 6.8 %collective-permute-done.6 = f32[32,2048]{1,0:T(8,128)S(1)} collective-permute-done((f32[32,2048]{1,0:T(8,128)S(1)}, f32[32,2048]{1,0:T(8,128)S(1)}, u32[]{:S(2)}, u32[]{:S(2)}) %collective-permute-start.6) | collective-permute-done | bytes 262176 | tf_op jit(solution)/shard_map/ppermute | solution.py:123
  154.7 8.0 %collective-permute-done.7 = f32[32,2048]{1,0:T(8,128)S(1)} collective-permute-done((f32[32,2048]{1,0:T(8,128)S(1)}, f32[32,2048]{1,0:T(8,128)S(1)}, u32[]{:S(2)}, u32[]{:S(2)}) %collective-permute-start.7) | collective-permute-done | bytes 262176 | tf_op jit(solution)/shard_map/ppermute | solution.py:123
  162.7 17.2 %collective-permute-start.8 = (f32[32,2048]{1,0:T(8,128)S(1)}, f32[32,2048]{1,0:T(8,128)}, u32[]{:S(2)}, u32[]{:S(2)}) collective-permute-start(f32[32,2048]{1,0:T(8,128)S(1)} %add.235), channel_id=1, source_target_pairs={{0,16},{2,18},{4,20},{6,22},{8,24},{10,26},{12,28},{14,30},{16,0},... | collective-permute-start | bytes 786440 | tf_op jit(solution)/shard_map/ppermute | solution.py:123
  179.9 10.6 %collective-permute-done.8 = f32[32,2048]{1,0:T(8,128)} collective-permute-done((f32[32,2048]{1,0:T(8,128)S(1)}, f32[32,2048]{1,0:T(8,128)}, u32[]{:S(2)}, u32[]{:S(2)}) %collective-permute-start.8) | collective-permute-done | bytes 262176 | tf_op jit(solution)/shard_map/ppermute | solution.py:123
  193.0 3.8 %fusion.14 = f32[256,2048]{1,0:T(8,128)S(1)} fusion(bf16[256,1024]{0,1:T(8,128)(2,1)} %bitcast.65, bf16[1024,2048]{1,0:T(8,128)(2,1)} %param.15), kind=kOutput, calls=%fused_computation.88 | convolution fusion | flops 1073741824 | bytes 6815744 | tf_op jit(solution)/shard_map/dot_general | solution.py:288
  204.2 1.8 collective-permute-done.11
  206.1 3.5 %collective-permute-done.12 = f32[32]{0:T(128)S(1)} collective-permute-done((f32[32]{0:T(128)S(1)}, f32[32]{0:T(128)S(1)}, u32[]{:S(2)}, u32[]{:S(2)}) %collective-permute-start.12) | collective-permute-done | bytes 160 | tf_op jit(solution)/shard_map/ppermute | solution.py:123
  212.2 1.8 collective-permute-done.13
  215.5 2.7 %add_convert_fusion = bf16[256,1024]{1,0:T(8,128)(2,1)} fusion(bf16[256,1024]{1,0:T(8,128)(2,1)} %collective-permute-done.4, f32[256,2048]{1,0:T(8,128)} %copy-done.3, s32[]{:T(128)S(6)} %select_n.102, f32[256,2048]{1,0:T(8,128)} %convert_element_type.58), kind=kLoop, calls=%fused_computation.12 | loop fusion | flops 1048576 | bytes 3145732 | tf_op jit(solution)/shard_map/convert_element_type | solution.py:295
  (134 shorter events, 56.0 us)
Async XLA Ops:
  7.2 3.5 %copy-start = (bf16[2048,512]{1,0:T(8,128)(2,1)S(1)}, bf16[2048,512]{1,0:T(8,128)(2,1)}, u32[]{:S(2)}) copy-start(bf16[2048,512]{1,0:T(8,128)(2,1)} %param.14) | copy-start | bytes 6291460
  7.2 68.2 %all-gather.2.cloned.1.call-start = ((), (), s32[]{:S(2)}) async-start(), calls=%async_computation | async-start | bytes 4456448 | tf_op jit(solution)/shard_map/all_gather | solution.py:162
  12.5 4.4 %copy-start.11 = (s32[32]{0:T(128)}, s32[32]{0:T(128)S(1)}, u32[]{:S(2)}) copy-start(s32[32]{0:T(128)S(1)} %reduce) | copy-start | bytes 388
  18.0 49.7 %collective-permute-start = (bf16[4,256,64]{2,1,0:T(8,128)(2,1)S(1)}, bf16[4,256,64]{2,1,0:T(8,128)(2,1)}, u32[]{:S(2)}, u32[]{:S(2)}) collective-permute-start(bf16[4,256,64]{2,1,0:T(8,128)(2,1)S(1)} %bitcast.70), channel_id=1, source_target_pairs={{0,8},{2,10},{4,12},{6,14},{8,16},{10,18},{12,20},{14,22},{16,24},... | collective-permute-start | bytes 393224 | tf_op jit(solution)/shard_map/ppermute | solution.py:132
  23.6 45.8 %collective-permute-start.1 = (bf16[4,256,64]{2,1,0:T(8,128)(2,1)S(1)}, bf16[4,256,64]{2,1,0:T(8,128)(2,1)}, u32[]{:S(2)}, u32[]{:S(2)}) collective-permute-start(bf16[4,256,64]{2,1,0:T(8,128)(2,1)S(1)} %bitcast.71), channel_id=1, source_target_pairs={{0,6},{2,8},{4,10},{6,12},{8,14},{10,16},{12,18},{14,20},{16,22},{... | collective-permute-start | bytes 393224 | tf_op jit(solution)/shard_map/ppermute | solution.py:132
  26.9 44.2 %collective-permute-start.2 = (bf16[4,256,64]{2,1,0:T(8,128)(2,1)S(1)}, bf16[4,256,64]{2,1,0:T(8,128)(2,1)}, u32[]{:S(2)}, u32[]{:S(2)}) collective-permute-start(bf16[4,256,64]{2,1,0:T(8,128)(2,1)S(1)} %bitcast.72), channel_id=1, source_target_pairs={{0,4},{2,6},{4,8},{6,10},{8,12},{10,14},{12,16},{14,18},{16,20},{1... | collective-permute-start | bytes 393224 | tf_op jit(solution)/shard_map/ppermute | solution.py:132
  30.3 42.5 %collective-permute-start.3 = (bf16[4,256,64]{2,1,0:T(8,128)(2,1)S(1)}, bf16[4,256,64]{2,1,0:T(8,128)(2,1)}, u32[]{:S(2)}, u32[]{:S(2)}) collective-permute-start(bf16[4,256,64]{2,1,0:T(8,128)(2,1)S(1)} %bitcast.73), channel_id=1, source_target_pairs={{0,2},{2,4},{4,6},{6,8},{8,10},{10,12},{12,14},{14,16},{16,18},{18... | collective-permute-start | bytes 393224 | tf_op jit(solution)/shard_map/ppermute | solution.py:132
  49.3 4.0 %copy-start.8 = (f32[256,32]{0,1:T(8,128)S(1)}, f32[256,32]{0,1:T(8,128)}, u32[]{:S(2)}) copy-start(f32[256,32]{0,1:T(8,128)} %copy-done.7) | copy-start | bytes 98308
  49.3 4.0 %copy-start.10 = (f32[256,32]{0,1:T(8,128)S(1)}, f32[256,32]{0,1:T(8,128)}, u32[]{:S(2)}) copy-start(f32[256,32]{0,1:T(8,128)} %copy-done.9) | copy-start | bytes 98308
  83.8 42.1 %copy-start.14 = (s32[32]{0:T(128)S(1)}, s32[32]{0:T(128)}, u32[]{:S(2)}) copy-start(s32[32]{0:T(128)} %get-tuple-element.14) | copy-start | bytes 388
  129.2 50.6 %copy-start.15 = (bf16[2048]{0:T(1024)(128)(2,1)S(1)}, bf16[2048]{0:T(1024)(128)(2,1)}, u32[]{:S(2)}) copy-start(bf16[2048]{0:T(1024)(128)(2,1)} %param.16) | copy-start | bytes 12292
  129.6 3.6 %collective-permute-start.5 = (f32[32,2048]{1,0:T(8,128)S(1)}, f32[32,2048]{1,0:T(8,128)S(1)}, u32[]{:S(2)}, u32[]{:S(2)}) collective-permute-start(f32[32,2048]{1,0:T(8,128)S(1)} %fusion), channel_id=1, source_target_pairs={{0,2},{2,0},{4,6},{6,4},{8,10},{10,8},{12,14},{14,12},{16,18},{18,... | collective-permute-start | bytes 786440 | tf_op jit(solution)/shard_map/ppermute | solution.py:123
  133.2 21.3 %collective-permute-start.6 = (f32[32,2048]{1,0:T(8,128)S(1)}, f32[32,2048]{1,0:T(8,128)S(1)}, u32[]{:S(2)}, u32[]{:S(2)}) collective-permute-start(f32[32,2048]{1,0:T(8,128)S(1)} %add.233), channel_id=1, source_target_pairs={{0,4},{2,6},{4,0},{6,2},{8,12},{10,14},{12,8},{14,10},{16,20},{18,... | collective-permute-start | bytes 786440 | tf_op jit(solution)/shard_map/ppermute | solution.py:123
  154.6 8.1 %collective-permute-start.7 = (f32[32,2048]{1,0:T(8,128)S(1)}, f32[32,2048]{1,0:T(8,128)S(1)}, u32[]{:S(2)}, u32[]{:S(2)}) collective-permute-start(f32[32,2048]{1,0:T(8,128)S(1)} %add.234), channel_id=1, source_target_pairs={{0,8},{2,10},{4,12},{6,14},{8,0},{10,2},{12,4},{14,6},{16,24},{18,... | collective-permute-start | bytes 786440 | tf_op jit(solution)/shard_map/ppermute | solution.py:123
  162.7 27.7 %collective-permute-start.8 = (f32[32,2048]{1,0:T(8,128)S(1)}, f32[32,2048]{1,0:T(8,128)}, u32[]{:S(2)}, u32[]{:S(2)}) collective-permute-start(f32[32,2048]{1,0:T(8,128)S(1)} %add.235), channel_id=1, source_target_pairs={{0,16},{2,18},{4,20},{6,22},{8,24},{10,26},{12,28},{14,30},{16,0},... | collective-permute-start | bytes 786440 | tf_op jit(solution)/shard_map/ppermute | solution.py:123
  191.4 8.2 %collective-permute-start.9 = (f32[32,2048]{1,0:T(8,128)S(1)}, f32[32,2048]{1,0:T(8,128)S(1)}, u32[]{:S(2)}, u32[]{:S(2)}) collective-permute-start(f32[32,2048]{1,0:T(8,128)S(1)} %add.236), channel_id=1, source_target_pairs={{0,1},{1,0},{2,3},{3,2},{4,5},{5,4},{6,7},{7,6},{8,9},{9,8},{10,11... | collective-permute-start | bytes 786440 | tf_op jit(solution)/shard_map/ppermute | solution.py:123
  193.0 6.9 %copy-start.2 = (bf16[2048,1000]{0,1:T(8,128)(2,1)S(1)}, bf16[2048,1000]{0,1:T(8,128)(2,1)}, u32[]{:S(2)}) copy-start(bf16[2048,1000]{0,1:T(8,128)(2,1)} %param.17) | copy-start | bytes 12288004
  198.9 16.6 %collective-permute-start.4 = (bf16[256,1024]{1,0:T(8,128)(2,1)}, bf16[256,1024]{1,0:T(8,128)(2,1)}, u32[]{:S(2)}, u32[]{:S(2)}) collective-permute-start(bf16[256,1024]{1,0:T(8,128)(2,1)} %dynamic-slice_convert_fusion), channel_id=1, source_target_pairs={{0,1},{1,0},{2,3},{3,2},{4,5},{5,4},{6,7},{7,6},{8,9},{9,8},{10,11... | collective-permute-start | bytes 1572872 | tf_op jit(solution)/shard_map/ppermute | solution.py:294
  199.9 3.6 %copy-start.5 = (bf16[256,256]{1,0:T(8,128)(2,1)S(1)}, bf16[256,256]{1,0:T(8,128)(2,1)}, u32[]{:S(2)}) copy-start(bf16[256,256]{1,0:T(8,128)(2,1)} %copy-done.4) | copy-start | bytes 393220
  201.3 1.2 collective-permute-start.10
  202.5 3.5 %collective-permute-start.11 = (f32[32]{0:T(128)S(1)}, f32[32]{0:T(128)S(1)}, u32[]{:S(2)}, u32[]{:S(2)}) collective-permute-start(f32[32]{0:T(128)S(1)} %max.26), channel_id=1, source_target_pairs={{0,4},{2,6},{4,0},{6,2},{8,12},{10,14},{12,8},{14,10},{16,20},{18,... | collective-permute-start | bytes 392 | tf_op jit(solution)/shard_map/ppermute | solution.py:123
  206.1 3.5 %collective-permute-start.12 = (f32[32]{0:T(128)S(1)}, f32[32]{0:T(128)S(1)}, u32[]{:S(2)}, u32[]{:S(2)}) collective-permute-start(f32[32]{0:T(128)S(1)} %max.27), channel_id=1, source_target_pairs={{0,8},{2,10},{4,12},{6,14},{8,0},{10,2},{12,4},{14,6},{16,24},{18,... | collective-permute-start | bytes 392 | tf_op jit(solution)/shard_map/ppermute | solution.py:123
  209.6 4.4 %collective-permute-start.13 = (f32[32]{0:T(128)S(1)}, f32[32]{0:T(128)S(1)}, u32[]{:S(2)}, u32[]{:S(2)}) collective-permute-start(f32[32]{0:T(128)S(1)} %max.28), channel_id=1, source_target_pairs={{0,16},{2,18},{4,20},{6,22},{8,24},{10,26},{12,28},{14,30},{16,0},... | collective-permute-start | bytes 392 | tf_op jit(solution)/shard_map/ppermute | solution.py:123
  214.0 4.2 %collective-permute-start.14 = (f32[32]{0:T(128)S(1)}, f32[32]{0:T(128)S(1)}, u32[]{:S(2)}, u32[]{:S(2)}) collective-permute-start(f32[32]{0:T(128)S(1)} %max.29), channel_id=1, source_target_pairs={{0,1},{1,0},{2,3},{3,2},{4,5},{5,4},{6,7},{7,6},{8,9},{9,8},{10,11... | collective-permute-start | bytes 392 | tf_op jit(solution)/shard_map/ppermute | solution.py:123
  (10 other events, 12.1 us)
Sparse Core Ops, SparseCore 0:
  10.8 64.6 all-gather.1

commit v6 on v4

--- a/solution.py
+++ b/solution.py
@@ -61,7 +61,7 @@
 
 def attention_kernel(
     table, q_ref, rg_ref, rr_ref, rp_ref, pk_ref, pv_ref, sk_ref, sv_ref, kr_ref, kp_ref,
-    o_ref, m_ref, l_ref, acc_ref, *, kv_heads, prefix_chunk, suffix_chunk, chunks_per_group
+    o_ref, m_ref, l_ref, acc_ref, *, kv_heads, prefix_chunk, suffix_chunk, parts_per_group
 ):
     tile = pl.program_id(0)
     p_lo = table[4 * tile]
@@ -92,11 +92,26 @@
             )
             m_ref[...] = new_max
 
-        def prefix_step(chunk, carry):
-            start = pl.multiple_of(chunk * prefix_chunk, prefix_chunk)
-            key = pk_ref[head, pl.ds(start, prefix_chunk), :]
-            value = pv_ref[head, pl.ds(start, prefix_chunk), :]
-            update(key, value, row_group == chunk // chunks_per_group)
+        def prefix_step(group, carry):
+            allowed = row_group == group
+            for part in range(parts_per_group):
+                lanes = slice(part * prefix_chunk, (part + 1) * prefix_chunk)
+                key_t = pk_ref[group, head, :, lanes]
+                value_t = pv_ref[group, head, :, lanes]
+                scores = jnp.dot(query, key_t, preferred_element_type=jnp.float32) * (
+                    1.0 / math.sqrt(HD)
+                )
+                scores = jnp.where(allowed, scores, -jnp.inf)
+                old_max = m_ref[...]
+                new_max = jnp.maximum(old_max, jnp.max(scores, axis=1, keepdims=True))
+                factor = jnp.exp(old_max - new_max)
+                weights = jnp.exp(scores - new_max)
+                l_ref[...] = l_ref[...] * factor + jnp.sum(weights, axis=1, keepdims=True)
+                acc_ref[...] = acc_ref[...] * factor + lax.dot_general(
+                    weights.astype(jnp.bfloat16), value_t, (((1,), (1,)), ((), ())),
+                    preferred_element_type=jnp.float32,
+                )
+                m_ref[...] = new_max
             return carry
 
         lax.fori_loop(p_lo, p_hi, prefix_step, 0)
@@ -161,7 +176,7 @@
     own_prefix = jnp.transpose(own_prefix.reshape(G, prefix_rows, 2 * kv_heads, HD), (2, 0, 1, 3))
     all_prefix = lax.all_gather(own_prefix, "seq", axis=2, tiled=True)
     prefix_total = seq_devices * prefix_rows
-    all_prefix = all_prefix.reshape(2 * kv_heads, G * prefix_total, HD)
+    all_prefix = jnp.transpose(all_prefix, (1, 0, 3, 2))
 
     activations = tokens.astype(jnp.float32)
     normed = (
@@ -218,8 +233,8 @@
     tile_rows = tile_tokens * repeat_count
     first_token = jnp.arange(tile_count, dtype=jnp.int32) * tile_tokens
     last_token = first_token + tile_tokens - 1
-    p_lo = group_of[first_token] * chunks_per_group
-    p_hi = (group_of[last_token] + 1) * chunks_per_group
+    p_lo = group_of[first_token]
+    p_hi = group_of[last_token] + 1
     s_lo = jnp.maximum((starts[request[first_token]] - window_start) // suffix_chunk, 0)
     s_hi = jnp.minimum((position[last_token] - window_start) // suffix_chunk + 1, suffix_chunks)
     table = jnp.stack([p_lo, p_hi, s_lo, s_hi], 1).reshape(-1).astype(jnp.int32)
@@ -236,6 +251,10 @@
 
     def half(shape, index):
         return pl.BlockSpec((kv_heads,) + shape[1:], lambda tile, table: (index, 0, 0))
+
+    def prefix_half(index):
+        shape = (G, kv_heads, HD, prefix_total)
+        return pl.BlockSpec(shape, lambda tile, table: (0, index, 0, 0))
 
     row_spec = pl.BlockSpec((tile_rows, 1), lambda tile, table: (tile, 0))
     context = pl.pallas_call(
@@ -244,7 +263,7 @@
             kv_heads=kv_heads,
             prefix_chunk=prefix_chunk,
             suffix_chunk=suffix_chunk,
-            chunks_per_group=chunks_per_group,
+            parts_per_group=chunks_per_group,
         ),
         grid_spec=pltpu.PrefetchScalarGridSpec(
             num_scalar_prefetch=1,
@@ -254,8 +273,8 @@
                 row_spec,
                 row_spec,
                 row_spec,
-                half(all_prefix.shape, 0),
-                half(all_prefix.shape, 1),
+                prefix_half(0),
+                prefix_half(1),
                 half(suffix_window.shape, 0),
                 half(suffix_window.shape, 1),
                 whole(key_request.shape),

time: 208 us -> 187 us (0.90)
  local copies, waits for them, and re-layouts: 33.7 us -> 26 us
  Pallas kernels: 39.4 us -> 32.7 us
  other arithmetic: 12.1 us -> 9.52 us
    all_gather x1 -> x0, local copies, waits for them, and re-layouts: 8.42 us -> none  [per_device(): all_prefix = lax.all_gather(own_prefix, 'seq', axis=2, tiled=True)]
    pallas_call x1, Pallas kernels: 39.4 us -> 32.7 us  [per_device(): pl.pallas_call(functools.partial(attention_kernel, kv_heads=kv_heads, pre...]
    ppermute x9, waiting for transfers between devices: 21 us -> 16.9 us  [butterfly(): partner = lax.ppermute(block, axis, [(i, i ^ step) for i in range(count)])]
    ppermute x1, waiting for transfers between devices: 8.47 us -> 10.6 us  [per_device(): received = lax.ppermute(sent.astype(jnp.bfloat16), 'mp', [(0, 1), (1, 0)])]
    unnamed x42 -> x40, local copies, waits for them, and re-layouts: 4.83 us -> 4.54 us
  transfers between devices with their start and end apart: 15 -> 15, of which waited for: 11 -> 11; matrix products, arithmetic and copies ran while one was open for 15% -> 16% of each run, Pallas kernels for 0% -> 0%
where the time goes in v6:
time: 187 us; the launch traced here: 186 us
  waiting for transfers between devices  49.6 us (27%)
  starting transfers between devices  37.3 us (20%)
  Pallas kernels  32.7 us (17%)
  local copies, waits for them, and re-layouts  26 us (14%)
  between operations  14.5 us (8%)
  matrix products  11.5 us (6%)
  other arithmetic  9.52 us (5%)
  blocking collectives  4.94 us (3%)
    pallas_call x1, Pallas kernels, per_device(): pl.pallas_call(functools.partial(attention_kernel, kv_heads=kv_heads, pre...  32.7 us
    all_gather x1, waiting for transfers between devices, per_device(): all_prefix = lax.all_gather(own_prefix, 'seq', axis=2, tiled=True)  22.1 us
    ppermute x9, starting transfers between devices, butterfly(): partner = lax.ppermute(block, axis, [(i, i ^ step) for i in range(count)])  20.8 us
    ppermute x9, waiting for transfers between devices, butterfly(): partner = lax.ppermute(block, axis, [(i, i ^ step) for i in range(count)])  16.9 us
    ppermute x4, starting transfers between devices, shifted_back(): return lax.ppermute(block, axis, route)  15 us
    ppermute x1, waiting for transfers between devices, per_device(): received = lax.ppermute(sent.astype(jnp.bfloat16), 'mp', [(0, 1), (1, 0)])  10.6 us
    dot_general x1, matrix products, per_device(): mixture = jnp.dot(context, w_out, preferred_element_type=jnp.float32)  5.04 us
    all_gather x1, blocking collectives, per_device(): lax.all_gather(summed, 'mp', axis=1, tiled=True).astype(jnp.float32)  4.94 us
  transfers between devices with their start and end apart: 15, of which 11 were waited for; matrix products, arithmetic and copies ran while one was open for 16% of the time, Pallas kernels for 0%

profile of v6, /device:TPU:0, one launch (start us, length us, event | category | flops | bytes accessed | tf_op | source)
XLA Modules:
  0.0 186.1 jit_solution(7463995357847631424)
XLA Ops:
  18.5 5.6 %collective-permute-start = (bf16[4,256,64]{2,1,0:T(8,128)(2,1)}, bf16[4,256,64]{2,1,0:T(8,128)(2,1)}, u32[]{:S(2)}, u32[]{:S(2)}) collective-permute-start(bf16[4,256,64]{2,1,0:T(8,128)(2,1)} %bitcast.19), channel_id=1, source_target_pairs={{0,8},{2,10},{4,12},{6,14},{8,16},{10,18},{12,20},{14,22},{16,24},... | collective-permute-start | bytes 393224 | tf_op jit(solution)/shard_map/ppermute | solution.py:147
  24.1 3.3 %collective-permute-start.1 = (bf16[4,256,64]{2,1,0:T(8,128)(2,1)}, bf16[4,256,64]{2,1,0:T(8,128)(2,1)}, u32[]{:S(2)}, u32[]{:S(2)}) collective-permute-start(bf16[4,256,64]{2,1,0:T(8,128)(2,1)} %bitcast.19), channel_id=1, source_target_pairs={{0,6},{2,8},{4,10},{6,12},{8,14},{10,16},{12,18},{14,20},{16,22},{... | collective-permute-start | bytes 393224 | tf_op jit(solution)/shard_map/ppermute | solution.py:147
  27.4 3.4 %collective-permute-start.2 = (bf16[4,256,64]{2,1,0:T(8,128)(2,1)}, bf16[4,256,64]{2,1,0:T(8,128)(2,1)}, u32[]{:S(2)}, u32[]{:S(2)}) collective-permute-start(bf16[4,256,64]{2,1,0:T(8,128)(2,1)} %bitcast.19), channel_id=1, source_target_pairs={{0,4},{2,6},{4,8},{6,10},{8,12},{10,14},{12,16},{14,18},{16,20},{1... | collective-permute-start | bytes 393224 | tf_op jit(solution)/shard_map/ppermute | solution.py:147
  30.8 2.6 %collective-permute-start.3 = (bf16[4,256,64]{2,1,0:T(8,128)(2,1)}, bf16[4,256,64]{2,1,0:T(8,128)(2,1)}, u32[]{:S(2)}, u32[]{:S(2)}) collective-permute-start(bf16[4,256,64]{2,1,0:T(8,128)(2,1)} %bitcast.19), channel_id=1, source_target_pairs={{0,2},{2,4},{4,6},{6,8},{8,10},{10,12},{12,14},{14,16},{16,18},{18... | collective-permute-start | bytes 393224 | tf_op jit(solution)/shard_map/ppermute | solution.py:147
  36.8 4.1 %fusion.1 = f32[256,1024]{0,1:T(8,128)S(1)} fusion(bf16[2048,1024]{1,0:T(8,128)(2,1)} %param.13, f32[2048]{0:T(1024)} %copy-done.13, f32[256]{0:T(256)} %copy-done.17, bf16[256,2048]{1,0:T(8,128)(2,1)S(1)} %copy-done.2), kind=kOutput, calls=%fused_computation.17 | convolution fusion | flops 1075838976 | bytes 6300672 | tf_op jit(solution)/shard_map/dot_general | solution.py:210
  53.3 22.1 %all-gather.2.cloned.1.call-done = bf16[4,4,2048,64]{2,3,0,1:T(8,128)(2,1)} async-done(((bf16[4,4,128,64]{2,3,0,1:T(8,128)(2,1)}), bf16[4,4,2048,64]{2,3,0,1:T(8,128)(2,1)}) %all-gather.2.cloned.1.call-update) | async-done | bytes 4194320 | tf_op jit(solution)/shard_map/all_gather | solution.py:177
  75.4 32.7 %shard_map.120 = bf16[2,2048,64]{2,1,0:T(8,128)(2,1)} custom-call(s32[8]{0:T(128)} %reshape.323.table, bf16[2,2048,64]{2,1,0:T(8,128)(2,1)} %bitcast.59, s32[2048,1]{1,0:T(8,128)} %broadcast_in_dim_reshape.12.rg_ref, s32[2048,1]{1,0:T(8,128)} %broadcast_in_dim_reshape.13.rr_ref, s32[2048,1]{1,0:T(8,128)} %broadcast_in_dim_reshape.14.rp_ref, ...), custom_call_target="tpu_custom_call" | custom-call | tf_op jit(solution)/shard_map/pallas_call | solution.py:260
  108.1 2.5 %copy.42 = bf16[2,256,8,64]{1,3,2,0:T(8,128)(2,1)} copy(bf16[2,256,8,64]{3,2,1,0:T(8,128)(2,1)} %bitcast.60) | data formatting | bytes 1048576 | tf_op jit(solution)/shard_map/reshape | solution.py:296
  110.6 5.0 %fusion.10 = f32[256,2048]{1,0:T(8,128)} fusion(bf16[256,1024]{0,1:T(8,128)(2,1)} %bitcast.65, bf16[1024,2048]{1,0:T(8,128)(2,1)} %param.15), kind=kOutput, calls=%fused_computation.82 | convolution fusion | flops 1073741824 | bytes 6815744 | tf_op jit(solution)/shard_map/dot_general | solution.py:298
  115.6 2.1 %dynamic-slice_convert_fusion = bf16[256,1024]{1,0:T(8,128)(2,1)} fusion(f32[256,2048]{1,0:T(8,128)} %fusion.10, s32[]{:T(128)S(6)} %select_n.107), kind=kLoop, calls=%fused_computation.10 | loop fusion | bytes 1048580 | tf_op jit(solution)/shard_map/convert_element_type | solution.py:304
  119.2 1.6 convert_element_type.55
  120.8 10.6 %collective-permute-done.4 = bf16[256,1024]{1,0:T(8,128)(2,1)} collective-permute-done((bf16[256,1024]{1,0:T(8,128)(2,1)}, bf16[256,1024]{1,0:T(8,128)(2,1)}, u32[]{:S(2)}, u32[]{:S(2)}) %collective-permute-start.4) | collective-permute-done | bytes 524320 | tf_op jit(solution)/shard_map/ppermute | solution.py:304
  131.3 1.9 %add_convert_fusion = bf16[256,1024]{1,0:T(8,128)(2,1)S(1)} fusion(bf16[256,1024]{1,0:T(8,128)(2,1)} %collective-permute-done.4, f32[256,2048]{1,0:T(8,128)} %fusion.10, s32[]{:T(128)S(6)} %select_n.94, f32[256,2048]{1,0:T(8,128)} %convert_element_type.55), kind=kLoop, calls=%fused_computation.9 | loop fusion | flops 1048576 | bytes 3145732 | tf_op jit(solution)/shard_map/convert_element_type | solution.py:305
  135.8 1.6 collective-permute-start.6
  137.4 2.8 %collective-permute-done.6 = bf16[32,1024]{1,0:T(8,128)(2,1)S(1)} collective-permute-done((bf16[32,1024]{1,0:T(8,128)(2,1)S(1)}, bf16[32,1024]{1,0:T(8,128)(2,1)S(1)}, u32[]{:S(2)}, u32[]{:S(2)}) %collective-permute-start.6) | collective-permute-done | bytes 65568 | tf_op jit(solution)/shard_map/ppermute | solution.py:138
  140.3 7.9 %collective-permute-start.7 = (bf16[32,1024]{1,0:T(8,128)(2,1)S(1)}, bf16[32,1024]{1,0:T(8,128)(2,1)S(1)}, u32[]{:S(2)}, u32[]{:S(2)}) collective-permute-start(bf16[32,1024]{1,0:T(8,128)(2,1)S(1)} %add.230), channel_id=1, source_target_pairs={{0,8},{2,10},{4,12},{6,14},{8,0},{10,2},{12,4},{14,6},{16,24},{18,... | collective-permute-start | bytes 196616 | tf_op jit(solution)/shard_map/ppermute | solution.py:138
  148.2 2.2 %collective-permute-done.7 = bf16[32,1024]{1,0:T(8,128)(2,1)S(1)} collective-permute-done((bf16[32,1024]{1,0:T(8,128)(2,1)S(1)}, bf16[32,1024]{1,0:T(8,128)(2,1)S(1)}, u32[]{:S(2)}, u32[]{:S(2)}) %collective-permute-start.7) | collective-permute-done | bytes 65568 | tf_op jit(solution)/shard_map/ppermute | solution.py:138
  150.5 2.9 %collective-permute-start.8 = (bf16[32,1024]{1,0:T(8,128)(2,1)S(1)}, bf16[32,1024]{1,0:T(8,128)(2,1)S(1)}, u32[]{:S(2)}, u32[]{:S(2)}) collective-permute-start(bf16[32,1024]{1,0:T(8,128)(2,1)S(1)} %add.231), channel_id=1, source_target_pairs={{0,16},{2,18},{4,20},{6,22},{8,24},{10,26},{12,28},{14,30},{16,0},... | collective-permute-start | bytes 196616 | tf_op jit(solution)/shard_map/ppermute | solution.py:138
  153.4 2.3 %collective-permute-done.8 = bf16[32,1024]{1,0:T(8,128)(2,1)S(1)} collective-permute-done((bf16[32,1024]{1,0:T(8,128)(2,1)S(1)}, bf16[32,1024]{1,0:T(8,128)(2,1)S(1)}, u32[]{:S(2)}, u32[]{:S(2)}) %collective-permute-start.8) | collective-permute-done | bytes 65568 | tf_op jit(solution)/shard_map/ppermute | solution.py:138
  155.7 4.9 %all_gather.7 = bf16[32,2048]{1,0:T(8,128)(2,1)S(1)} all-gather(bf16[32,1024]{1,0:T(8,128)(2,1)S(1)} %add.232), channel_id=1, replica_groups=mesh['seq'=16,'mp'=2] {'mp'}, dimensions={1}, use_global_device_ids=true | all-gather | bytes 196608 | tf_op jit(solution)/shard_map/all_gather | solution.py:319
  163.9 3.2 %collective-permute-done.10 = f32[32]{0:T(128)S(1)} collective-permute-done((f32[32]{0:T(128)S(1)}, f32[32]{0:T(128)S(1)}, u32[]{:S(2)}, u32[]{:S(2)}) %collective-permute-start.10) | collective-permute-done | bytes 160 | tf_op jit(solution)/shard_map/ppermute | solution.py:138
  167.1 2.0 %collective-permute-start.11 = (f32[32]{0:T(128)S(1)}, f32[32]{0:T(128)S(1)}, u32[]{:S(2)}, u32[]{:S(2)}) collective-permute-start(f32[32]{0:T(128)S(1)} %max.27), channel_id=1, source_target_pairs={{0,8},{2,10},{4,12},{6,14},{8,0},{10,2},{12,4},{14,6},{16,24},{18,... | collective-permute-start | bytes 392 | tf_op jit(solution)/shard_map/ppermute | solution.py:138
  169.1 1.5 collective-permute-done.11
  170.6 3.0 %collective-permute-start.12 = (f32[32]{0:T(128)S(1)}, f32[32]{0:T(128)S(1)}, u32[]{:S(2)}, u32[]{:S(2)}) collective-permute-start(f32[32]{0:T(128)S(1)} %max.28), channel_id=1, source_target_pairs={{0,16},{2,18},{4,20},{6,22},{8,24},{10,26},{12,28},{14,30},{16,0},... | collective-permute-start | bytes 392 | tf_op jit(solution)/shard_map/ppermute | solution.py:138
  (129 shorter events, 39.5 us)
Async XLA Ops:
  7.2 68.2 %all-gather.2.cloned.1.call-start = ((), (), s32[]{:S(2)}) async-start(), calls=%async_computation | async-start | bytes 4456448 | tf_op jit(solution)/shard_map/all_gather | solution.py:177
  15.8 25.1 %copy-start.6 = (bf16[256,256]{1,0:T(8,128)(2,1)}, bf16[256,256]{1,0:T(8,128)(2,1)S(1)}, u32[]{:S(2)}) copy-start(bf16[256,256]{1,0:T(8,128)(2,1)S(1)} %copy.36) | copy-start | bytes 393220
  18.5 29.8 %collective-permute-start = (bf16[4,256,64]{2,1,0:T(8,128)(2,1)}, bf16[4,256,64]{2,1,0:T(8,128)(2,1)}, u32[]{:S(2)}, u32[]{:S(2)}) collective-permute-start(bf16[4,256,64]{2,1,0:T(8,128)(2,1)} %bitcast.19), channel_id=1, source_target_pairs={{0,8},{2,10},{4,12},{6,14},{8,16},{10,18},{12,20},{14,22},{16,24},... | collective-permute-start | bytes 393224 | tf_op jit(solution)/shard_map/ppermute | solution.py:147
  24.1 25.2 %collective-permute-start.1 = (bf16[4,256,64]{2,1,0:T(8,128)(2,1)}, bf16[4,256,64]{2,1,0:T(8,128)(2,1)}, u32[]{:S(2)}, u32[]{:S(2)}) collective-permute-start(bf16[4,256,64]{2,1,0:T(8,128)(2,1)} %bitcast.19), channel_id=1, source_target_pairs={{0,6},{2,8},{4,10},{6,12},{8,14},{10,16},{12,18},{14,20},{16,22},{... | collective-permute-start | bytes 393224 | tf_op jit(solution)/shard_map/ppermute | solution.py:147
  27.4 22.9 %collective-permute-start.2 = (bf16[4,256,64]{2,1,0:T(8,128)(2,1)}, bf16[4,256,64]{2,1,0:T(8,128)(2,1)}, u32[]{:S(2)}, u32[]{:S(2)}) collective-permute-start(bf16[4,256,64]{2,1,0:T(8,128)(2,1)} %bitcast.19), channel_id=1, source_target_pairs={{0,4},{2,6},{4,8},{6,10},{8,12},{10,14},{12,16},{14,18},{16,20},{1... | collective-permute-start | bytes 393224 | tf_op jit(solution)/shard_map/ppermute | solution.py:147
  30.8 20.5 %collective-permute-start.3 = (bf16[4,256,64]{2,1,0:T(8,128)(2,1)}, bf16[4,256,64]{2,1,0:T(8,128)(2,1)}, u32[]{:S(2)}, u32[]{:S(2)}) collective-permute-start(bf16[4,256,64]{2,1,0:T(8,128)(2,1)} %bitcast.19), channel_id=1, source_target_pairs={{0,2},{2,4},{4,6},{6,8},{8,10},{10,12},{12,14},{14,16},{16,18},{18... | collective-permute-start | bytes 393224 | tf_op jit(solution)/shard_map/ppermute | solution.py:147
  36.8 4.1 %copy-start.12 = (f32[256,32]{0,1:T(8,128)S(1)}, f32[256,32]{0,1:T(8,128)}, u32[]{:S(2)}) copy-start(f32[256,32]{0,1:T(8,128)} %copy-done.11) | copy-start | bytes 98308
  53.3 22.1 %copy-start.1 = (bf16[4,1280,64]{2,1,0:T(8,128)(2,1)}, bf16[4,1280,64]{2,1,0:T(8,128)(2,1)S(1)}, u32[]{:S(2)}) copy-start(bf16[4,1280,64]{2,1,0:T(8,128)(2,1)S(1)} %constant_dynamic-update-slice_fusion.sk_ref.sv_ref) | copy-start | bytes 1966084
  110.6 8.6 %copy-start.3 = (bf16[256,2048]{1,0:T(8,128)(2,1)S(1)}, bf16[256,2048]{1,0:T(8,128)(2,1)}, u32[]{:S(2)}) copy-start(bf16[256,2048]{1,0:T(8,128)(2,1)} %param.9) | copy-start | bytes 3145732
  117.7 13.6 %collective-permute-start.4 = (bf16[256,1024]{1,0:T(8,128)(2,1)}, bf16[256,1024]{1,0:T(8,128)(2,1)}, u32[]{:S(2)}, u32[]{:S(2)}) collective-permute-start(bf16[256,1024]{1,0:T(8,128)(2,1)} %dynamic-slice_convert_fusion), channel_id=1, source_target_pairs={{0,1},{1,0},{2,3},{3,2},{4,5},{5,4},{6,7},{7,6},{8,9},{9,8},{10,11... | collective-permute-start | bytes 1572872 | tf_op jit(solution)/shard_map/ppermute | solution.py:304
  120.7 12.5 %copy-start.16 = (s32[32]{0:T(128)S(1)}, s32[32]{0:T(128)}, u32[]{:S(2)}) copy-start(s32[32]{0:T(128)} %get-tuple-element.12) | copy-start | bytes 388
  120.7 32.7 %copy-start.14 = (bf16[2048]{0:T(1024)(128)(2,1)S(1)}, bf16[2048]{0:T(1024)(128)(2,1)}, u32[]{:S(2)}) copy-start(bf16[2048]{0:T(1024)(128)(2,1)} %param.16) | copy-start | bytes 12292
  120.8 40.2 %copy-start.4 = (bf16[2048,1000]{0,1:T(8,128)(2,1)S(1)}, bf16[2048,1000]{0,1:T(8,128)(2,1)}, u32[]{:S(2)}) copy-start(bf16[2048,1000]{0,1:T(8,128)(2,1)} %param.17) | copy-start | bytes 12288004
  133.3 29.1 %copy-start.5 = (bf16[256,1024]{1,0:T(8,128)(2,1)}, bf16[256,1024]{1,0:T(8,128)(2,1)S(1)}, u32[]{:S(2)}) copy-start(bf16[256,1024]{1,0:T(8,128)(2,1)S(1)} %add_convert_fusion) | copy-start | bytes 1572868
  133.5 2.3 %collective-permute-start.5 = (bf16[32,1024]{1,0:T(8,128)(2,1)S(1)}, bf16[32,1024]{1,0:T(8,128)(2,1)S(1)}, u32[]{:S(2)}, u32[]{:S(2)}) collective-permute-start(bf16[32,1024]{1,0:T(8,128)(2,1)S(1)} %convolution_convert_fusion), channel_id=1, source_target_pairs={{0,2},{2,0},{4,6},{6,4},{8,10},{10,8},{12,14},{14,12},{16,18},{18,... | collective-permute-start | bytes 196616 | tf_op jit(solution)/shard_map/ppermute | solution.py:138
  135.8 4.4 %collective-permute-start.6 = (bf16[32,1024]{1,0:T(8,128)(2,1)S(1)}, bf16[32,1024]{1,0:T(8,128)(2,1)S(1)}, u32[]{:S(2)}, u32[]{:S(2)}) collective-permute-start(bf16[32,1024]{1,0:T(8,128)(2,1)S(1)} %add.229), channel_id=1, source_target_pairs={{0,4},{2,6},{4,0},{6,2},{8,12},{10,14},{12,8},{14,10},{16,20},{18,... | collective-permute-start | bytes 196616 | tf_op jit(solution)/shard_map/ppermute | solution.py:138
  140.3 10.2 %collective-permute-start.7 = (bf16[32,1024]{1,0:T(8,128)(2,1)S(1)}, bf16[32,1024]{1,0:T(8,128)(2,1)S(1)}, u32[]{:S(2)}, u32[]{:S(2)}) collective-permute-start(bf16[32,1024]{1,0:T(8,128)(2,1)S(1)} %add.230), channel_id=1, source_target_pairs={{0,8},{2,10},{4,12},{6,14},{8,0},{10,2},{12,4},{14,6},{16,24},{18,... | collective-permute-start | bytes 196616 | tf_op jit(solution)/shard_map/ppermute | solution.py:138
  150.5 5.2 %collective-permute-start.8 = (bf16[32,1024]{1,0:T(8,128)(2,1)S(1)}, bf16[32,1024]{1,0:T(8,128)(2,1)S(1)}, u32[]{:S(2)}, u32[]{:S(2)}) collective-permute-start(bf16[32,1024]{1,0:T(8,128)(2,1)S(1)} %add.231), channel_id=1, source_target_pairs={{0,16},{2,18},{4,20},{6,22},{8,24},{10,26},{12,28},{14,30},{16,0},... | collective-permute-start | bytes 196616 | tf_op jit(solution)/shard_map/ppermute | solution.py:138
  160.9 15.7 %copy-start.7 = (bf16[256,256]{1,0:T(8,128)(2,1)S(1)}, bf16[256,256]{1,0:T(8,128)(2,1)}, u32[]{:S(2)}) copy-start(bf16[256,256]{1,0:T(8,128)(2,1)} %copy-done.6) | copy-start | bytes 393220
  162.3 1.2 collective-permute-start.9
  163.5 3.5 %collective-permute-start.10 = (f32[32]{0:T(128)S(1)}, f32[32]{0:T(128)S(1)}, u32[]{:S(2)}, u32[]{:S(2)}) collective-permute-start(f32[32]{0:T(128)S(1)} %max.26), channel_id=1, source_target_pairs={{0,4},{2,6},{4,0},{6,2},{8,12},{10,14},{12,8},{14,10},{16,20},{18,... | collective-permute-start | bytes 392 | tf_op jit(solution)/shard_map/ppermute | solution.py:138
  167.1 3.5 %collective-permute-start.11 = (f32[32]{0:T(128)S(1)}, f32[32]{0:T(128)S(1)}, u32[]{:S(2)}, u32[]{:S(2)}) collective-permute-start(f32[32]{0:T(128)S(1)} %max.27), channel_id=1, source_target_pairs={{0,8},{2,10},{4,12},{6,14},{8,0},{10,2},{12,4},{14,6},{16,24},{18,... | collective-permute-start | bytes 392 | tf_op jit(solution)/shard_map/ppermute | solution.py:138
  170.6 4.5 %collective-permute-start.12 = (f32[32]{0:T(128)S(1)}, f32[32]{0:T(128)S(1)}, u32[]{:S(2)}, u32[]{:S(2)}) collective-permute-start(f32[32]{0:T(128)S(1)} %max.28), channel_id=1, source_target_pairs={{0,16},{2,18},{4,20},{6,22},{8,24},{10,26},{12,28},{14,30},{16,0},... | collective-permute-start | bytes 392 | tf_op jit(solution)/shard_map/ppermute | solution.py:138
  175.2 3.5 %collective-permute-start.13 = (f32[32]{0:T(128)S(1)}, f32[32]{0:T(128)S(1)}, u32[]{:S(2)}, u32[]{:S(2)}) collective-permute-start(f32[32]{0:T(128)S(1)} %max.29), channel_id=1, source_target_pairs={{0,1},{1,0},{2,3},{3,2},{4,5},{5,4},{6,7},{7,6},{8,9},{9,8},{10,11... | collective-permute-start | bytes 392 | tf_op jit(solution)/shard_map/ppermute | solution.py:138
  (9 other events, 16.7 us)
Sparse Core Ops, SparseCore 0:
  10.8 64.5 all-gather.1

commit v7 on v4

--- a/solution.py
+++ b/solution.py
@@ -59,47 +59,33 @@
     return (new_max, new_sum, numerator)
 
 
-def attention_kernel(
-    table, q_ref, rg_ref, rr_ref, rp_ref, pk_ref, pv_ref, sk_ref, sv_ref, kr_ref, kp_ref,
-    o_ref, m_ref, l_ref, acc_ref, *, kv_heads, prefix_chunk, suffix_chunk, chunks_per_group
+def online_update(m_ref, l_ref, acc_ref, head, scores, value, value_contract):
+    old_max = m_ref[head]
+    new_max = jnp.maximum(old_max, jnp.max(scores, axis=1, keepdims=True))
+    factor = jnp.exp(old_max - new_max)
+    weights = jnp.exp(scores - new_max)
+    l_ref[head] = l_ref[head] * factor + jnp.sum(weights, axis=1, keepdims=True)
+    acc_ref[head] = acc_ref[head] * factor + lax.dot_general(
+        weights.astype(jnp.bfloat16), value, (((1,), (value_contract,)), ((), ())),
+        preferred_element_type=jnp.float32,
+    )
+    m_ref[head] = new_max
+
+
+def suffix_kernel(
+    table, q_ref, rr_ref, rp_ref, sk_ref, sv_ref, kr_ref, kp_ref, m_ref, l_ref, acc_ref,
+    *, kv_heads, suffix_chunk
 ):
     tile = pl.program_id(0)
-    p_lo = table[4 * tile]
-    p_hi = table[4 * tile + 1]
     s_lo = table[4 * tile + 2]
     s_hi = table[4 * tile + 3]
-    row_group = rg_ref[...]
     row_request = rr_ref[...]
     row_place = rp_ref[...]
     for head in range(kv_heads):
         query = q_ref[head]
-        m_ref[...] = jnp.full(m_ref.shape, -1e30, jnp.float32)
-        l_ref[...] = jnp.zeros(l_ref.shape, jnp.float32)
-        acc_ref[...] = jnp.zeros(acc_ref.shape, jnp.float32)
-
-        def update(key, value, allowed):
-            scores = lax.dot_general(
-                query, key, (((1,), (1,)), ((), ())), preferred_element_type=jnp.float32
-            ) * (1.0 / math.sqrt(HD))
-            scores = jnp.where(allowed, scores, -jnp.inf)
-            old_max = m_ref[...]
-            new_max = jnp.maximum(old_max, jnp.max(scores, axis=1, keepdims=True))
-            factor = jnp.exp(old_max - new_max)
-            weights = jnp.exp(scores - new_max)
-            l_ref[...] = l_ref[...] * factor + jnp.sum(weights, axis=1, keepdims=True)
-            acc_ref[...] = acc_ref[...] * factor + jnp.dot(
-                weights.astype(jnp.bfloat16), value, preferred_element_type=jnp.float32
-            )
-            m_ref[...] = new_max
-
-        def prefix_step(chunk, carry):
-            start = pl.multiple_of(chunk * prefix_chunk, prefix_chunk)
-            key = pk_ref[head, pl.ds(start, prefix_chunk), :]
-            value = pv_ref[head, pl.ds(start, prefix_chunk), :]
-            update(key, value, row_group == chunk // chunks_per_group)
-            return carry
-
-        lax.fori_loop(p_lo, p_hi, prefix_step, 0)
+        m_ref[head] = jnp.full(m_ref.shape[1:], -1e30, jnp.float32)
+        l_ref[head] = jnp.zeros(l_ref.shape[1:], jnp.float32)
+        acc_ref[head] = jnp.zeros(acc_ref.shape[1:], jnp.float32)
 
         def suffix_step(chunk, carry):
             start = pl.multiple_of(chunk * suffix_chunk, suffix_chunk)
@@ -107,11 +93,46 @@
             value = sv_ref[head, pl.ds(start, suffix_chunk), :]
             key_request = kr_ref[pl.ds(chunk, 1), :]
             key_place = kp_ref[pl.ds(chunk, 1), :]
-            update(key, value, (row_request == key_request) & (key_place <= row_place))
+            scores = lax.dot_general(
+                query, key, (((1,), (1,)), ((), ())), preferred_element_type=jnp.float32
+            ) * (1.0 / math.sqrt(HD))
+            allowed = (row_request == key_request) & (key_place <= row_place)
+            scores = jnp.where(allowed, scores, -jnp.inf)
+            online_update(m_ref, l_ref, acc_ref, head, scores, value, 0)
             return carry
 
         lax.fori_loop(s_lo, s_hi, suffix_step, 0)
-        o_ref[head] = (acc_ref[...] / l_ref[...]).astype(o_ref.dtype)
+
+
+def prefix_kernel(
+    table, q_ref, rg_ref, pk_ref, pv_ref, mi_ref, li_ref, ai_ref, o_ref, m_ref, l_ref, acc_ref,
+    *, kv_heads, prefix_chunk, parts_per_group
+):
+    tile = pl.program_id(0)
+    p_lo = table[4 * tile]
+    p_hi = table[4 * tile + 1]
+    row_group = rg_ref[...]
+    for head in range(kv_heads):
+        query = q_ref[head]
+        m_ref[0] = mi_ref[head]
+        l_ref[0] = li_ref[head]
+        acc_ref[0] = ai_ref[head]
+
+        def prefix_step(group, carry):
+            allowed = row_group == group
+            for part in range(parts_per_group):
+                lanes = slice(part * prefix_chunk, (part + 1) * prefix_chunk)
+                key_t = pk_ref[group, head, :, lanes]
+                value_t = pv_ref[group, head, :, lanes]
+                scores = jnp.dot(query, key_t, preferred_element_type=jnp.float32) * (
+                    1.0 / math.sqrt(HD)
+                )
+                scores = jnp.where(allowed, scores, -jnp.inf)
+                online_update(m_ref, l_ref, acc_ref, 0, scores, value_t, 1)
+            return carry
+
+        lax.fori_loop(p_lo, p_hi, prefix_step, 0)
+        o_ref[head] = (acc_ref[0] / l_ref[0]).astype(o_ref.dtype)
 
 
 def butterfly(block, axis, combine):
@@ -161,7 +182,7 @@
     own_prefix = jnp.transpose(own_prefix.reshape(G, prefix_rows, 2 * kv_heads, HD), (2, 0, 1, 3))
     all_prefix = lax.all_gather(own_prefix, "seq", axis=2, tiled=True)
     prefix_total = seq_devices * prefix_rows
-    all_prefix = all_prefix.reshape(2 * kv_heads, G * prefix_total, HD)
+    all_prefix = jnp.transpose(all_prefix, (1, 0, 3, 2))
 
     activations = tokens.astype(jnp.float32)
     normed = (
@@ -218,8 +239,8 @@
     tile_rows = tile_tokens * repeat_count
     first_token = jnp.arange(tile_count, dtype=jnp.int32) * tile_tokens
     last_token = first_token + tile_tokens - 1
-    p_lo = group_of[first_token] * chunks_per_group
-    p_hi = (group_of[last_token] + 1) * chunks_per_group
+    p_lo = group_of[first_token]
+    p_hi = group_of[last_token] + 1
     s_lo = jnp.maximum((starts[request[first_token]] - window_start) // suffix_chunk, 0)
     s_hi = jnp.minimum((position[last_token] - window_start) // suffix_chunk + 1, suffix_chunks)
     table = jnp.stack([p_lo, p_hi, s_lo, s_hi], 1).reshape(-1).astype(jnp.int32)
@@ -237,42 +258,61 @@
     def half(shape, index):
         return pl.BlockSpec((kv_heads,) + shape[1:], lambda tile, table: (index, 0, 0))
 
+    def prefix_half(index):
+        shape = (G, kv_heads, HD, prefix_total)
+        return pl.BlockSpec(shape, lambda tile, table: (0, index, 0, 0))
+
     row_spec = pl.BlockSpec((tile_rows, 1), lambda tile, table: (tile, 0))
-    context = pl.pallas_call(
-        functools.partial(
-            attention_kernel,
-            kv_heads=kv_heads,
-            prefix_chunk=prefix_chunk,
-            suffix_chunk=suffix_chunk,
-            chunks_per_group=chunks_per_group,
-        ),
+    rows_total = token_rows * repeat_count
+    state_shapes = [
+        jax.ShapeDtypeStruct((kv_heads, rows_total, 1), jnp.float32),
+        jax.ShapeDtypeStruct((kv_heads, rows_total, 1), jnp.float32),
+        jax.ShapeDtypeStruct((kv_heads, rows_total, HD), jnp.float32),
+    ]
+    state_specs = [
+        pl.BlockSpec((kv_heads, tile_rows, 1), lambda tile, table: (0, tile, 0)),
+        pl.BlockSpec((kv_heads, tile_rows, 1), lambda tile, table: (0, tile, 0)),
+        pl.BlockSpec((kv_heads, tile_rows, HD), lambda tile, table: (0, tile, 0)),
+    ]
+    query_spec = pl.BlockSpec((kv_heads, tile_rows, HD), lambda tile, table: (0, tile, 0))
+    state = pl.pallas_call(
+        functools.partial(suffix_kernel, kv_heads=kv_heads, suffix_chunk=suffix_chunk),
         grid_spec=pltpu.PrefetchScalarGridSpec(
             num_scalar_prefetch=1,
             grid=(tile_count,),
             in_specs=[
-                pl.BlockSpec((kv_heads, tile_rows, HD), lambda tile, table: (0, tile, 0)),
+                query_spec,
                 row_spec,
                 row_spec,
-                row_spec,
-                half(all_prefix.shape, 0),
-                half(all_prefix.shape, 1),
                 half(suffix_window.shape, 0),
                 half(suffix_window.shape, 1),
                 whole(key_request.shape),
                 whole(key_place.shape),
             ],
-            out_specs=pl.BlockSpec((kv_heads, tile_rows, HD), lambda tile, table: (0, tile, 0)),
+            out_specs=state_specs,
+        ),
+        out_shape=state_shapes,
+    )(table, query_rows, row_request, row_place, suffix_window, suffix_window, key_request, key_place)
+    context = pl.pallas_call(
+        functools.partial(
+            prefix_kernel,
+            kv_heads=kv_heads,
+            prefix_chunk=prefix_chunk,
+            parts_per_group=chunks_per_group,
+        ),
+        grid_spec=pltpu.PrefetchScalarGridSpec(
+            num_scalar_prefetch=1,
+            grid=(tile_count,),
+            in_specs=[query_spec, row_spec, prefix_half(0), prefix_half(1)] + state_specs,
+            out_specs=query_spec,
             scratch_shapes=[
-                pltpu.VMEM((tile_rows, 1), jnp.float32),
-                pltpu.VMEM((tile_rows, 1), jnp.float32),
-                pltpu.VMEM((tile_rows, HD), jnp.float32),
+                pltpu.VMEM((1, tile_rows, 1), jnp.float32),
+                pltpu.VMEM((1, tile_rows, 1), jnp.float32),
+                pltpu.VMEM((1, tile_rows, HD), jnp.float32),
             ],
         ),
-        out_shape=jax.ShapeDtypeStruct((kv_heads, token_rows * repeat_count, HD), jnp.bfloat16),
-    )(
-        table, query_rows, row_group, row_request, row_place, all_prefix, all_prefix,
-        suffix_window, suffix_window, key_request, key_place,
-    )
+        out_shape=jax.ShapeDtypeStruct((kv_heads, rows_total, HD), jnp.bfloat16),
+    )(table, query_rows, row_group, all_prefix, all_prefix, *state)
     context = jnp.transpose(
         context.reshape(kv_heads, token_rows, repeat_count, HD), (1, 0, 2, 3)
     ).reshape(token_rows, query_heads * HD)

time: 208 us -> 182 us (0.88)
  waiting for transfers between devices: 49.8 us -> 39.1 us
  local copies, waits for them, and re-layouts: 33.7 us -> 27.1 us
  other arithmetic: 12.1 us -> 9.52 us
    all_gather x1, waiting for transfers between devices: 20.3 us -> 11.7 us  [per_device(): all_prefix = lax.all_gather(own_prefix, 'seq', axis=2, tiled=True)]
    all_gather x1 -> x0, local copies, waits for them, and re-layouts: 8.42 us -> none  [per_device(): all_prefix = lax.all_gather(own_prefix, 'seq', axis=2, tiled=True)]
    unnamed x42, local copies, waits for them, and re-layouts: 4.83 us -> 6.93 us
    pallas_call x1 -> x2, Pallas kernels: 39.4 us -> 37.5 us  [the longest x1 28.1 us: per_device(): pl.pallas_call(functools.partial(prefix_kernel, kv_heads=kv_heads, prefix...]
  transfers between devices with their start and end apart: 15 -> 15, of which waited for: 11 -> 11; matrix products, arithmetic and copies ran while one was open for 15% -> 17% of each run, Pallas kernels for 0% -> 5%
where the time goes in v7:
time: 182 us; the launch traced here: 181 us
  waiting for transfers between devices  39.1 us (21%)
  starting transfers between devices  37.7 us (21%)
  Pallas kernels  37.5 us (21%)
  local copies, waits for them, and re-layouts  27.1 us (15%)
  between operations  14.5 us (8%)
  matrix products  10.1 us (6%)
  other arithmetic  9.52 us (5%)
  blocking collectives  4.94 us (3%)
    pallas_call x1, Pallas kernels, per_device(): pl.pallas_call(functools.partial(prefix_kernel, kv_heads=kv_heads, prefix...  28.1 us
    ppermute x9, starting transfers between devices, butterfly(): partner = lax.ppermute(block, axis, [(i, i ^ step) for i in range(count)])  21.2 us
    ppermute x9, waiting for transfers between devices, butterfly(): partner = lax.ppermute(block, axis, [(i, i ^ step) for i in range(count)])  20.9 us
    ppermute x4, starting transfers between devices, shifted_back(): return lax.ppermute(block, axis, route)  15 us
    all_gather x1, waiting for transfers between devices, per_device(): all_prefix = lax.all_gather(own_prefix, 'seq', axis=2, tiled=True)  11.7 us
    pallas_call x1, Pallas kernels, per_device(): pl.pallas_call(functools.partial(suffix_kernel, kv_heads=kv_heads, suffix...  9.39 us
    unnamed x42, local copies, waits for them, and re-layouts  6.93 us
    ppermute x1, waiting for transfers between devices, per_device(): received = lax.ppermute(sent.astype(jnp.bfloat16), 'mp', [(0, 1), (1, 0)])  6.48 us
  transfers between devices with their start and end apart: 15, of which 11 were waited for; matrix products, arithmetic and copies ran while one was open for 17% of the time, Pallas kernels for 5%

profile of v7, /device:TPU:0, one launch (start us, length us, event | category | flops | bytes accessed | tf_op | source)
XLA Modules:
  0.0 180.5 jit_solution(4835917884487146)
XLA Ops:
  18.5 5.6 %collective-permute-start = (bf16[4,256,64]{2,1,0:T(8,128)(2,1)}, bf16[4,256,64]{2,1,0:T(8,128)(2,1)}, u32[]{:S(2)}, u32[]{:S(2)}) collective-permute-start(bf16[4,256,64]{2,1,0:T(8,128)(2,1)} %bitcast.19), channel_id=1, source_target_pairs={{0,8},{2,10},{4,12},{6,14},{8,16},{10,18},{12,20},{14,22},{16,24},... | collective-permute-start | bytes 393224 | tf_op jit(solution)/shard_map/ppermute | solution.py:153
  24.1 3.3 %collective-permute-start.1 = (bf16[4,256,64]{2,1,0:T(8,128)(2,1)}, bf16[4,256,64]{2,1,0:T(8,128)(2,1)}, u32[]{:S(2)}, u32[]{:S(2)}) collective-permute-start(bf16[4,256,64]{2,1,0:T(8,128)(2,1)} %bitcast.19), channel_id=1, source_target_pairs={{0,6},{2,8},{4,10},{6,12},{8,14},{10,16},{12,18},{14,20},{16,22},{... | collective-permute-start | bytes 393224 | tf_op jit(solution)/shard_map/ppermute | solution.py:153
  27.4 3.4 %collective-permute-start.2 = (bf16[4,256,64]{2,1,0:T(8,128)(2,1)}, bf16[4,256,64]{2,1,0:T(8,128)(2,1)}, u32[]{:S(2)}, u32[]{:S(2)}) collective-permute-start(bf16[4,256,64]{2,1,0:T(8,128)(2,1)} %bitcast.19), channel_id=1, source_target_pairs={{0,4},{2,6},{4,8},{6,10},{8,12},{10,14},{12,16},{14,18},{16,20},{1... | collective-permute-start | bytes 393224 | tf_op jit(solution)/shard_map/ppermute | solution.py:153
  30.8 2.6 %collective-permute-start.3 = (bf16[4,256,64]{2,1,0:T(8,128)(2,1)}, bf16[4,256,64]{2,1,0:T(8,128)(2,1)}, u32[]{:S(2)}, u32[]{:S(2)}) collective-permute-start(bf16[4,256,64]{2,1,0:T(8,128)(2,1)} %bitcast.19), channel_id=1, source_target_pairs={{0,2},{2,4},{4,6},{6,8},{8,10},{10,12},{12,14},{14,16},{16,18},{18... | collective-permute-start | bytes 393224 | tf_op jit(solution)/shard_map/ppermute | solution.py:153
  36.8 4.0 %fusion.1 = f32[256,1024]{0,1:T(8,128)S(1)} fusion(bf16[2048,1024]{1,0:T(8,128)(2,1)} %param.13, f32[2048]{0:T(1024)} %copy-done.14, f32[256]{0:T(256)} %copy-done.18, bf16[256,2048]{1,0:T(8,128)(2,1)S(1)} %copy-done.2), kind=kOutput, calls=%fused_computation.17 | convolution fusion | flops 1075838976 | bytes 6300672 | tf_op jit(solution)/shard_map/dot_general | solution.py:216
  54.3 9.4 %shard_map.120 = (f32[2,2048,1]{2,1,0:T(8,128)}, f32[2,2048,1]{2,1,0:T(8,128)}, f32[2,2048,64]{2,1,0:T(8,128)}) custom-call(s32[8]{0:T(128)} %reshape.323.table, bf16[2,2048,64]{2,1,0:T(8,128)(2,1)} %bitcast.59, s32[2048,1]{1,0:T(8,128)} %broadcast_in_dim_reshape.13.rr_ref, s32[2048,1]{1,0:T(8,128)} %broadcast_in_dim_reshape.14.rp_ref, ...), custom_call_target="tpu_custom_call" | custom-call | tf_op jit(solution)/shard_map/pallas_call | solution.py:278
  63.7 11.7 %all-gather.2.cloned.1.call-done = bf16[4,4,2048,64]{2,3,0,1:T(8,128)(2,1)} async-done(((bf16[4,4,128,64]{2,3,0,1:T(8,128)(2,1)}), bf16[4,4,2048,64]{2,3,0,1:T(8,128)(2,1)}) %all-gather.2.cloned.1.call-update) | async-done | bytes 4194320 | tf_op jit(solution)/shard_map/all_gather | solution.py:183
  75.4 28.1 %shard_map.121 = bf16[2,2048,64]{2,1,0:T(8,128)(2,1)} custom-call(s32[8]{0:T(128)} %reshape.323.table, bf16[2,2048,64]{2,1,0:T(8,128)(2,1)} %bitcast.60, s32[2048,1]{1,0:T(8,128)} %broadcast_in_dim_reshape.12.rg_ref, bf16[4,4,64,2048]{3,2,1,0:T(8,128)(2,1)} %bitcast.57, bf16[4,4,64,2048]{3,2,1,0:T(8,128)(2,1)} %bitcast.58, ...), custom_call_target="tpu_custom_call" | custom-call | tf_op jit(solution)/shard_map/pallas_call | solution.py:296
  103.5 2.5 %copy.42 = bf16[2,256,8,64]{1,3,2,0:T(8,128)(2,1)} copy(bf16[2,256,8,64]{3,2,1,0:T(8,128)(2,1)} %bitcast.61) | data formatting | bytes 1048576 | tf_op jit(solution)/shard_map/reshape | solution.py:317
  106.0 3.7 %fusion.10 = f32[256,2048]{1,0:T(8,128)S(1)} fusion(bf16[256,1024]{0,1:T(8,128)(2,1)} %bitcast.66, bf16[1024,2048]{1,0:T(8,128)(2,1)} %param.15), kind=kOutput, calls=%fused_computation.82 | convolution fusion | flops 1073741824 | bytes 6815744 | tf_op jit(solution)/shard_map/dot_general | solution.py:319
  113.3 1.5 convert_element_type.55
  114.9 6.5 %collective-permute-done.4 = bf16[256,1024]{1,0:T(8,128)(2,1)} collective-permute-done((bf16[256,1024]{1,0:T(8,128)(2,1)}, bf16[256,1024]{1,0:T(8,128)(2,1)}, u32[]{:S(2)}, u32[]{:S(2)}) %collective-permute-start.4) | collective-permute-done | bytes 524320 | tf_op jit(solution)/shard_map/ppermute | solution.py:325
  121.4 1.9 %add_convert_fusion = bf16[256,1024]{1,0:T(8,128)(2,1)S(1)} fusion(bf16[256,1024]{1,0:T(8,128)(2,1)} %collective-permute-done.4, f32[256,2048]{1,0:T(8,128)} %copy-done.6, s32[]{:T(128)S(6)} %select_n.94, f32[256,2048]{1,0:T(8,128)} %convert_element_type.55), kind=kLoop, calls=%fused_computation.9 | loop fusion | flops 1048576 | bytes 3145732 | tf_op jit(solution)/shard_map/convert_element_type | solution.py:326
  123.6 10.0 %collective-permute-start.5 = (bf16[32,1024]{1,0:T(8,128)(2,1)S(1)}, bf16[32,1024]{1,0:T(8,128)(2,1)S(1)}, u32[]{:S(2)}, u32[]{:S(2)}) collective-permute-start(bf16[32,1024]{1,0:T(8,128)(2,1)S(1)} %convolution_convert_fusion), channel_id=1, source_target_pairs={{0,2},{2,0},{4,6},{6,4},{8,10},{10,8},{12,14},{14,12},{16,18},{18,... | collective-permute-start | bytes 196616 | tf_op jit(solution)/shard_map/ppermute | solution.py:144
  134.5 4.3 %collective-permute-done.6 = bf16[32,1024]{1,0:T(8,128)(2,1)S(1)} collective-permute-done((bf16[32,1024]{1,0:T(8,128)(2,1)S(1)}, bf16[32,1024]{1,0:T(8,128)(2,1)S(1)}, u32[]{:S(2)}, u32[]{:S(2)}) %collective-permute-start.6) | collective-permute-done | bytes 65568 | tf_op jit(solution)/shard_map/ppermute | solution.py:144
  139.0 4.3 %collective-permute-done.7 = bf16[32,1024]{1,0:T(8,128)(2,1)S(1)} collective-permute-done((bf16[32,1024]{1,0:T(8,128)(2,1)S(1)}, bf16[32,1024]{1,0:T(8,128)(2,1)S(1)}, u32[]{:S(2)}, u32[]{:S(2)}) %collective-permute-start.7) | collective-permute-done | bytes 65568 | tf_op jit(solution)/shard_map/ppermute | solution.py:144
  143.2 4.8 %collective-permute-start.8 = (bf16[32,1024]{1,0:T(8,128)(2,1)S(1)}, bf16[32,1024]{1,0:T(8,128)(2,1)S(1)}, u32[]{:S(2)}, u32[]{:S(2)}) collective-permute-start(bf16[32,1024]{1,0:T(8,128)(2,1)S(1)} %add.231), channel_id=1, source_target_pairs={{0,16},{2,18},{4,20},{6,22},{8,24},{10,26},{12,28},{14,30},{16,0},... | collective-permute-start | bytes 196616 | tf_op jit(solution)/shard_map/ppermute | solution.py:144
  148.0 2.2 %collective-permute-done.8 = bf16[32,1024]{1,0:T(8,128)(2,1)S(1)} collective-permute-done((bf16[32,1024]{1,0:T(8,128)(2,1)S(1)}, bf16[32,1024]{1,0:T(8,128)(2,1)S(1)}, u32[]{:S(2)}, u32[]{:S(2)}) %collective-permute-start.8) | collective-permute-done | bytes 65568 | tf_op jit(solution)/shard_map/ppermute | solution.py:144
  150.3 4.9 %all_gather.7 = bf16[32,2048]{1,0:T(8,128)(2,1)S(1)} all-gather(bf16[32,1024]{1,0:T(8,128)(2,1)S(1)} %add.232), channel_id=1, replica_groups=mesh['seq'=16,'mp'=2] {'mp'}, dimensions={1}, use_global_device_ids=true | all-gather | bytes 196608 | tf_op jit(solution)/shard_map/all_gather | solution.py:340
  158.1 1.9 %collective-permute-start.10 = (f32[32]{0:T(128)S(1)}, f32[32]{0:T(128)S(1)}, u32[]{:S(2)}, u32[]{:S(2)}) collective-permute-start(f32[32]{0:T(128)S(1)} %max.26), channel_id=1, source_target_pairs={{0,4},{2,6},{4,0},{6,2},{8,12},{10,14},{12,8},{14,10},{16,20},{18,... | collective-permute-start | bytes 392 | tf_op jit(solution)/shard_map/ppermute | solution.py:144
  160.0 1.6 collective-permute-done.10
  161.6 3.5 %collective-permute-done.11 = f32[32]{0:T(128)S(1)} collective-permute-done((f32[32]{0:T(128)S(1)}, f32[32]{0:T(128)S(1)}, u32[]{:S(2)}, u32[]{:S(2)}) %collective-permute-start.11) | collective-permute-done | bytes 160 | tf_op jit(solution)/shard_map/ppermute | solution.py:144
  165.2 2.9 %collective-permute-start.12 = (f32[32]{0:T(128)S(1)}, f32[32]{0:T(128)S(1)}, u32[]{:S(2)}, u32[]{:S(2)}) collective-permute-start(f32[32]{0:T(128)S(1)} %max.28), channel_id=1, source_target_pairs={{0,16},{2,18},{4,20},{6,22},{8,24},{10,26},{12,28},{14,30},{16,0},... | collective-permute-start | bytes 392 | tf_op jit(solution)/shard_map/ppermute | solution.py:144
  168.1 1.5 collective-permute-done.12
  (132 shorter events, 39.6 us)
Async XLA Ops:
  7.2 68.2 %all-gather.2.cloned.1.call-start = ((), (), s32[]{:S(2)}) async-start(), calls=%async_computation | async-start | bytes 4456448 | tf_op jit(solution)/shard_map/all_gather | solution.py:183
  15.8 25.1 %copy-start.7 = (bf16[256,256]{1,0:T(8,128)(2,1)}, bf16[256,256]{1,0:T(8,128)(2,1)S(1)}, u32[]{:S(2)}) copy-start(bf16[256,256]{1,0:T(8,128)(2,1)S(1)} %copy.36) | copy-start | bytes 393220
  18.5 29.8 %collective-permute-start = (bf16[4,256,64]{2,1,0:T(8,128)(2,1)}, bf16[4,256,64]{2,1,0:T(8,128)(2,1)}, u32[]{:S(2)}, u32[]{:S(2)}) collective-permute-start(bf16[4,256,64]{2,1,0:T(8,128)(2,1)} %bitcast.19), channel_id=1, source_target_pairs={{0,8},{2,10},{4,12},{6,14},{8,16},{10,18},{12,20},{14,22},{16,24},... | collective-permute-start | bytes 393224 | tf_op jit(solution)/shard_map/ppermute | solution.py:153
  24.1 25.1 %collective-permute-start.1 = (bf16[4,256,64]{2,1,0:T(8,128)(2,1)}, bf16[4,256,64]{2,1,0:T(8,128)(2,1)}, u32[]{:S(2)}, u32[]{:S(2)}) collective-permute-start(bf16[4,256,64]{2,1,0:T(8,128)(2,1)} %bitcast.19), channel_id=1, source_target_pairs={{0,6},{2,8},{4,10},{6,12},{8,14},{10,16},{12,18},{14,20},{16,22},{... | collective-permute-start | bytes 393224 | tf_op jit(solution)/shard_map/ppermute | solution.py:153
  27.4 22.8 %collective-permute-start.2 = (bf16[4,256,64]{2,1,0:T(8,128)(2,1)}, bf16[4,256,64]{2,1,0:T(8,128)(2,1)}, u32[]{:S(2)}, u32[]{:S(2)}) collective-permute-start(bf16[4,256,64]{2,1,0:T(8,128)(2,1)} %bitcast.19), channel_id=1, source_target_pairs={{0,4},{2,6},{4,8},{6,10},{8,12},{10,14},{12,16},{14,18},{16,20},{1... | collective-permute-start | bytes 393224 | tf_op jit(solution)/shard_map/ppermute | solution.py:153
  30.8 20.4 %collective-permute-start.3 = (bf16[4,256,64]{2,1,0:T(8,128)(2,1)}, bf16[4,256,64]{2,1,0:T(8,128)(2,1)}, u32[]{:S(2)}, u32[]{:S(2)}) collective-permute-start(bf16[4,256,64]{2,1,0:T(8,128)(2,1)} %bitcast.19), channel_id=1, source_target_pairs={{0,2},{2,4},{4,6},{6,8},{8,10},{10,12},{12,14},{14,16},{16,18},{18... | collective-permute-start | bytes 393224 | tf_op jit(solution)/shard_map/ppermute | solution.py:153
  36.8 4.0 %copy-start.11 = (f32[256,32]{0,1:T(8,128)S(1)}, f32[256,32]{0,1:T(8,128)}, u32[]{:S(2)}) copy-start(f32[256,32]{0,1:T(8,128)} %copy-done.10) | copy-start | bytes 98308
  36.8 4.1 %copy-start.13 = (f32[256,32]{0,1:T(8,128)S(1)}, f32[256,32]{0,1:T(8,128)}, u32[]{:S(2)}) copy-start(f32[256,32]{0,1:T(8,128)} %copy-done.12) | copy-start | bytes 98308
  106.0 7.4 %copy-start.3 = (bf16[256,2048]{1,0:T(8,128)(2,1)S(1)}, bf16[256,2048]{1,0:T(8,128)(2,1)}, u32[]{:S(2)}) copy-start(bf16[256,2048]{1,0:T(8,128)(2,1)} %param.9) | copy-start | bytes 3145732
  111.9 9.5 %collective-permute-start.4 = (bf16[256,1024]{1,0:T(8,128)(2,1)}, bf16[256,1024]{1,0:T(8,128)(2,1)}, u32[]{:S(2)}, u32[]{:S(2)}) collective-permute-start(bf16[256,1024]{1,0:T(8,128)(2,1)} %dynamic-slice_convert_fusion), channel_id=1, source_target_pairs={{0,1},{1,0},{2,3},{3,2},{4,5},{5,4},{6,7},{7,6},{8,9},{9,8},{10,11... | collective-permute-start | bytes 1572872 | tf_op jit(solution)/shard_map/ppermute | solution.py:325
  114.9 8.5 %copy-start.17 = (s32[32]{0:T(128)S(1)}, s32[32]{0:T(128)}, u32[]{:S(2)}) copy-start(s32[32]{0:T(128)} %get-tuple-element.18) | copy-start | bytes 388
  114.9 33.1 %copy-start.15 = (bf16[2048]{0:T(1024)(128)(2,1)S(1)}, bf16[2048]{0:T(1024)(128)(2,1)}, u32[]{:S(2)}) copy-start(bf16[2048]{0:T(1024)(128)(2,1)} %param.16) | copy-start | bytes 12292
  114.9 40.6 %copy-start.4 = (bf16[2048,1000]{0,1:T(8,128)(2,1)S(1)}, bf16[2048,1000]{0,1:T(8,128)(2,1)}, u32[]{:S(2)}) copy-start(bf16[2048,1000]{0,1:T(8,128)(2,1)} %param.17) | copy-start | bytes 12288004
  123.3 33.6 %copy-start.5 = (bf16[256,1024]{1,0:T(8,128)(2,1)}, bf16[256,1024]{1,0:T(8,128)(2,1)S(1)}, u32[]{:S(2)}) copy-start(bf16[256,1024]{1,0:T(8,128)(2,1)S(1)} %add_convert_fusion) | copy-start | bytes 1572868
  123.6 10.9 %collective-permute-start.5 = (bf16[32,1024]{1,0:T(8,128)(2,1)S(1)}, bf16[32,1024]{1,0:T(8,128)(2,1)S(1)}, u32[]{:S(2)}, u32[]{:S(2)}) collective-permute-start(bf16[32,1024]{1,0:T(8,128)(2,1)S(1)} %convolution_convert_fusion), channel_id=1, source_target_pairs={{0,2},{2,0},{4,6},{6,4},{8,10},{10,8},{12,14},{14,12},{16,18},{18,... | collective-permute-start | bytes 196616 | tf_op jit(solution)/shard_map/ppermute | solution.py:144
  134.4 4.4 %collective-permute-start.6 = (bf16[32,1024]{1,0:T(8,128)(2,1)S(1)}, bf16[32,1024]{1,0:T(8,128)(2,1)S(1)}, u32[]{:S(2)}, u32[]{:S(2)}) collective-permute-start(bf16[32,1024]{1,0:T(8,128)(2,1)S(1)} %add.229), channel_id=1, source_target_pairs={{0,4},{2,6},{4,0},{6,2},{8,12},{10,14},{12,8},{14,10},{16,20},{18,... | collective-permute-start | bytes 196616 | tf_op jit(solution)/shard_map/ppermute | solution.py:144
  138.9 4.3 %collective-permute-start.7 = (bf16[32,1024]{1,0:T(8,128)(2,1)S(1)}, bf16[32,1024]{1,0:T(8,128)(2,1)S(1)}, u32[]{:S(2)}, u32[]{:S(2)}) collective-permute-start(bf16[32,1024]{1,0:T(8,128)(2,1)S(1)} %add.230), channel_id=1, source_target_pairs={{0,8},{2,10},{4,12},{6,14},{8,0},{10,2},{12,4},{14,6},{16,24},{18,... | collective-permute-start | bytes 196616 | tf_op jit(solution)/shard_map/ppermute | solution.py:144
  143.2 7.0 %collective-permute-start.8 = (bf16[32,1024]{1,0:T(8,128)(2,1)S(1)}, bf16[32,1024]{1,0:T(8,128)(2,1)S(1)}, u32[]{:S(2)}, u32[]{:S(2)}) collective-permute-start(bf16[32,1024]{1,0:T(8,128)(2,1)S(1)} %add.231), channel_id=1, source_target_pairs={{0,16},{2,18},{4,20},{6,22},{8,24},{10,26},{12,28},{14,30},{16,0},... | collective-permute-start | bytes 196616 | tf_op jit(solution)/shard_map/ppermute | solution.py:144
  155.5 15.6 %copy-start.8 = (bf16[256,256]{1,0:T(8,128)(2,1)S(1)}, bf16[256,256]{1,0:T(8,128)(2,1)}, u32[]{:S(2)}) copy-start(bf16[256,256]{1,0:T(8,128)(2,1)} %copy-done.7) | copy-start | bytes 393220
  156.9 1.2 collective-permute-start.9
  158.1 3.5 %collective-permute-start.10 = (f32[32]{0:T(128)S(1)}, f32[32]{0:T(128)S(1)}, u32[]{:S(2)}, u32[]{:S(2)}) collective-permute-start(f32[32]{0:T(128)S(1)} %max.26), channel_id=1, source_target_pairs={{0,4},{2,6},{4,0},{6,2},{8,12},{10,14},{12,8},{14,10},{16,20},{18,... | collective-permute-start | bytes 392 | tf_op jit(solution)/shard_map/ppermute | solution.py:144
  161.6 3.5 %collective-permute-start.11 = (f32[32]{0:T(128)S(1)}, f32[32]{0:T(128)S(1)}, u32[]{:S(2)}, u32[]{:S(2)}) collective-permute-start(f32[32]{0:T(128)S(1)} %max.27), channel_id=1, source_target_pairs={{0,8},{2,10},{4,12},{6,14},{8,0},{10,2},{12,4},{14,6},{16,24},{18,... | collective-permute-start | bytes 392 | tf_op jit(solution)/shard_map/ppermute | solution.py:144
  165.2 4.4 %collective-permute-start.12 = (f32[32]{0:T(128)S(1)}, f32[32]{0:T(128)S(1)}, u32[]{:S(2)}, u32[]{:S(2)}) collective-permute-start(f32[32]{0:T(128)S(1)} %max.28), channel_id=1, source_target_pairs={{0,16},{2,18},{4,20},{6,22},{8,24},{10,26},{12,28},{14,30},{16,0},... | collective-permute-start | bytes 392 | tf_op jit(solution)/shard_map/ppermute | solution.py:144
  169.6 3.5 %collective-permute-start.13 = (f32[32]{0:T(128)S(1)}, f32[32]{0:T(128)S(1)}, u32[]{:S(2)}, u32[]{:S(2)}) collective-permute-start(f32[32]{0:T(128)S(1)} %max.29), channel_id=1, source_target_pairs={{0,1},{1,0},{2,3},{3,2},{4,5},{5,4},{6,7},{7,6},{8,9},{9,8},{10,11... | collective-permute-start | bytes 392 | tf_op jit(solution)/shard_map/ppermute | solution.py:144
  (10 other events, 15.0 us)
Sparse Core Ops, SparseCore 0:
  10.8 64.6 all-gather.1

commit v8 on v7

--- a/solution.py
+++ b/solution.py
@@ -17,7 +17,7 @@
 MOST = 1024
 PREFIX_CHUNK = 512
 SUFFIX_CHUNK = 256
-TILE_TOKENS = 128
+TILE_TOKENS = 32
 
 
 epsilon = 1e-05

time: 182 us -> 207 us (1.14)
  Pallas kernels: 37.5 us -> 53.6 us
  starting transfers between devices: 37.7 us -> 52.1 us
  waiting for transfers between devices: 39.1 us -> 35 us
    ppermute x9, starting transfers between devices: 21.2 us -> 35.6 us  [butterfly(): partner = lax.ppermute(block, axis, [(i, i ^ step) for i in range(count)])]
    pallas_call x1, Pallas kernels: 28.1 us -> 39.5 us  [per_device(): pl.pallas_call(functools.partial(prefix_kernel, kv_heads=kv_heads, prefix...]
    pallas_call x1, Pallas kernels: 9.39 us -> 14.1 us  [per_device(): pl.pallas_call(functools.partial(suffix_kernel, kv_heads=kv_heads, suffix...]
    all_gather x1, waiting for transfers between devices: 11.7 us -> 7.08 us  [per_device(): all_prefix = lax.all_gather(own_prefix, 'seq', axis=2, tiled=True)]
    ppermute x1, waiting for transfers between devices: 6.48 us -> 10.4 us  [per_device(): received = lax.ppermute(sent.astype(jnp.bfloat16), 'mp', [(0, 1), (1, 0)])]
    ppermute x9, waiting for transfers between devices: 20.9 us -> 17.5 us  [butterfly(): partner = lax.ppermute(block, axis, [(i, i ^ step) for i in range(count)])]
  transfers between devices with their start and end apart: 15 -> 15, of which waited for: 11 -> 11; matrix products, arithmetic and copies ran while one was open for 17% -> 15% of each run, Pallas kernels for 5% -> 7%
where the time goes in v8:
time: 207 us
  Pallas kernels  53.6 us (26%)
  starting transfers between devices  52.1 us (25%)
  waiting for transfers between devices  35 us (17%)
  local copies, waits for them, and re-layouts  27.2 us (13%)
  between operations  14.5 us (7%)
  matrix products  10.1 us (5%)
  other arithmetic  9.52 us (5%)
  blocking collectives  4.94 us (2%)
    pallas_call x1, Pallas kernels, per_device(): pl.pallas_call(functools.partial(prefix_kernel, kv_heads=kv_heads, prefix...  39.5 us
    ppermute x9, starting transfers between devices, butterfly(): partner = lax.ppermute(block, axis, [(i, i ^ step) for i in range(count)])  35.6 us
    ppermute x9, waiting for transfers between devices, butterfly(): partner = lax.ppermute(block, axis, [(i, i ^ step) for i in range(count)])  17.5 us
    ppermute x4, starting transfers between devices, shifted_back(): return lax.ppermute(block, axis, route)  15 us
    pallas_call x1, Pallas kernels, per_device(): pl.pallas_call(functools.partial(suffix_kernel, kv_heads=kv_heads, suffix...  14.1 us
    ppermute x1, waiting for transfers between devices, per_device(): received = lax.ppermute(sent.astype(jnp.bfloat16), 'mp', [(0, 1), (1, 0)])  10.4 us
    all_gather x1, waiting for transfers between devices, per_device(): all_prefix = lax.all_gather(own_prefix, 'seq', axis=2, tiled=True)  7.08 us
    unnamed x42, local copies, waits for them, and re-layouts  6.93 us
  transfers between devices with their start and end apart: 15, of which 11 were waited for; matrix products, arithmetic and copies ran while one was open for 15% of the time, Pallas kernels for 7%

profile of v8, /device:TPU:0, one launch (start us, length us, event | category | flops | bytes accessed | tf_op | source)
XLA Modules:
  0.0 207.0 jit_solution(17241898901058952626)
XLA Ops:
  18.5 5.6 %collective-permute-start = (bf16[4,256,64]{2,1,0:T(8,128)(2,1)}, bf16[4,256,64]{2,1,0:T(8,128)(2,1)}, u32[]{:S(2)}, u32[]{:S(2)}) collective-permute-start(bf16[4,256,64]{2,1,0:T(8,128)(2,1)} %bitcast.19), channel_id=1, source_target_pairs={{0,8},{2,10},{4,12},{6,14},{8,16},{10,18},{12,20},{14,22},{16,24},... | collective-permute-start | bytes 393224 | tf_op jit(solution)/shard_map/ppermute | solution.py:153
  24.1 3.3 %collective-permute-start.1 = (bf16[4,256,64]{2,1,0:T(8,128)(2,1)}, bf16[4,256,64]{2,1,0:T(8,128)(2,1)}, u32[]{:S(2)}, u32[]{:S(2)}) collective-permute-start(bf16[4,256,64]{2,1,0:T(8,128)(2,1)} %bitcast.19), channel_id=1, source_target_pairs={{0,6},{2,8},{4,10},{6,12},{8,14},{10,16},{12,18},{14,20},{16,22},{... | collective-permute-start | bytes 393224 | tf_op jit(solution)/shard_map/ppermute | solution.py:153
  27.4 3.4 %collective-permute-start.2 = (bf16[4,256,64]{2,1,0:T(8,128)(2,1)}, bf16[4,256,64]{2,1,0:T(8,128)(2,1)}, u32[]{:S(2)}, u32[]{:S(2)}) collective-permute-start(bf16[4,256,64]{2,1,0:T(8,128)(2,1)} %bitcast.19), channel_id=1, source_target_pairs={{0,4},{2,6},{4,8},{6,10},{8,12},{10,14},{12,16},{14,18},{16,20},{1... | collective-permute-start | bytes 393224 | tf_op jit(solution)/shard_map/ppermute | solution.py:153
  30.8 2.6 %collective-permute-start.3 = (bf16[4,256,64]{2,1,0:T(8,128)(2,1)}, bf16[4,256,64]{2,1,0:T(8,128)(2,1)}, u32[]{:S(2)}, u32[]{:S(2)}) collective-permute-start(bf16[4,256,64]{2,1,0:T(8,128)(2,1)} %bitcast.19), channel_id=1, source_target_pairs={{0,2},{2,4},{4,6},{6,8},{8,10},{10,12},{12,14},{14,16},{16,18},{18... | collective-permute-start | bytes 393224 | tf_op jit(solution)/shard_map/ppermute | solution.py:153
  36.9 4.0 %fusion.1 = f32[256,1024]{0,1:T(8,128)S(1)} fusion(bf16[2048,1024]{1,0:T(8,128)(2,1)} %param.13, f32[2048]{0:T(1024)} %copy-done.14, f32[256]{0:T(256)} %copy-done.18, bf16[256,2048]{1,0:T(8,128)(2,1)S(1)} %copy-done.2), kind=kOutput, calls=%fused_computation.17 | convolution fusion | flops 1075838976 | bytes 6300672 | tf_op jit(solution)/shard_map/dot_general | solution.py:216
  54.3 14.1 %shard_map.120 = (f32[2,2048,1]{2,1,0:T(8,128)}, f32[2,2048,1]{2,1,0:T(8,128)}, f32[2,2048,64]{2,1,0:T(8,128)}) custom-call(s32[32]{0:T(128)} %reshape.323.table, bf16[2,2048,64]{2,1,0:T(8,128)(2,1)} %bitcast.59, s32[2048,1]{1,0:T(8,128)} %broadcast_in_dim_reshape.13.rr_ref, s32[2048,1]{1,0:T(8,128)} %broadcast_in_dim_reshape.14.rp_ref, ...), custom_call_target="tpu_custom_call" | custom-call | tf_op jit(solution)/shard_map/pallas_call | solution.py:278
  68.4 7.1 %all-gather.2.cloned.1.call-done = bf16[4,4,2048,64]{2,3,0,1:T(8,128)(2,1)} async-done(((bf16[4,4,128,64]{2,3,0,1:T(8,128)(2,1)}), bf16[4,4,2048,64]{2,3,0,1:T(8,128)(2,1)}) %all-gather.2.cloned.1.call-update) | async-done | bytes 4194320 | tf_op jit(solution)/shard_map/all_gather | solution.py:183
  75.5 39.5 %shard_map.121 = bf16[2,2048,64]{2,1,0:T(8,128)(2,1)} custom-call(s32[32]{0:T(128)} %reshape.323.table, bf16[2,2048,64]{2,1,0:T(8,128)(2,1)} %bitcast.60, s32[2048,1]{1,0:T(8,128)} %broadcast_in_dim_reshape.12.rg_ref, bf16[4,4,64,2048]{3,2,1,0:T(8,128)(2,1)} %bitcast.57, bf16[4,4,64,2048]{3,2,1,0:T(8,128)(2,1)} %bitcast.58, ...), custom_call_target="tpu_custom_call" | custom-call | tf_op jit(solution)/shard_map/pallas_call | solution.py:296
  115.0 2.5 %copy.42 = bf16[2,256,8,64]{1,3,2,0:T(8,128)(2,1)} copy(bf16[2,256,8,64]{3,2,1,0:T(8,128)(2,1)} %bitcast.61) | data formatting | bytes 1048576 | tf_op jit(solution)/shard_map/reshape | solution.py:317
  117.5 3.7 %fusion.10 = f32[256,2048]{1,0:T(8,128)S(1)} fusion(bf16[256,1024]{0,1:T(8,128)(2,1)} %bitcast.66, bf16[1024,2048]{1,0:T(8,128)(2,1)} %param.15), kind=kOutput, calls=%fused_computation.82 | convolution fusion | flops 1073741824 | bytes 6815744 | tf_op jit(solution)/shard_map/dot_general | solution.py:319
  126.4 10.4 %collective-permute-done.4 = bf16[256,1024]{1,0:T(8,128)(2,1)} collective-permute-done((bf16[256,1024]{1,0:T(8,128)(2,1)}, bf16[256,1024]{1,0:T(8,128)(2,1)}, u32[]{:S(2)}, u32[]{:S(2)}) %collective-permute-start.4) | collective-permute-done | bytes 524320 | tf_op jit(solution)/shard_map/ppermute | solution.py:325
  136.9 1.9 add_convert_fusion
  141.5 4.7 %collective-permute-start.6 = (bf16[32,1024]{1,0:T(8,128)(2,1)S(1)}, bf16[32,1024]{1,0:T(8,128)(2,1)S(1)}, u32[]{:S(2)}, u32[]{:S(2)}) collective-permute-start(bf16[32,1024]{1,0:T(8,128)(2,1)S(1)} %add.229), channel_id=1, source_target_pairs={{0,4},{2,6},{4,0},{6,2},{8,12},{10,14},{12,8},{14,10},{16,20},{18,... | collective-permute-start | bytes 196616 | tf_op jit(solution)/shard_map/ppermute | solution.py:144
  146.2 2.4 %collective-permute-done.6 = bf16[32,1024]{1,0:T(8,128)(2,1)S(1)} collective-permute-done((bf16[32,1024]{1,0:T(8,128)(2,1)S(1)}, bf16[32,1024]{1,0:T(8,128)(2,1)S(1)}, u32[]{:S(2)}, u32[]{:S(2)}) %collective-permute-start.6) | collective-permute-done | bytes 65568 | tf_op jit(solution)/shard_map/ppermute | solution.py:144
  148.6 20.5 %collective-permute-start.7 = (bf16[32,1024]{1,0:T(8,128)(2,1)S(1)}, bf16[32,1024]{1,0:T(8,128)(2,1)S(1)}, u32[]{:S(2)}, u32[]{:S(2)}) collective-permute-start(bf16[32,1024]{1,0:T(8,128)(2,1)S(1)} %add.230), channel_id=1, source_target_pairs={{0,8},{2,10},{4,12},{6,14},{8,0},{10,2},{12,4},{14,6},{16,24},{18,... | collective-permute-start | bytes 196616 | tf_op jit(solution)/shard_map/ppermute | solution.py:144
  169.2 2.2 %collective-permute-done.7 = bf16[32,1024]{1,0:T(8,128)(2,1)S(1)} collective-permute-done((bf16[32,1024]{1,0:T(8,128)(2,1)S(1)}, bf16[32,1024]{1,0:T(8,128)(2,1)S(1)}, u32[]{:S(2)}, u32[]{:S(2)}) %collective-permute-start.7) | collective-permute-done | bytes 65568 | tf_op jit(solution)/shard_map/ppermute | solution.py:144
  171.4 1.8 collective-permute-start.8
  173.3 3.4 %collective-permute-done.8 = bf16[32,1024]{1,0:T(8,128)(2,1)S(1)} collective-permute-done((bf16[32,1024]{1,0:T(8,128)(2,1)S(1)}, bf16[32,1024]{1,0:T(8,128)(2,1)S(1)}, u32[]{:S(2)}, u32[]{:S(2)}) %collective-permute-start.8) | collective-permute-done | bytes 65568 | tf_op jit(solution)/shard_map/ppermute | solution.py:144
  176.7 4.9 %all_gather.7 = bf16[32,2048]{1,0:T(8,128)(2,1)S(1)} all-gather(bf16[32,1024]{1,0:T(8,128)(2,1)S(1)} %add.232), channel_id=1, replica_groups=mesh['seq'=16,'mp'=2] {'mp'}, dimensions={1}, use_global_device_ids=true | all-gather | bytes 196608 | tf_op jit(solution)/shard_map/all_gather | solution.py:340
  184.5 1.7 collective-permute-start.10
  186.3 1.8 collective-permute-done.10
  188.1 2.1 %collective-permute-start.11 = (f32[32]{0:T(128)S(1)}, f32[32]{0:T(128)S(1)}, u32[]{:S(2)}, u32[]{:S(2)}) collective-permute-start(f32[32]{0:T(128)S(1)} %max.27), channel_id=1, source_target_pairs={{0,8},{2,10},{4,12},{6,14},{8,0},{10,2},{12,4},{14,6},{16,24},{18,... | collective-permute-start | bytes 392 | tf_op jit(solution)/shard_map/ppermute | solution.py:144
  191.7 1.7 collective-permute-start.12
  193.4 2.8 %collective-permute-done.12 = f32[32]{0:T(128)S(1)} collective-permute-done((f32[32]{0:T(128)S(1)}, f32[32]{0:T(128)S(1)}, u32[]{:S(2)}, u32[]{:S(2)}) %collective-permute-start.12) | collective-permute-done | bytes 160 | tf_op jit(solution)/shard_map/ppermute | solution.py:144
  (132 shorter events, 44.1 us)
Async XLA Ops:
  7.2 68.3 %all-gather.2.cloned.1.call-start = ((), (), s32[]{:S(2)}) async-start(), calls=%async_computation | async-start | bytes 4456448 | tf_op jit(solution)/shard_map/all_gather | solution.py:183
  15.8 25.1 %copy-start.7 = (bf16[256,256]{1,0:T(8,128)(2,1)}, bf16[256,256]{1,0:T(8,128)(2,1)S(1)}, u32[]{:S(2)}) copy-start(bf16[256,256]{1,0:T(8,128)(2,1)S(1)} %copy.36) | copy-start | bytes 393220
  18.5 29.8 %collective-permute-start = (bf16[4,256,64]{2,1,0:T(8,128)(2,1)}, bf16[4,256,64]{2,1,0:T(8,128)(2,1)}, u32[]{:S(2)}, u32[]{:S(2)}) collective-permute-start(bf16[4,256,64]{2,1,0:T(8,128)(2,1)} %bitcast.19), channel_id=1, source_target_pairs={{0,8},{2,10},{4,12},{6,14},{8,16},{10,18},{12,20},{14,22},{16,24},... | collective-permute-start | bytes 393224 | tf_op jit(solution)/shard_map/ppermute | solution.py:153
  24.1 25.2 %collective-permute-start.1 = (bf16[4,256,64]{2,1,0:T(8,128)(2,1)}, bf16[4,256,64]{2,1,0:T(8,128)(2,1)}, u32[]{:S(2)}, u32[]{:S(2)}) collective-permute-start(bf16[4,256,64]{2,1,0:T(8,128)(2,1)} %bitcast.19), channel_id=1, source_target_pairs={{0,6},{2,8},{4,10},{6,12},{8,14},{10,16},{12,18},{14,20},{16,22},{... | collective-permute-start | bytes 393224 | tf_op jit(solution)/shard_map/ppermute | solution.py:153
  27.4 22.9 %collective-permute-start.2 = (bf16[4,256,64]{2,1,0:T(8,128)(2,1)}, bf16[4,256,64]{2,1,0:T(8,128)(2,1)}, u32[]{:S(2)}, u32[]{:S(2)}) collective-permute-start(bf16[4,256,64]{2,1,0:T(8,128)(2,1)} %bitcast.19), channel_id=1, source_target_pairs={{0,4},{2,6},{4,8},{6,10},{8,12},{10,14},{12,16},{14,18},{16,20},{1... | collective-permute-start | bytes 393224 | tf_op jit(solution)/shard_map/ppermute | solution.py:153
  30.8 20.4 %collective-permute-start.3 = (bf16[4,256,64]{2,1,0:T(8,128)(2,1)}, bf16[4,256,64]{2,1,0:T(8,128)(2,1)}, u32[]{:S(2)}, u32[]{:S(2)}) collective-permute-start(bf16[4,256,64]{2,1,0:T(8,128)(2,1)} %bitcast.19), channel_id=1, source_target_pairs={{0,2},{2,4},{4,6},{6,8},{8,10},{10,12},{12,14},{14,16},{16,18},{18... | collective-permute-start | bytes 393224 | tf_op jit(solution)/shard_map/ppermute | solution.py:153
  36.9 4.0 %copy-start.11 = (f32[256,32]{0,1:T(8,128)S(1)}, f32[256,32]{0,1:T(8,128)}, u32[]{:S(2)}) copy-start(f32[256,32]{0,1:T(8,128)} %copy-done.10) | copy-start | bytes 98308
  36.9 4.1 %copy-start.13 = (f32[256,32]{0,1:T(8,128)S(1)}, f32[256,32]{0,1:T(8,128)}, u32[]{:S(2)}) copy-start(f32[256,32]{0,1:T(8,128)} %copy-done.12) | copy-start | bytes 98308
  117.5 7.4 %copy-start.3 = (bf16[256,2048]{1,0:T(8,128)(2,1)S(1)}, bf16[256,2048]{1,0:T(8,128)(2,1)}, u32[]{:S(2)}) copy-start(bf16[256,2048]{1,0:T(8,128)(2,1)} %param.9) | copy-start | bytes 3145732
  123.4 13.5 %collective-permute-start.4 = (bf16[256,1024]{1,0:T(8,128)(2,1)}, bf16[256,1024]{1,0:T(8,128)(2,1)}, u32[]{:S(2)}, u32[]{:S(2)}) collective-permute-start(bf16[256,1024]{1,0:T(8,128)(2,1)} %dynamic-slice_convert_fusion), channel_id=1, source_target_pairs={{0,1},{1,0},{2,3},{3,2},{4,5},{5,4},{6,7},{7,6},{8,9},{9,8},{10,11... | collective-permute-start | bytes 1572872 | tf_op jit(solution)/shard_map/ppermute | solution.py:325
  126.4 12.4 %copy-start.17 = (s32[32]{0:T(128)S(1)}, s32[32]{0:T(128)}, u32[]{:S(2)}) copy-start(s32[32]{0:T(128)} %get-tuple-element.18) | copy-start | bytes 388
  126.4 46.8 %copy-start.15 = (bf16[2048]{0:T(1024)(128)(2,1)S(1)}, bf16[2048]{0:T(1024)(128)(2,1)}, u32[]{:S(2)}) copy-start(bf16[2048]{0:T(1024)(128)(2,1)} %param.16) | copy-start | bytes 12292
  126.4 55.4 %copy-start.4 = (bf16[2048,1000]{0,1:T(8,128)(2,1)S(1)}, bf16[2048,1000]{0,1:T(8,128)(2,1)}, u32[]{:S(2)}) copy-start(bf16[2048,1000]{0,1:T(8,128)(2,1)} %param.17) | copy-start | bytes 12288004
  138.8 44.5 %copy-start.5 = (bf16[256,1024]{1,0:T(8,128)(2,1)}, bf16[256,1024]{1,0:T(8,128)(2,1)S(1)}, u32[]{:S(2)}) copy-start(bf16[256,1024]{1,0:T(8,128)(2,1)S(1)} %add_convert_fusion) | copy-start | bytes 1572868
  139.1 2.4 %collective-permute-start.5 = (bf16[32,1024]{1,0:T(8,128)(2,1)S(1)}, bf16[32,1024]{1,0:T(8,128)(2,1)S(1)}, u32[]{:S(2)}, u32[]{:S(2)}) collective-permute-start(bf16[32,1024]{1,0:T(8,128)(2,1)S(1)} %convolution_convert_fusion), channel_id=1, source_target_pairs={{0,2},{2,0},{4,6},{6,4},{8,10},{10,8},{12,14},{14,12},{16,18},{18,... | collective-permute-start | bytes 196616 | tf_op jit(solution)/shard_map/ppermute | solution.py:144
  141.5 7.1 %collective-permute-start.6 = (bf16[32,1024]{1,0:T(8,128)(2,1)S(1)}, bf16[32,1024]{1,0:T(8,128)(2,1)S(1)}, u32[]{:S(2)}, u32[]{:S(2)}) collective-permute-start(bf16[32,1024]{1,0:T(8,128)(2,1)S(1)} %add.229), channel_id=1, source_target_pairs={{0,4},{2,6},{4,0},{6,2},{8,12},{10,14},{12,8},{14,10},{16,20},{18,... | collective-permute-start | bytes 196616 | tf_op jit(solution)/shard_map/ppermute | solution.py:144
  148.6 22.8 %collective-permute-start.7 = (bf16[32,1024]{1,0:T(8,128)(2,1)S(1)}, bf16[32,1024]{1,0:T(8,128)(2,1)S(1)}, u32[]{:S(2)}, u32[]{:S(2)}) collective-permute-start(bf16[32,1024]{1,0:T(8,128)(2,1)S(1)} %add.230), channel_id=1, source_target_pairs={{0,8},{2,10},{4,12},{6,14},{8,0},{10,2},{12,4},{14,6},{16,24},{18,... | collective-permute-start | bytes 196616 | tf_op jit(solution)/shard_map/ppermute | solution.py:144
  171.4 5.2 %collective-permute-start.8 = (bf16[32,1024]{1,0:T(8,128)(2,1)S(1)}, bf16[32,1024]{1,0:T(8,128)(2,1)S(1)}, u32[]{:S(2)}, u32[]{:S(2)}) collective-permute-start(bf16[32,1024]{1,0:T(8,128)(2,1)S(1)} %add.231), channel_id=1, source_target_pairs={{0,16},{2,18},{4,20},{6,22},{8,24},{10,26},{12,28},{14,30},{16,0},... | collective-permute-start | bytes 196616 | tf_op jit(solution)/shard_map/ppermute | solution.py:144
  181.9 15.7 %copy-start.8 = (bf16[256,256]{1,0:T(8,128)(2,1)S(1)}, bf16[256,256]{1,0:T(8,128)(2,1)}, u32[]{:S(2)}) copy-start(bf16[256,256]{1,0:T(8,128)(2,1)} %copy-done.7) | copy-start | bytes 393220
  183.3 1.2 collective-permute-start.9
  184.5 3.5 %collective-permute-start.10 = (f32[32]{0:T(128)S(1)}, f32[32]{0:T(128)S(1)}, u32[]{:S(2)}, u32[]{:S(2)}) collective-permute-start(f32[32]{0:T(128)S(1)} %max.26), channel_id=1, source_target_pairs={{0,4},{2,6},{4,0},{6,2},{8,12},{10,14},{12,8},{14,10},{16,20},{18,... | collective-permute-start | bytes 392 | tf_op jit(solution)/shard_map/ppermute | solution.py:144
  188.1 3.6 %collective-permute-start.11 = (f32[32]{0:T(128)S(1)}, f32[32]{0:T(128)S(1)}, u32[]{:S(2)}, u32[]{:S(2)}) collective-permute-start(f32[32]{0:T(128)S(1)} %max.27), channel_id=1, source_target_pairs={{0,8},{2,10},{4,12},{6,14},{8,0},{10,2},{12,4},{14,6},{16,24},{18,... | collective-permute-start | bytes 392 | tf_op jit(solution)/shard_map/ppermute | solution.py:144
  191.7 4.4 %collective-permute-start.12 = (f32[32]{0:T(128)S(1)}, f32[32]{0:T(128)S(1)}, u32[]{:S(2)}, u32[]{:S(2)}) collective-permute-start(f32[32]{0:T(128)S(1)} %max.28), channel_id=1, source_target_pairs={{0,16},{2,18},{4,20},{6,22},{8,24},{10,26},{12,28},{14,30},{16,0},... | collective-permute-start | bytes 392 | tf_op jit(solution)/shard_map/ppermute | solution.py:144
  196.1 3.5 %collective-permute-start.13 = (f32[32]{0:T(128)S(1)}, f32[32]{0:T(128)S(1)}, u32[]{:S(2)}, u32[]{:S(2)}) collective-permute-start(f32[32]{0:T(128)S(1)} %max.29), channel_id=1, source_target_pairs={{0,1},{1,0},{2,3},{3,2},{4,5},{5,4},{6,7},{7,6},{8,9},{9,8},{10,11... | collective-permute-start | bytes 392 | tf_op jit(solution)/shard_map/ppermute | solution.py:144
  (10 other events, 15.0 us)
Sparse Core Ops, SparseCore 0:
  10.8 64.7 all-gather.1

commit v9 on v7

--- a/solution.py
+++ b/solution.py
@@ -333,7 +333,18 @@
     onehot = (local_last[:, None] == jnp.arange(token_rows, dtype=jnp.int32)[None, :]).astype(
         jnp.bfloat16
     )
-    last_part = jnp.dot(onehot, hidden, preferred_element_type=jnp.float32).astype(jnp.bfloat16)
+    context_last = jnp.dot(onehot, context, preferred_element_type=jnp.float32)
+    mixture_last = jnp.dot(
+        context_last.astype(jnp.bfloat16), w_out, preferred_element_type=jnp.float32
+    )
+    columns_last = jnp.dot(onehot, own_columns.astype(jnp.bfloat16), preferred_element_type=jnp.float32)
+    if mp_devices == 2:
+        kept = lax.dynamic_slice_in_dim(mixture_last, mp_index * part_width, part_width, 1)
+        sent = lax.dynamic_slice_in_dim(mixture_last, (1 - mp_index) * part_width, part_width, 1)
+        received = lax.ppermute(sent.astype(jnp.bfloat16), "mp", [(0, 1), (1, 0)])
+        last_part = (columns_last + (kept + received.astype(jnp.float32))).astype(jnp.bfloat16)
+    else:
+        last_part = jnp.dot(onehot, hidden, preferred_element_type=jnp.float32).astype(jnp.bfloat16)
     summed = butterfly(last_part, "seq", jnp.add)
     if summed is None:
         summed = lax.psum(last_part, "seq")

time: 182 us -> 181 us (level)
  waiting for transfers between devices: 39.1 us -> 31.1 us
  blocking collectives: 4.94 us -> 9.83 us
  matrix products: 10.1 us -> 14.9 us
    ppermute x1 -> x2, waiting for transfers between devices: 6.48 us -> 1.55 us  [per_device(): received = lax.ppermute(sent.astype(jnp.bfloat16), 'mp', [(0, 1), (1, 0)])]
    all_gather x1, blocking collectives: 4.94 us -> 9.83 us  [per_device(): lax.all_gather(summed, 'mp', axis=1, tiled=True).astype(jnp.float32)]
    dot_general x1 -> x2, matrix products: 0.22 us -> 4.87 us  [the longest x1 3.42 us: per_device(): jnp.dot(context_last.astype(jnp.bfloat16), w_out, preferred_element_type=...]
    ppermute x9, waiting for transfers between devices: 20.9 us -> 17.8 us  [butterfly(): partner = lax.ppermute(block, axis, [(i, i ^ step) for i in range(count)])]
    ppermute x9, starting transfers between devices: 21.2 us -> 18.4 us  [butterfly(): partner = lax.ppermute(block, axis, [(i, i ^ step) for i in range(count)])]
    unnamed x42 -> x40, local copies, waits for them, and re-layouts: 6.93 us -> 5.61 us
  transfers between devices with their start and end apart: 15 -> 16, of which waited for: 11 -> 10; matrix products, arithmetic and copies ran while one was open for 17% -> 20% of each run, Pallas kernels for 5% -> 5%
where the time goes in v9:
time: 181 us; the launch traced here: 179 us
  Pallas kernels  37.6 us (21%)
  starting transfers between devices  36.5 us (20%)
  waiting for transfers between devices  31.1 us (17%)
  local copies, waits for them, and re-layouts  25.7 us (14%)
  matrix products  14.9 us (8%)
  between operations  14.5 us (8%)
  blocking collectives  9.83 us (5%)
  other arithmetic  8.65 us (5%)
    pallas_call x1, Pallas kernels, per_device(): pl.pallas_call(functools.partial(prefix_kernel, kv_heads=kv_heads, prefix...  28.2 us
    ppermute x9, starting transfers between devices, butterfly(): partner = lax.ppermute(block, axis, [(i, i ^ step) for i in range(count)])  18.4 us
    ppermute x9, waiting for transfers between devices, butterfly(): partner = lax.ppermute(block, axis, [(i, i ^ step) for i in range(count)])  17.8 us
    ppermute x4, starting transfers between devices, shifted_back(): return lax.ppermute(block, axis, route)  15 us
    all_gather x1, waiting for transfers between devices, per_device(): all_prefix = lax.all_gather(own_prefix, 'seq', axis=2, tiled=True)  11.7 us
    all_gather x1, blocking collectives, per_device(): lax.all_gather(summed, 'mp', axis=1, tiled=True).astype(jnp.float32)  9.83 us
    pallas_call x1, Pallas kernels, per_device(): pl.pallas_call(functools.partial(suffix_kernel, kv_heads=kv_heads, suffix...  9.39 us
    unnamed x40, local copies, waits for them, and re-layouts  5.61 us
  transfers between devices with their start and end apart: 16, of which 10 were waited for; matrix products, arithmetic and copies ran while one was open for 20% of the time, Pallas kernels for 5%

profile of v9, /device:TPU:0, one launch (start us, length us, event | category | flops | bytes accessed | tf_op | source)
XLA Modules:
  0.0 178.7 jit_solution(3134393816278631542)
XLA Ops:
  18.5 5.6 %collective-permute-start = (bf16[4,256,64]{2,1,0:T(8,128)(2,1)}, bf16[4,256,64]{2,1,0:T(8,128)(2,1)}, u32[]{:S(2)}, u32[]{:S(2)}) collective-permute-start(bf16[4,256,64]{2,1,0:T(8,128)(2,1)} %bitcast.19), channel_id=1, source_target_pairs={{0,8},{2,10},{4,12},{6,14},{8,16},{10,18},{12,20},{14,22},{16,24},... | collective-permute-start | bytes 393224 | tf_op jit(solution)/shard_map/ppermute | solution.py:153
  24.1 3.3 %collective-permute-start.1 = (bf16[4,256,64]{2,1,0:T(8,128)(2,1)}, bf16[4,256,64]{2,1,0:T(8,128)(2,1)}, u32[]{:S(2)}, u32[]{:S(2)}) collective-permute-start(bf16[4,256,64]{2,1,0:T(8,128)(2,1)} %bitcast.19), channel_id=1, source_target_pairs={{0,6},{2,8},{4,10},{6,12},{8,14},{10,16},{12,18},{14,20},{16,22},{... | collective-permute-start | bytes 393224 | tf_op jit(solution)/shard_map/ppermute | solution.py:153
  27.4 3.4 %collective-permute-start.2 = (bf16[4,256,64]{2,1,0:T(8,128)(2,1)}, bf16[4,256,64]{2,1,0:T(8,128)(2,1)}, u32[]{:S(2)}, u32[]{:S(2)}) collective-permute-start(bf16[4,256,64]{2,1,0:T(8,128)(2,1)} %bitcast.19), channel_id=1, source_target_pairs={{0,4},{2,6},{4,8},{6,10},{8,12},{10,14},{12,16},{14,18},{16,20},{1... | collective-permute-start | bytes 393224 | tf_op jit(solution)/shard_map/ppermute | solution.py:153
  30.8 2.6 %collective-permute-start.3 = (bf16[4,256,64]{2,1,0:T(8,128)(2,1)}, bf16[4,256,64]{2,1,0:T(8,128)(2,1)}, u32[]{:S(2)}, u32[]{:S(2)}) collective-permute-start(bf16[4,256,64]{2,1,0:T(8,128)(2,1)} %bitcast.19), channel_id=1, source_target_pairs={{0,2},{2,4},{4,6},{6,8},{8,10},{10,12},{12,14},{14,16},{16,18},{18... | collective-permute-start | bytes 393224 | tf_op jit(solution)/shard_map/ppermute | solution.py:153
  36.9 4.1 %fusion.3 = f32[256,1024]{0,1:T(8,128)S(1)} fusion(bf16[2048,1024]{1,0:T(8,128)(2,1)} %param.13, f32[2048]{0:T(1024)} %copy-done.13, f32[256]{0:T(256)} %copy-done.17, bf16[256,2048]{1,0:T(8,128)(2,1)S(1)} %copy-done.3), kind=kOutput, calls=%fused_computation.20 | convolution fusion | flops 1075838976 | bytes 6300672 | tf_op jit(solution)/shard_map/dot_general | solution.py:216
  41.8 1.5 copy.33
  54.3 9.4 %shard_map.120 = (f32[2,2048,1]{2,1,0:T(8,128)}, f32[2,2048,1]{2,1,0:T(8,128)}, f32[2,2048,64]{2,1,0:T(8,128)}) custom-call(s32[8]{0:T(128)} %reshape.323.table, bf16[2,2048,64]{2,1,0:T(8,128)(2,1)} %bitcast.60, s32[2048,1]{1,0:T(8,128)} %broadcast_in_dim_reshape.13.rr_ref, s32[2048,1]{1,0:T(8,128)} %broadcast_in_dim_reshape.14.rp_ref, ...), custom_call_target="tpu_custom_call" | custom-call | tf_op jit(solution)/shard_map/pallas_call | solution.py:278
  63.7 11.7 %all-gather.2.cloned.1.call-done = bf16[4,4,2048,64]{2,3,0,1:T(8,128)(2,1)} async-done(((bf16[4,4,128,64]{2,3,0,1:T(8,128)(2,1)}), bf16[4,4,2048,64]{2,3,0,1:T(8,128)(2,1)}) %all-gather.2.cloned.1.call-update) | async-done | bytes 4194320 | tf_op jit(solution)/shard_map/all_gather | solution.py:183
  75.4 28.2 %shard_map.121 = bf16[2,2048,64]{2,1,0:T(8,128)(2,1)} custom-call(s32[8]{0:T(128)} %reshape.323.table, bf16[2,2048,64]{2,1,0:T(8,128)(2,1)} %bitcast.61, s32[2048,1]{1,0:T(8,128)} %broadcast_in_dim_reshape.12.rg_ref, bf16[4,4,64,2048]{3,2,1,0:T(8,128)(2,1)} %bitcast.58, bf16[4,4,64,2048]{3,2,1,0:T(8,128)(2,1)} %bitcast.59, ...), custom_call_target="tpu_custom_call" | custom-call | tf_op jit(solution)/shard_map/pallas_call | solution.py:296
  103.6 2.5 %copy.42 = bf16[2,256,8,64]{1,3,2,0:T(8,128)(2,1)} copy(bf16[2,256,8,64]{3,2,1,0:T(8,128)(2,1)} %bitcast.62) | data formatting | bytes 1048576 | tf_op jit(solution)/shard_map/reshape | solution.py:317
  106.1 3.4 %fusion = f32[32,2048]{1,0:T(8,128)S(1)} fusion(bf16[1024,2048]{1,0:T(8,128)(2,1)} %param.15, bf16[256,1024]{0,1:T(8,128)(2,1)} %bitcast.63, s32[32]{0:T(128)S(1)} %copy-done.14), kind=kOutput, calls=%fused_computation.9 | convolution fusion | flops 151035904 | bytes 4980864 | tf_op jit(solution)/shard_map/dot_general | solution.py:337
  111.6 1.6 convert_element_type.67
  113.2 1.5 collective-permute-done.5
  116.2 10.0 %collective-permute-start.6 = (bf16[32,1024]{1,0:T(8,128)(2,1)S(1)}, bf16[32,1024]{1,0:T(8,128)(2,1)S(1)}, u32[]{:S(2)}, u32[]{:S(2)}) collective-permute-start(bf16[32,1024]{1,0:T(8,128)(2,1)S(1)} %add_convert_fusion.2), channel_id=1, source_target_pairs={{0,2},{2,0},{4,6},{6,4},{8,10},{10,8},{12,14},{14,12},{16,18},{18,... | collective-permute-start | bytes 196616 | tf_op jit(solution)/shard_map/ppermute | solution.py:144
  127.2 4.3 %collective-permute-done.7 = bf16[32,1024]{1,0:T(8,128)(2,1)S(1)} collective-permute-done((bf16[32,1024]{1,0:T(8,128)(2,1)S(1)}, bf16[32,1024]{1,0:T(8,128)(2,1)S(1)}, u32[]{:S(2)}, u32[]{:S(2)}) %collective-permute-start.7) | collective-permute-done | bytes 65568 | tf_op jit(solution)/shard_map/ppermute | solution.py:144
  132.7 3.8 %fusion.15 = f32[256,2048]{1,0:T(8,128)S(1)} fusion(bf16[256,1024]{0,1:T(8,128)(2,1)} %bitcast.64, bf16[1024,2048]{1,0:T(8,128)(2,1)} %param.15), kind=kOutput, calls=%fused_computation.89 | convolution fusion | flops 1073741824 | bytes 6815744 | tf_op jit(solution)/shard_map/dot_general | solution.py:319
  136.5 2.1 %collective-permute-start.9 = (bf16[32,1024]{1,0:T(8,128)(2,1)S(1)}, bf16[32,1024]{1,0:T(8,128)(2,1)S(1)}, u32[]{:S(2)}, u32[]{:S(2)}) collective-permute-start(bf16[32,1024]{1,0:T(8,128)(2,1)S(1)} %add.241), channel_id=1, source_target_pairs={{0,16},{2,18},{4,20},{6,22},{8,24},{10,26},{12,28},{14,30},{16,0},... | collective-permute-start | bytes 196616 | tf_op jit(solution)/shard_map/ppermute | solution.py:144
  138.7 1.5 collective-permute-start.4
  140.3 2.2 %collective-permute-done.9 = bf16[32,1024]{1,0:T(8,128)(2,1)S(1)} collective-permute-done((bf16[32,1024]{1,0:T(8,128)(2,1)S(1)}, bf16[32,1024]{1,0:T(8,128)(2,1)S(1)}, u32[]{:S(2)}, u32[]{:S(2)}) %collective-permute-start.9) | collective-permute-done | bytes 65568 | tf_op jit(solution)/shard_map/ppermute | solution.py:144
  142.5 9.8 %all_gather.7 = bf16[32,2048]{1,0:T(8,128)(2,1)S(1)} all-gather(bf16[32,1024]{1,0:T(8,128)(2,1)S(1)} %add.242), channel_id=1, replica_groups=mesh['seq'=16,'mp'=2] {'mp'}, dimensions={1}, use_global_device_ids=true | all-gather | bytes 196608 | tf_op jit(solution)/shard_map/all_gather | solution.py:351
  156.0 2.7 %collective-permute-done.11 = f32[32]{0:T(128)S(1)} collective-permute-done((f32[32]{0:T(128)S(1)}, f32[32]{0:T(128)S(1)}, u32[]{:S(2)}, u32[]{:S(2)}) %collective-permute-start.11) | collective-permute-done | bytes 160 | tf_op jit(solution)/shard_map/ppermute | solution.py:144
  158.7 1.7 collective-permute-start.12
  160.4 1.8 %collective-permute-done.12 = f32[32]{0:T(128)S(1)} collective-permute-done((f32[32]{0:T(128)S(1)}, f32[32]{0:T(128)S(1)}, u32[]{:S(2)}, u32[]{:S(2)}) %collective-permute-start.12) | collective-permute-done | bytes 160 | tf_op jit(solution)/shard_map/ppermute | solution.py:144
  163.3 3.4 %collective-permute-done.13 = f32[32]{0:T(128)S(1)} collective-permute-done((f32[32]{0:T(128)S(1)}, f32[32]{0:T(128)S(1)}, u32[]{:S(2)}, u32[]{:S(2)}) %collective-permute-start.13) | collective-permute-done | bytes 160 | tf_op jit(solution)/shard_map/ppermute | solution.py:144
  (134 shorter events, 41.9 us)
Async XLA Ops:
  7.2 68.2 %all-gather.2.cloned.1.call-start = ((), (), s32[]{:S(2)}) async-start(), calls=%async_computation | async-start | bytes 4456448 | tf_op jit(solution)/shard_map/all_gather | solution.py:183
  15.8 25.1 %copy-start.6 = (bf16[256,256]{1,0:T(8,128)(2,1)}, bf16[256,256]{1,0:T(8,128)(2,1)S(1)}, u32[]{:S(2)}) copy-start(bf16[256,256]{1,0:T(8,128)(2,1)S(1)} %copy.36) | copy-start | bytes 393220
  18.5 29.8 %collective-permute-start = (bf16[4,256,64]{2,1,0:T(8,128)(2,1)}, bf16[4,256,64]{2,1,0:T(8,128)(2,1)}, u32[]{:S(2)}, u32[]{:S(2)}) collective-permute-start(bf16[4,256,64]{2,1,0:T(8,128)(2,1)} %bitcast.19), channel_id=1, source_target_pairs={{0,8},{2,10},{4,12},{6,14},{8,16},{10,18},{12,20},{14,22},{16,24},... | collective-permute-start | bytes 393224 | tf_op jit(solution)/shard_map/ppermute | solution.py:153
  24.1 25.1 %collective-permute-start.1 = (bf16[4,256,64]{2,1,0:T(8,128)(2,1)}, bf16[4,256,64]{2,1,0:T(8,128)(2,1)}, u32[]{:S(2)}, u32[]{:S(2)}) collective-permute-start(bf16[4,256,64]{2,1,0:T(8,128)(2,1)} %bitcast.19), channel_id=1, source_target_pairs={{0,6},{2,8},{4,10},{6,12},{8,14},{10,16},{12,18},{14,20},{16,22},{... | collective-permute-start | bytes 393224 | tf_op jit(solution)/shard_map/ppermute | solution.py:153
  27.4 22.8 %collective-permute-start.2 = (bf16[4,256,64]{2,1,0:T(8,128)(2,1)}, bf16[4,256,64]{2,1,0:T(8,128)(2,1)}, u32[]{:S(2)}, u32[]{:S(2)}) collective-permute-start(bf16[4,256,64]{2,1,0:T(8,128)(2,1)} %bitcast.19), channel_id=1, source_target_pairs={{0,4},{2,6},{4,8},{6,10},{8,12},{10,14},{12,16},{14,18},{16,20},{1... | collective-permute-start | bytes 393224 | tf_op jit(solution)/shard_map/ppermute | solution.py:153
  30.8 20.4 %collective-permute-start.3 = (bf16[4,256,64]{2,1,0:T(8,128)(2,1)}, bf16[4,256,64]{2,1,0:T(8,128)(2,1)}, u32[]{:S(2)}, u32[]{:S(2)}) collective-permute-start(bf16[4,256,64]{2,1,0:T(8,128)(2,1)} %bitcast.19), channel_id=1, source_target_pairs={{0,2},{2,4},{4,6},{6,8},{8,10},{10,12},{12,14},{14,16},{16,18},{18... | collective-permute-start | bytes 393224 | tf_op jit(solution)/shard_map/ppermute | solution.py:153
  36.9 4.1 %copy-start.12 = (f32[256,32]{0,1:T(8,128)S(1)}, f32[256,32]{0,1:T(8,128)}, u32[]{:S(2)}) copy-start(f32[256,32]{0,1:T(8,128)} %copy-done.11) | copy-start | bytes 98308
  75.4 30.7 %copy-start.14 = (s32[32]{0:T(128)S(1)}, s32[32]{0:T(128)}, u32[]{:S(2)}) copy-start(s32[32]{0:T(128)} %get-tuple-element.18) | copy-start | bytes 388
  106.1 5.5 %copy-start.4 = (bf16[256,2048]{1,0:T(8,128)(2,1)S(1)}, bf16[256,2048]{1,0:T(8,128)(2,1)}, u32[]{:S(2)}) copy-start(bf16[256,2048]{1,0:T(8,128)(2,1)} %param.9) | copy-start | bytes 3145732
  110.2 17.0 %copy-start.15 = (bf16[2048]{0:T(1024)(128)(2,1)S(1)}, bf16[2048]{0:T(1024)(128)(2,1)}, u32[]{:S(2)}) copy-start(bf16[2048]{0:T(1024)(128)(2,1)} %param.16) | copy-start | bytes 12292
  110.2 4.6 %collective-permute-start.5 = (bf16[32,1024]{1,0:T(8,128)(2,1)}, bf16[32,1024]{1,0:T(8,128)(2,1)}, u32[]{:S(2)}, u32[]{:S(2)}) collective-permute-start(bf16[32,1024]{1,0:T(8,128)(2,1)} %dynamic-slice_convert_fusion.3), channel_id=1, source_target_pairs={{0,1},{1,0},{2,3},{3,2},{4,5},{5,4},{6,7},{7,6},{8,9},{9,8},{10,11... | collective-permute-start | bytes 196616 | tf_op jit(solution)/shard_map/ppermute | solution.py:344
  116.2 10.9 %collective-permute-start.6 = (bf16[32,1024]{1,0:T(8,128)(2,1)S(1)}, bf16[32,1024]{1,0:T(8,128)(2,1)S(1)}, u32[]{:S(2)}, u32[]{:S(2)}) collective-permute-start(bf16[32,1024]{1,0:T(8,128)(2,1)S(1)} %add_convert_fusion.2), channel_id=1, source_target_pairs={{0,2},{2,0},{4,6},{6,4},{8,10},{10,8},{12,14},{14,12},{16,18},{18,... | collective-permute-start | bytes 196616 | tf_op jit(solution)/shard_map/ppermute | solution.py:144
  127.1 4.4 %collective-permute-start.7 = (bf16[32,1024]{1,0:T(8,128)(2,1)S(1)}, bf16[32,1024]{1,0:T(8,128)(2,1)S(1)}, u32[]{:S(2)}, u32[]{:S(2)}) collective-permute-start(bf16[32,1024]{1,0:T(8,128)(2,1)S(1)} %add.239), channel_id=1, source_target_pairs={{0,4},{2,6},{4,0},{6,2},{8,12},{10,14},{12,8},{14,10},{16,20},{18,... | collective-permute-start | bytes 196616 | tf_op jit(solution)/shard_map/ppermute | solution.py:144
  131.5 4.9 %collective-permute-start.8 = (bf16[32,1024]{1,0:T(8,128)(2,1)S(1)}, bf16[32,1024]{1,0:T(8,128)(2,1)S(1)}, u32[]{:S(2)}, u32[]{:S(2)}) collective-permute-start(bf16[32,1024]{1,0:T(8,128)(2,1)S(1)} %add.240), channel_id=1, source_target_pairs={{0,8},{2,10},{4,12},{6,14},{8,0},{10,2},{12,4},{14,6},{16,24},{18,... | collective-permute-start | bytes 196616 | tf_op jit(solution)/shard_map/ppermute | solution.py:144
  132.7 19.8 %copy-start.5 = (bf16[2048,1000]{0,1:T(8,128)(2,1)S(1)}, bf16[2048,1000]{0,1:T(8,128)(2,1)}, u32[]{:S(2)}) copy-start(bf16[2048,1000]{0,1:T(8,128)(2,1)} %param.17) | copy-start | bytes 12288004
  136.5 5.9 %collective-permute-start.9 = (bf16[32,1024]{1,0:T(8,128)(2,1)S(1)}, bf16[32,1024]{1,0:T(8,128)(2,1)S(1)}, u32[]{:S(2)}, u32[]{:S(2)}) collective-permute-start(bf16[32,1024]{1,0:T(8,128)(2,1)S(1)} %add.241), channel_id=1, source_target_pairs={{0,16},{2,18},{4,20},{6,22},{8,24},{10,26},{12,28},{14,30},{16,0},... | collective-permute-start | bytes 196616 | tf_op jit(solution)/shard_map/ppermute | solution.py:144
  138.7 32.0 %collective-permute-start.4 = (bf16[256,1024]{1,0:T(8,128)(2,1)S(1)}, bf16[256,1024]{1,0:T(8,128)(2,1)S(1)}, u32[]{:S(2)}, u32[]{:S(2)}) collective-permute-start(bf16[256,1024]{1,0:T(8,128)(2,1)S(1)} %dynamic-slice_convert_fusion), channel_id=1, source_target_pairs={{0,1},{1,0},{2,3},{3,2},{4,5},{5,4},{6,7},{7,6},{8,9},{9,8},{10,11... | collective-permute-start | bytes 1572872 | tf_op jit(solution)/shard_map/ppermute | solution.py:325
  152.6 15.6 %copy-start.7 = (bf16[256,256]{1,0:T(8,128)(2,1)S(1)}, bf16[256,256]{1,0:T(8,128)(2,1)}, u32[]{:S(2)}) copy-start(bf16[256,256]{1,0:T(8,128)(2,1)} %copy-done.6) | copy-start | bytes 393220
  152.6 18.2 %copy-start.1 = (f32[256,2048]{1,0:T(8,128)S(1)}, f32[256,2048]{1,0:T(8,128)}, u32[]{:S(2)}) copy-start(f32[256,2048]{1,0:T(8,128)} %convert_element_type.67) | copy-start | bytes 6291460
  154.0 1.2 collective-permute-start.10
  155.2 3.5 %collective-permute-start.11 = (f32[32]{0:T(128)S(1)}, f32[32]{0:T(128)S(1)}, u32[]{:S(2)}, u32[]{:S(2)}) collective-permute-start(f32[32]{0:T(128)S(1)} %max.26), channel_id=1, source_target_pairs={{0,4},{2,6},{4,0},{6,2},{8,12},{10,14},{12,8},{14,10},{16,20},{18,... | collective-permute-start | bytes 392 | tf_op jit(solution)/shard_map/ppermute | solution.py:144
  158.7 3.5 %collective-permute-start.12 = (f32[32]{0:T(128)S(1)}, f32[32]{0:T(128)S(1)}, u32[]{:S(2)}, u32[]{:S(2)}) collective-permute-start(f32[32]{0:T(128)S(1)} %max.27), channel_id=1, source_target_pairs={{0,8},{2,10},{4,12},{6,14},{8,0},{10,2},{12,4},{14,6},{16,24},{18,... | collective-permute-start | bytes 392 | tf_op jit(solution)/shard_map/ppermute | solution.py:144
  162.3 4.4 %collective-permute-start.13 = (f32[32]{0:T(128)S(1)}, f32[32]{0:T(128)S(1)}, u32[]{:S(2)}, u32[]{:S(2)}) collective-permute-start(f32[32]{0:T(128)S(1)} %max.28), channel_id=1, source_target_pairs={{0,16},{2,18},{4,20},{6,22},{8,24},{10,26},{12,28},{14,30},{16,0},... | collective-permute-start | bytes 392 | tf_op jit(solution)/shard_map/ppermute | solution.py:144
  166.7 3.5 %collective-permute-start.14 = (f32[32]{0:T(128)S(1)}, f32[32]{0:T(128)S(1)}, u32[]{:S(2)}, u32[]{:S(2)}) collective-permute-start(f32[32]{0:T(128)S(1)} %max.29), channel_id=1, source_target_pairs={{0,1},{1,0},{2,3},{3,2},{4,5},{5,4},{6,7},{7,6},{8,9},{9,8},{10,11... | collective-permute-start | bytes 392 | tf_op jit(solution)/shard_map/ppermute | solution.py:144
  (10 other events, 17.8 us)
Sparse Core Ops, SparseCore 0:
  10.8 64.6 all-gather.1

commit v10 on v7

--- a/solution.py
+++ b/solution.py
@@ -179,10 +179,15 @@
         ],
         2,
     )
-    own_prefix = jnp.transpose(own_prefix.reshape(G, prefix_rows, 2 * kv_heads, HD), (2, 0, 1, 3))
-    all_prefix = lax.all_gather(own_prefix, "seq", axis=2, tiled=True)
+    own_prefix = jnp.transpose(own_prefix.reshape(G, prefix_rows, 2 * kv_heads, HD), (0, 2, 3, 1))
+    prefix_pieces = [own_prefix] + [
+        lax.ppermute(
+            own_prefix, "seq", [(i, (i + distance) % seq_devices) for i in range(seq_devices)]
+        )
+        for distance in range(1, seq_devices)
+    ]
+    all_prefix = jnp.concatenate(prefix_pieces, 3)
     prefix_total = seq_devices * prefix_rows
-    all_prefix = jnp.transpose(all_prefix, (1, 0, 3, 2))
 
     activations = tokens.astype(jnp.float32)
     normed = (

time: 182 us -> 253 us (1.39)
  starting transfers between devices: 37.7 us -> 113 us
  local copies, waits for them, and re-layouts: 27.1 us -> 42.8 us
  between operations: 14.5 us -> 1.21 us
  waiting for transfers between devices: 39.1 us -> 29.6 us
    ppermute x0 -> x15, starting transfers between devices: none -> 85.1 us  [per_device(): lax.ppermute(own_prefix, 'seq', [(i, (i + distance) % seq_devices) for i...]
    unnamed x42 -> x61, local copies, waits for them, and re-layouts: 6.93 us -> 22 us
    all_gather x1 -> x0, waiting for transfers between devices: 11.7 us -> none  [per_device(): all_prefix = lax.all_gather(own_prefix, 'seq', axis=2, tiled=True)]
    ppermute x9, starting transfers between devices: 21.2 us -> 15.4 us  [butterfly(): partner = lax.ppermute(block, axis, [(i, i ^ step) for i in range(count)])]
    ppermute x4, starting transfers between devices: 15 us -> 11.1 us  [shifted_back(): return lax.ppermute(block, axis, route)]
    ppermute x4, waiting for transfers between devices: 0.01 us -> 3.67 us  [shifted_back(): return lax.ppermute(block, axis, route)]
  transfers between devices with their start and end apart: 15 -> 29, of which waited for: 11 -> 12; matrix products, arithmetic and copies ran while one was open for 17% -> 19% of each run, Pallas kernels for 5% -> 4%
where the time goes in v10:
time: 253 us; the launch traced here: 252 us
  starting transfers between devices  113 us (45%)
  local copies, waits for them, and re-layouts  42.8 us (17%)
  Pallas kernels  37.3 us (15%)
  waiting for transfers between devices  29.6 us (12%)
  matrix products  11.4 us (5%)
  other arithmetic  11.3 us (4%)
  blocking collectives  4.94 us (2%)
    ppermute x15, starting transfers between devices, per_device(): lax.ppermute(own_prefix, 'seq', [(i, (i + distance) % seq_devices) for i...  85.1 us
    pallas_call x1, Pallas kernels, per_device(): pl.pallas_call(functools.partial(prefix_kernel, kv_heads=kv_heads, prefix...  27.9 us
    unnamed x61, local copies, waits for them, and re-layouts  22 us
    ppermute x9, waiting for transfers between devices, butterfly(): partner = lax.ppermute(block, axis, [(i, i ^ step) for i in range(count)])  18.5 us
    ppermute x9, starting transfers between devices, butterfly(): partner = lax.ppermute(block, axis, [(i, i ^ step) for i in range(count)])  15.4 us
    ppermute x4, starting transfers between devices, shifted_back(): return lax.ppermute(block, axis, route)  11.1 us
    pallas_call x1, Pallas kernels, per_device(): pl.pallas_call(functools.partial(suffix_kernel, kv_heads=kv_heads, suffix...  9.44 us
    ppermute x1, waiting for transfers between devices, per_device(): received = lax.ppermute(sent.astype(jnp.bfloat16), 'mp', [(0, 1), (1, 0)])  6.88 us
  transfers between devices with their start and end apart: 29, of which 12 were waited for; matrix products, arithmetic and copies ran while one was open for 19% of the time, Pallas kernels for 4%

profile of v10, /device:TPU:0, one launch (start us, length us, event | category | flops | bytes accessed | tf_op | source)
XLA Modules:
  0.0 251.7 jit_solution(12554336543768125158)
XLA Ops:
  3.3 2.5 %collective-permute-start.1 = (bf16[4,4,64,128]{3,2,1,0:T(8,128)(2,1)}, bf16[4,4,64,128]{3,2,1,0:T(8,128)(2,1)}, u32[]{:S(2)}, u32[]{:S(2)}) collective-permute-start(bf16[4,4,64,128]{3,2,1,0:T(8,128)(2,1)} %bitcast.14), channel_id=1, source_target_pairs={{0,4},{2,6},{4,8},{6,10},{8,12},{10,14},{12,16},{14,18},{16,20},{1... | collective-permute-start | bytes 786440 | tf_op jit(solution)/shard_map/ppermute | solution.py:184
  20.3 4.3 %collective-permute-start.15 = (bf16[4,256,64]{2,1,0:T(8,128)(2,1)}, bf16[4,256,64]{2,1,0:T(8,128)(2,1)}, u32[]{:S(2)}, u32[]{:S(2)}) collective-permute-start(bf16[4,256,64]{2,1,0:T(8,128)(2,1)} %bitcast.19), channel_id=1, source_target_pairs={{0,8},{2,10},{4,12},{6,14},{8,16},{10,18},{12,20},{14,22},{16,24},... | collective-permute-start | bytes 393224 | tf_op jit(solution)/shard_map/ppermute | solution.py:153
  24.6 2.7 %collective-permute-start.16 = (bf16[4,256,64]{2,1,0:T(8,128)(2,1)}, bf16[4,256,64]{2,1,0:T(8,128)(2,1)}, u32[]{:S(2)}, u32[]{:S(2)}) collective-permute-start(bf16[4,256,64]{2,1,0:T(8,128)(2,1)} %bitcast.19), channel_id=1, source_target_pairs={{0,6},{2,8},{4,10},{6,12},{8,14},{10,16},{12,18},{14,20},{16,22},{... | collective-permute-start | bytes 393224 | tf_op jit(solution)/shard_map/ppermute | solution.py:153
  27.3 4.1 %fusion.1 = f32[256,1024]{0,1:T(8,128)S(1)} fusion(bf16[2048,1024]{1,0:T(8,128)(2,1)} %param.13, f32[2048]{0:T(1024)} %copy-done.16, f32[256]{0:T(256)} %copy-done.20, bf16[256,2048]{1,0:T(8,128)(2,1)S(1)} %copy-done.2), kind=kOutput, calls=%fused_computation.17 | convolution fusion | flops 1075838976 | bytes 6300672 | tf_op jit(solution)/shard_map/dot_general | solution.py:221
  43.8 2.8 %collective-permute-start.17 = (bf16[4,256,64]{2,1,0:T(8,128)(2,1)}, bf16[4,256,64]{2,1,0:T(8,128)(2,1)S(1)}, u32[]{:S(2)}, u32[]{:S(2)}) collective-permute-start(bf16[4,256,64]{2,1,0:T(8,128)(2,1)} %bitcast.19), channel_id=1, source_target_pairs={{0,4},{2,6},{4,8},{6,10},{8,12},{10,14},{12,16},{14,18},{16,20},{1... | collective-permute-start | bytes 393224 | tf_op jit(solution)/shard_map/ppermute | solution.py:153
  49.9 3.7 %collective-permute-done.17 = bf16[4,256,64]{2,1,0:T(8,128)(2,1)S(1)} collective-permute-done((bf16[4,256,64]{2,1,0:T(8,128)(2,1)}, bf16[4,256,64]{2,1,0:T(8,128)(2,1)S(1)}, u32[]{:S(2)}, u32[]{:S(2)}) %collective-permute-start.17) | collective-permute-done | bytes 131104 | tf_op jit(solution)/shard_map/ppermute | solution.py:153
  58.2 9.4 %shard_map.120 = (f32[2,2048,1]{2,1,0:T(8,128)}, f32[2,2048,1]{2,1,0:T(8,128)}, f32[2,2048,64]{2,1,0:T(8,128)}) custom-call(s32[8]{0:T(128)} %reshape.323.table, bf16[2,2048,64]{2,1,0:T(8,128)(2,1)} %bitcast.56, s32[2048,1]{1,0:T(8,128)} %broadcast_in_dim_reshape.13.rr_ref, s32[2048,1]{1,0:T(8,128)} %broadcast_in_dim_reshape.14.rp_ref, ...), custom_call_target="tpu_custom_call" | custom-call | tf_op jit(solution)/shard_map/pallas_call | solution.py:283
  67.7 6.0 %collective-permute-start.5 = (bf16[4,4,64,128]{3,2,1,0:T(8,128)(2,1)}, bf16[4,4,64,128]{3,2,1,0:T(8,128)(2,1)S(1)}, u32[]{:S(2)}, u32[]{:S(2)}) collective-permute-start(bf16[4,4,64,128]{3,2,1,0:T(8,128)(2,1)} %bitcast.14), channel_id=1, source_target_pairs={{0,12},{2,14},{4,16},{6,18},{8,20},{10,22},{12,24},{14,26},{16,28}... | collective-permute-start | bytes 786440 | tf_op jit(solution)/shard_map/ppermute | solution.py:184
  75.4 5.2 %collective-permute-start.6 = (bf16[4,4,64,128]{3,2,1,0:T(8,128)(2,1)}, bf16[4,4,64,128]{3,2,1,0:T(8,128)(2,1)S(1)}, u32[]{:S(2)}, u32[]{:S(2)}) collective-permute-start(bf16[4,4,64,128]{3,2,1,0:T(8,128)(2,1)} %bitcast.14), channel_id=1, source_target_pairs={{0,14},{2,16},{4,18},{6,20},{8,22},{10,24},{12,26},{14,28},{16,30}... | collective-permute-start | bytes 786440 | tf_op jit(solution)/shard_map/ppermute | solution.py:184
  82.3 10.9 %collective-permute-start.7 = (bf16[4,4,64,128]{3,2,1,0:T(8,128)(2,1)}, bf16[4,4,64,128]{3,2,1,0:T(8,128)(2,1)S(1)}, u32[]{:S(2)}, u32[]{:S(2)}) collective-permute-start(bf16[4,4,64,128]{3,2,1,0:T(8,128)(2,1)} %bitcast.14), channel_id=1, source_target_pairs={{0,16},{2,18},{4,20},{6,22},{8,24},{10,26},{12,28},{14,30},{16,0},... | collective-permute-start | bytes 786440 | tf_op jit(solution)/shard_map/ppermute | solution.py:184
  98.4 15.0 %collective-permute-start.10 = (bf16[4,4,64,128]{3,2,1,0:T(8,128)(2,1)}, bf16[4,4,64,128]{3,2,1,0:T(8,128)(2,1)S(1)}, u32[]{:S(2)}, u32[]{:S(2)}) collective-permute-start(bf16[4,4,64,128]{3,2,1,0:T(8,128)(2,1)} %bitcast.14), channel_id=1, source_target_pairs={{0,22},{2,24},{4,26},{6,28},{8,30},{10,0},{12,2},{14,4},{16,6},{18... | collective-permute-start | bytes 786440 | tf_op jit(solution)/shard_map/ppermute | solution.py:184
  114.1 11.0 %collective-permute-start.11 = (bf16[4,4,64,128]{3,2,1,0:T(8,128)(2,1)}, bf16[4,4,64,128]{3,2,1,0:T(8,128)(2,1)S(1)}, u32[]{:S(2)}, u32[]{:S(2)}) collective-permute-start(bf16[4,4,64,128]{3,2,1,0:T(8,128)(2,1)} %bitcast.14), channel_id=1, source_target_pairs={{0,24},{2,26},{4,28},{6,30},{8,0},{10,2},{12,4},{14,6},{16,8},{18,... | collective-permute-start | bytes 786440 | tf_op jit(solution)/shard_map/ppermute | solution.py:184
  126.0 12.7 %collective-permute-start.12 = (bf16[4,4,64,128]{3,2,1,0:T(8,128)(2,1)}, bf16[4,4,64,128]{3,2,1,0:T(8,128)(2,1)S(1)}, u32[]{:S(2)}, u32[]{:S(2)}) collective-permute-start(bf16[4,4,64,128]{3,2,1,0:T(8,128)(2,1)} %bitcast.14), channel_id=1, source_target_pairs={{0,26},{2,28},{4,30},{6,0},{8,2},{10,4},{12,6},{14,8},{16,10},{18,... | collective-permute-start | bytes 786440 | tf_op jit(solution)/shard_map/ppermute | solution.py:184
  139.4 12.0 %collective-permute-start.13 = (bf16[4,4,64,128]{3,2,1,0:T(8,128)(2,1)}, bf16[4,4,64,128]{3,2,1,0:T(8,128)(2,1)S(1)}, u32[]{:S(2)}, u32[]{:S(2)}) collective-permute-start(bf16[4,4,64,128]{3,2,1,0:T(8,128)(2,1)} %bitcast.14), channel_id=1, source_target_pairs={{0,28},{2,30},{4,0},{6,2},{8,4},{10,6},{12,8},{14,10},{16,12},{18,... | collective-permute-start | bytes 786440 | tf_op jit(solution)/shard_map/ppermute | solution.py:184
  152.1 4.3 %collective-permute-start.14 = (bf16[4,4,64,128]{3,2,1,0:T(8,128)(2,1)}, bf16[4,4,64,128]{3,2,1,0:T(8,128)(2,1)S(1)}, u32[]{:S(2)}, u32[]{:S(2)}) collective-permute-start(bf16[4,4,64,128]{3,2,1,0:T(8,128)(2,1)} %bitcast.14), channel_id=1, source_target_pairs={{0,30},{2,0},{4,2},{6,4},{8,6},{10,8},{12,10},{14,12},{16,14},{18,... | collective-permute-start | bytes 786440 | tf_op jit(solution)/shard_map/ppermute | solution.py:184
  161.4 27.9 %shard_map.121 = bf16[2,2048,64]{2,1,0:T(8,128)(2,1)} custom-call(s32[8]{0:T(128)} %reshape.323.table, bf16[2,2048,64]{2,1,0:T(8,128)(2,1)} %bitcast.57, s32[2048,1]{1,0:T(8,128)} %broadcast_in_dim_reshape.12.rg_ref, bf16[4,4,64,2048]{3,2,1,0:T(8,128)(2,1)} %constant_dynamic-update-slice_fusion.pk_ref.pv_ref, ...), custom_call_target="tpu_custom_call" | custom-call | tf_op jit(solution)/shard_map/pallas_call | solution.py:301
  191.7 3.7 %fusion.10 = f32[256,2048]{1,0:T(8,128)S(1)} fusion(bf16[256,1024]{0,1:T(8,128)(2,1)} %bitcast.62, bf16[1024,2048]{1,0:T(8,128)(2,1)} %param.15), kind=kOutput, calls=%fused_computation.98 | convolution fusion | flops 1073741824 | bytes 6815744 | tf_op jit(solution)/shard_map/dot_general | solution.py:324
  200.7 6.9 %collective-permute-done.19 = bf16[256,1024]{1,0:T(8,128)(2,1)} collective-permute-done((bf16[256,1024]{1,0:T(8,128)(2,1)}, bf16[256,1024]{1,0:T(8,128)(2,1)}, u32[]{:S(2)}, u32[]{:S(2)}) %collective-permute-start.19) | collective-permute-done | bytes 524320 | tf_op jit(solution)/shard_map/ppermute | solution.py:330
  211.2 4.3 %collective-permute-done.21 = bf16[32,1024]{1,0:T(8,128)(2,1)S(1)} collective-permute-done((bf16[32,1024]{1,0:T(8,128)(2,1)S(1)}, bf16[32,1024]{1,0:T(8,128)(2,1)S(1)}, u32[]{:S(2)}, u32[]{:S(2)}) %collective-permute-start.21) | collective-permute-done | bytes 65568 | tf_op jit(solution)/shard_map/ppermute | solution.py:144
  215.4 3.9 %collective-permute-start.22 = (bf16[32,1024]{1,0:T(8,128)(2,1)S(1)}, bf16[32,1024]{1,0:T(8,128)(2,1)S(1)}, u32[]{:S(2)}, u32[]{:S(2)}) collective-permute-start(bf16[32,1024]{1,0:T(8,128)(2,1)S(1)} %add.230), channel_id=1, source_target_pairs={{0,8},{2,10},{4,12},{6,14},{8,0},{10,2},{12,4},{14,6},{16,24},{18,... | collective-permute-start | bytes 196616 | tf_op jit(solution)/shard_map/ppermute | solution.py:144
  221.6 4.2 %collective-permute-start.23 = (bf16[32,1024]{1,0:T(8,128)(2,1)S(1)}, bf16[32,1024]{1,0:T(8,128)(2,1)S(1)}, u32[]{:S(2)}, u32[]{:S(2)}) collective-permute-start(bf16[32,1024]{1,0:T(8,128)(2,1)S(1)} %add.231), channel_id=1, source_target_pairs={{0,16},{2,18},{4,20},{6,22},{8,24},{10,26},{12,28},{14,30},{16,0},... | collective-permute-start | bytes 196616 | tf_op jit(solution)/shard_map/ppermute | solution.py:144
  228.1 4.9 %all_gather.3 = bf16[32,2048]{1,0:T(8,128)(2,1)S(1)} all-gather(bf16[32,1024]{1,0:T(8,128)(2,1)S(1)} %add.232), channel_id=1, replica_groups=mesh['seq'=16,'mp'=2] {'mp'}, dimensions={1}, use_global_device_ids=true | all-gather | bytes 196608 | tf_op jit(solution)/shard_map/all_gather | solution.py:345
  236.4 3.0 %collective-permute-done.25 = f32[32]{0:T(128)S(1)} collective-permute-done((f32[32]{0:T(128)S(1)}, f32[32]{0:T(128)S(1)}, u32[]{:S(2)}, u32[]{:S(2)}) %collective-permute-start.25) | collective-permute-done | bytes 160 | tf_op jit(solution)/shard_map/ppermute | solution.py:144
  243.0 3.1 %collective-permute-start.27 = (f32[32]{0:T(128)S(1)}, f32[32]{0:T(128)S(1)}, u32[]{:S(2)}, u32[]{:S(2)}) collective-permute-start(f32[32]{0:T(128)S(1)} %max.28), channel_id=1, source_target_pairs={{0,16},{2,18},{4,20},{6,22},{8,24},{10,26},{12,28},{14,30},{16,0},... | collective-permute-start | bytes 392 | tf_op jit(solution)/shard_map/ppermute | solution.py:144
  (179 shorter events, 81.9 us)
Async XLA Ops:
  2.9 64.8 %collective-permute-start = (bf16[4,4,64,128]{3,2,1,0:T(8,128)(2,1)}, bf16[4,4,64,128]{3,2,1,0:T(8,128)(2,1)}, u32[]{:S(2)}, u32[]{:S(2)}) collective-permute-start(bf16[4,4,64,128]{3,2,1,0:T(8,128)(2,1)} %bitcast.14), channel_id=1, source_target_pairs={{0,2},{2,4},{4,6},{6,8},{8,10},{10,12},{12,14},{14,16},{16,18},{18... | collective-permute-start | bytes 786440 | tf_op jit(solution)/shard_map/ppermute | solution.py:184
  3.3 72.0 %collective-permute-start.1 = (bf16[4,4,64,128]{3,2,1,0:T(8,128)(2,1)}, bf16[4,4,64,128]{3,2,1,0:T(8,128)(2,1)}, u32[]{:S(2)}, u32[]{:S(2)}) collective-permute-start(bf16[4,4,64,128]{3,2,1,0:T(8,128)(2,1)} %bitcast.14), channel_id=1, source_target_pairs={{0,4},{2,6},{4,8},{6,10},{8,12},{10,14},{12,16},{14,18},{16,20},{1... | collective-permute-start | bytes 786440 | tf_op jit(solution)/shard_map/ppermute | solution.py:184
  5.9 76.5 %collective-permute-start.2 = (bf16[4,4,64,128]{3,2,1,0:T(8,128)(2,1)}, bf16[4,4,64,128]{3,2,1,0:T(8,128)(2,1)}, u32[]{:S(2)}, u32[]{:S(2)}) collective-permute-start(bf16[4,4,64,128]{3,2,1,0:T(8,128)(2,1)} %bitcast.14), channel_id=1, source_target_pairs={{0,6},{2,8},{4,10},{6,12},{8,14},{10,16},{12,18},{14,20},{16,22},{... | collective-permute-start | bytes 786440 | tf_op jit(solution)/shard_map/ppermute | solution.py:184
  20.3 23.5 %collective-permute-start.15 = (bf16[4,256,64]{2,1,0:T(8,128)(2,1)}, bf16[4,256,64]{2,1,0:T(8,128)(2,1)}, u32[]{:S(2)}, u32[]{:S(2)}) collective-permute-start(bf16[4,256,64]{2,1,0:T(8,128)(2,1)} %bitcast.19), channel_id=1, source_target_pairs={{0,8},{2,10},{4,12},{6,14},{8,16},{10,18},{12,20},{14,22},{16,24},... | collective-permute-start | bytes 393224 | tf_op jit(solution)/shard_map/ppermute | solution.py:153
  24.6 23.0 %collective-permute-start.16 = (bf16[4,256,64]{2,1,0:T(8,128)(2,1)}, bf16[4,256,64]{2,1,0:T(8,128)(2,1)}, u32[]{:S(2)}, u32[]{:S(2)}) collective-permute-start(bf16[4,256,64]{2,1,0:T(8,128)(2,1)} %bitcast.19), channel_id=1, source_target_pairs={{0,6},{2,8},{4,10},{6,12},{8,14},{10,16},{12,18},{14,20},{16,22},{... | collective-permute-start | bytes 393224 | tf_op jit(solution)/shard_map/ppermute | solution.py:153
  43.8 9.8 %collective-permute-start.17 = (bf16[4,256,64]{2,1,0:T(8,128)(2,1)}, bf16[4,256,64]{2,1,0:T(8,128)(2,1)S(1)}, u32[]{:S(2)}, u32[]{:S(2)}) collective-permute-start(bf16[4,256,64]{2,1,0:T(8,128)(2,1)} %bitcast.19), channel_id=1, source_target_pairs={{0,4},{2,6},{4,8},{6,10},{8,12},{10,14},{12,16},{14,18},{16,20},{1... | collective-permute-start | bytes 393224 | tf_op jit(solution)/shard_map/ppermute | solution.py:153
  47.5 8.5 %collective-permute-start.18 = (bf16[4,256,64]{2,1,0:T(8,128)(2,1)}, bf16[4,256,64]{2,1,0:T(8,128)(2,1)S(1)}, u32[]{:S(2)}, u32[]{:S(2)}) collective-permute-start(bf16[4,256,64]{2,1,0:T(8,128)(2,1)} %bitcast.19), channel_id=1, source_target_pairs={{0,2},{2,4},{4,6},{6,8},{8,10},{10,12},{12,14},{14,16},{16,18},{18... | collective-permute-start | bytes 393224 | tf_op jit(solution)/shard_map/ppermute | solution.py:153
  53.6 41.4 %collective-permute-start.3 = (bf16[4,4,64,128]{3,2,1,0:T(8,128)(2,1)}, bf16[4,4,64,128]{3,2,1,0:T(8,128)(2,1)}, u32[]{:S(2)}, u32[]{:S(2)}) collective-permute-start(bf16[4,4,64,128]{3,2,1,0:T(8,128)(2,1)} %bitcast.14), channel_id=1, source_target_pairs={{0,8},{2,10},{4,12},{6,14},{8,16},{10,18},{12,20},{14,22},{16,24},... | collective-permute-start | bytes 786440 | tf_op jit(solution)/shard_map/ppermute | solution.py:184
  56.1 40.5 %collective-permute-start.4 = (bf16[4,4,64,128]{3,2,1,0:T(8,128)(2,1)}, bf16[4,4,64,128]{3,2,1,0:T(8,128)(2,1)}, u32[]{:S(2)}, u32[]{:S(2)}) collective-permute-start(bf16[4,4,64,128]{3,2,1,0:T(8,128)(2,1)} %bitcast.14), channel_id=1, source_target_pairs={{0,10},{2,12},{4,14},{6,16},{8,18},{10,20},{12,22},{14,24},{16,26}... | collective-permute-start | bytes 786440 | tf_op jit(solution)/shard_map/ppermute | solution.py:184
  67.7 30.7 %collective-permute-start.5 = (bf16[4,4,64,128]{3,2,1,0:T(8,128)(2,1)}, bf16[4,4,64,128]{3,2,1,0:T(8,128)(2,1)S(1)}, u32[]{:S(2)}, u32[]{:S(2)}) collective-permute-start(bf16[4,4,64,128]{3,2,1,0:T(8,128)(2,1)} %bitcast.14), channel_id=1, source_target_pairs={{0,12},{2,14},{4,16},{6,18},{8,20},{10,22},{12,24},{14,26},{16,28}... | collective-permute-start | bytes 786440 | tf_op jit(solution)/shard_map/ppermute | solution.py:184
  75.4 38.8 %collective-permute-start.6 = (bf16[4,4,64,128]{3,2,1,0:T(8,128)(2,1)}, bf16[4,4,64,128]{3,2,1,0:T(8,128)(2,1)S(1)}, u32[]{:S(2)}, u32[]{:S(2)}) collective-permute-start(bf16[4,4,64,128]{3,2,1,0:T(8,128)(2,1)} %bitcast.14), channel_id=1, source_target_pairs={{0,14},{2,16},{4,18},{6,20},{8,22},{10,24},{12,26},{14,28},{16,30}... | collective-permute-start | bytes 786440 | tf_op jit(solution)/shard_map/ppermute | solution.py:184
  82.3 43.6 %collective-permute-start.7 = (bf16[4,4,64,128]{3,2,1,0:T(8,128)(2,1)}, bf16[4,4,64,128]{3,2,1,0:T(8,128)(2,1)S(1)}, u32[]{:S(2)}, u32[]{:S(2)}) collective-permute-start(bf16[4,4,64,128]{3,2,1,0:T(8,128)(2,1)} %bitcast.14), channel_id=1, source_target_pairs={{0,16},{2,18},{4,20},{6,22},{8,24},{10,26},{12,28},{14,30},{16,0},... | collective-permute-start | bytes 786440 | tf_op jit(solution)/shard_map/ppermute | solution.py:184
  94.9 44.5 %collective-permute-start.8 = (bf16[4,4,64,128]{3,2,1,0:T(8,128)(2,1)}, bf16[4,4,64,128]{3,2,1,0:T(8,128)(2,1)S(1)}, u32[]{:S(2)}, u32[]{:S(2)}) collective-permute-start(bf16[4,4,64,128]{3,2,1,0:T(8,128)(2,1)} %bitcast.14), channel_id=1, source_target_pairs={{0,18},{2,20},{4,22},{6,24},{8,26},{10,28},{12,30},{14,0},{16,2},{... | collective-permute-start | bytes 786440 | tf_op jit(solution)/shard_map/ppermute | solution.py:184
  96.6 55.5 %collective-permute-start.9 = (bf16[4,4,64,128]{3,2,1,0:T(8,128)(2,1)}, bf16[4,4,64,128]{3,2,1,0:T(8,128)(2,1)S(1)}, u32[]{:S(2)}, u32[]{:S(2)}) collective-permute-start(bf16[4,4,64,128]{3,2,1,0:T(8,128)(2,1)} %bitcast.14), channel_id=1, source_target_pairs={{0,20},{2,22},{4,24},{6,26},{8,28},{10,30},{12,0},{14,2},{16,4},{1... | collective-permute-start | bytes 786440 | tf_op jit(solution)/shard_map/ppermute | solution.py:184
  98.4 58.8 %collective-permute-start.10 = (bf16[4,4,64,128]{3,2,1,0:T(8,128)(2,1)}, bf16[4,4,64,128]{3,2,1,0:T(8,128)(2,1)S(1)}, u32[]{:S(2)}, u32[]{:S(2)}) collective-permute-start(bf16[4,4,64,128]{3,2,1,0:T(8,128)(2,1)} %bitcast.14), channel_id=1, source_target_pairs={{0,22},{2,24},{4,26},{6,28},{8,30},{10,0},{12,2},{14,4},{16,6},{18... | collective-permute-start | bytes 786440 | tf_op jit(solution)/shard_map/ppermute | solution.py:184
  114.1 43.8 %collective-permute-start.11 = (bf16[4,4,64,128]{3,2,1,0:T(8,128)(2,1)}, bf16[4,4,64,128]{3,2,1,0:T(8,128)(2,1)S(1)}, u32[]{:S(2)}, u32[]{:S(2)}) collective-permute-start(bf16[4,4,64,128]{3,2,1,0:T(8,128)(2,1)} %bitcast.14), channel_id=1, source_target_pairs={{0,24},{2,26},{4,28},{6,30},{8,0},{10,2},{12,4},{14,6},{16,8},{18,... | collective-permute-start | bytes 786440 | tf_op jit(solution)/shard_map/ppermute | solution.py:184
  126.0 32.7 %collective-permute-start.12 = (bf16[4,4,64,128]{3,2,1,0:T(8,128)(2,1)}, bf16[4,4,64,128]{3,2,1,0:T(8,128)(2,1)S(1)}, u32[]{:S(2)}, u32[]{:S(2)}) collective-permute-start(bf16[4,4,64,128]{3,2,1,0:T(8,128)(2,1)} %bitcast.14), channel_id=1, source_target_pairs={{0,26},{2,28},{4,30},{6,0},{8,2},{10,4},{12,6},{14,8},{16,10},{18,... | collective-permute-start | bytes 786440 | tf_op jit(solution)/shard_map/ppermute | solution.py:184
  139.4 20.0 %collective-permute-start.13 = (bf16[4,4,64,128]{3,2,1,0:T(8,128)(2,1)}, bf16[4,4,64,128]{3,2,1,0:T(8,128)(2,1)S(1)}, u32[]{:S(2)}, u32[]{:S(2)}) collective-permute-start(bf16[4,4,64,128]{3,2,1,0:T(8,128)(2,1)} %bitcast.14), channel_id=1, source_target_pairs={{0,28},{2,30},{4,0},{6,2},{8,4},{10,6},{12,8},{14,10},{16,12},{18,... | collective-permute-start | bytes 786440 | tf_op jit(solution)/shard_map/ppermute | solution.py:184
  152.1 8.5 %collective-permute-start.14 = (bf16[4,4,64,128]{3,2,1,0:T(8,128)(2,1)}, bf16[4,4,64,128]{3,2,1,0:T(8,128)(2,1)S(1)}, u32[]{:S(2)}, u32[]{:S(2)}) collective-permute-start(bf16[4,4,64,128]{3,2,1,0:T(8,128)(2,1)} %bitcast.14), channel_id=1, source_target_pairs={{0,30},{2,0},{4,2},{6,4},{8,6},{10,8},{12,10},{14,12},{16,14},{18,... | collective-permute-start | bytes 786440 | tf_op jit(solution)/shard_map/ppermute | solution.py:184
  197.7 9.9 %collective-permute-start.19 = (bf16[256,1024]{1,0:T(8,128)(2,1)}, bf16[256,1024]{1,0:T(8,128)(2,1)}, u32[]{:S(2)}, u32[]{:S(2)}) collective-permute-start(bf16[256,1024]{1,0:T(8,128)(2,1)} %dynamic-slice_convert_fusion), channel_id=1, source_target_pairs={{0,1},{1,0},{2,3},{3,2},{4,5},{5,4},{6,7},{7,6},{8,9},{9,8},{10,11... | collective-permute-start | bytes 1572872 | tf_op jit(solution)/shard_map/ppermute | solution.py:330
  211.1 4.3 %collective-permute-start.21 = (bf16[32,1024]{1,0:T(8,128)(2,1)S(1)}, bf16[32,1024]{1,0:T(8,128)(2,1)S(1)}, u32[]{:S(2)}, u32[]{:S(2)}) collective-permute-start(bf16[32,1024]{1,0:T(8,128)(2,1)S(1)} %add.229), channel_id=1, source_target_pairs={{0,4},{2,6},{4,0},{6,2},{8,12},{10,14},{12,8},{14,10},{16,20},{18,... | collective-permute-start | bytes 196616 | tf_op jit(solution)/shard_map/ppermute | solution.py:144
  215.4 6.2 %collective-permute-start.22 = (bf16[32,1024]{1,0:T(8,128)(2,1)S(1)}, bf16[32,1024]{1,0:T(8,128)(2,1)S(1)}, u32[]{:S(2)}, u32[]{:S(2)}) collective-permute-start(bf16[32,1024]{1,0:T(8,128)(2,1)S(1)} %add.230), channel_id=1, source_target_pairs={{0,8},{2,10},{4,12},{6,14},{8,0},{10,2},{12,4},{14,6},{16,24},{18,... | collective-permute-start | bytes 196616 | tf_op jit(solution)/shard_map/ppermute | solution.py:144
  221.6 6.5 %collective-permute-start.23 = (bf16[32,1024]{1,0:T(8,128)(2,1)S(1)}, bf16[32,1024]{1,0:T(8,128)(2,1)S(1)}, u32[]{:S(2)}, u32[]{:S(2)}) collective-permute-start(bf16[32,1024]{1,0:T(8,128)(2,1)S(1)} %add.231), channel_id=1, source_target_pairs={{0,16},{2,18},{4,20},{6,22},{8,24},{10,26},{12,28},{14,30},{16,0},... | collective-permute-start | bytes 196616 | tf_op jit(solution)/shard_map/ppermute | solution.py:144
  243.0 4.6 %collective-permute-start.27 = (f32[32]{0:T(128)S(1)}, f32[32]{0:T(128)S(1)}, u32[]{:S(2)}, u32[]{:S(2)}) collective-permute-start(f32[32]{0:T(128)S(1)} %max.28), channel_id=1, source_target_pairs={{0,16},{2,18},{4,20},{6,22},{8,24},{10,26},{12,28},{14,30},{16,0},... | collective-permute-start | bytes 392 | tf_op jit(solution)/shard_map/ppermute | solution.py:144
  (26 other events, 297.6 us)

commit v11 on v7

--- a/solution.py
+++ b/solution.py
@@ -316,15 +316,23 @@
     context = jnp.transpose(
         context.reshape(kv_heads, token_rows, repeat_count, HD), (1, 0, 2, 3)
     ).reshape(token_rows, query_heads * HD)
-    mixture = jnp.dot(context, w_out, preferred_element_type=jnp.float32)
     mp_devices = lax.axis_size("mp")
     own_columns = lax.dynamic_slice_in_dim(activations, mp_index * part_width, part_width, 1)
     if mp_devices == 2:
-        kept = lax.dynamic_slice_in_dim(mixture, mp_index * part_width, part_width, 1)
-        sent = lax.dynamic_slice_in_dim(mixture, (1 - mp_index) * part_width, part_width, 1)
+        sent = jnp.dot(
+            context,
+            lax.dynamic_slice_in_dim(w_out, (1 - mp_index) * part_width, part_width, 1),
+            preferred_element_type=jnp.float32,
+        )
         received = lax.ppermute(sent.astype(jnp.bfloat16), "mp", [(0, 1), (1, 0)])
+        kept = jnp.dot(
+            context,
+            lax.dynamic_slice_in_dim(w_out, mp_index * part_width, part_width, 1),
+            preferred_element_type=jnp.float32,
+        )
         hidden = (own_columns + (kept + received.astype(jnp.float32))).astype(jnp.bfloat16)
     else:
+        mixture = jnp.dot(context, w_out, preferred_element_type=jnp.float32)
         mixture = lax.psum_scatter(
             mixture.astype(jnp.bfloat16), "mp", scatter_dimension=1, tiled=True
         ).astype(jnp.float32)

time: 182 us -> 179 us (0.984)
  starting transfers between devices: 37.7 us -> 32.5 us
  waiting for transfers between devices: 39.1 us -> 43.7 us
  matrix products: 10.1 us -> 12.9 us
  local copies, waits for them, and re-layouts: 27.1 us -> 25 us
  other arithmetic: 9.52 us -> 7.6 us
    ppermute x9, starting transfers between devices: 21.2 us -> 16 us  [butterfly(): partner = lax.ppermute(block, axis, [(i, i ^ step) for i in range(count)])]
    ppermute x1, waiting for transfers between devices: 6.48 us -> 11.4 us  [per_device(): received = lax.ppermute(sent.astype(jnp.bfloat16), 'mp', [(0, 1), (1, 0)])]
    dot_general x1 -> x2, matrix products: 3.7 us -> 6.41 us  [the longest x1 3.36 us: per_device(): jnp.dot(context, lax.dynamic_slice_in_dim(w_out, (1 - mp_index) * part_wi...]
    convert_element_type x1 -> x0, other arithmetic: 1.95 us -> none  [per_device(): (own_columns + (kept + received.astype(jnp.float32))).astype(jnp.bfloat16)]
    unnamed x42 -> x40, local copies, waits for them, and re-layouts: 6.93 us -> 5.63 us
where the time goes in v11:
time: 179 us
  waiting for transfers between devices  43.7 us (24%)
  Pallas kernels  37.5 us (21%)
  starting transfers between devices  32.5 us (18%)
  local copies, waits for them, and re-layouts  25 us (14%)
  between operations  14.5 us (8%)
  matrix products  12.9 us (7%)
  other arithmetic  7.6 us (4%)
  blocking collectives  4.94 us (3%)
    pallas_call x1, Pallas kernels, per_device(): pl.pallas_call(functools.partial(prefix_kernel, kv_heads=kv_heads, prefix...  28.1 us
    ppermute x9, waiting for transfers between devices, butterfly(): partner = lax.ppermute(block, axis, [(i, i ^ step) for i in range(count)])  20.6 us
    ppermute x9, starting transfers between devices, butterfly(): partner = lax.ppermute(block, axis, [(i, i ^ step) for i in range(count)])  16 us
    ppermute x4, starting transfers between devices, shifted_back(): return lax.ppermute(block, axis, route)  15 us
    all_gather x1, waiting for transfers between devices, per_device(): all_prefix = lax.all_gather(own_prefix, 'seq', axis=2, tiled=True)  11.7 us
    ppermute x1, waiting for transfers between devices, per_device(): received = lax.ppermute(sent.astype(jnp.bfloat16), 'mp', [(0, 1), (1, 0)])  11.4 us
    pallas_call x1, Pallas kernels, per_device(): pl.pallas_call(functools.partial(suffix_kernel, kv_heads=kv_heads, suffix...  9.39 us
    unnamed x40, local copies, waits for them, and re-layouts  5.63 us
  transfers between devices with their start and end apart: 15, of which 11 were waited for; matrix products, arithmetic and copies ran while one was open for 17% of the time, Pallas kernels for 5%

profile of v11, /device:TPU:0, one launch (start us, length us, event | category | flops | bytes accessed | tf_op | source)
XLA Modules:
  0.0 178.6 jit_solution(15259940167107139529)
XLA Ops:
  18.5 5.6 %collective-permute-start = (bf16[4,256,64]{2,1,0:T(8,128)(2,1)}, bf16[4,256,64]{2,1,0:T(8,128)(2,1)}, u32[]{:S(2)}, u32[]{:S(2)}) collective-permute-start(bf16[4,256,64]{2,1,0:T(8,128)(2,1)} %bitcast.19), channel_id=1, source_target_pairs={{0,8},{2,10},{4,12},{6,14},{8,16},{10,18},{12,20},{14,22},{16,24},... | collective-permute-start | bytes 393224 | tf_op jit(solution)/shard_map/ppermute | solution.py:153
  24.2 3.3 %collective-permute-start.1 = (bf16[4,256,64]{2,1,0:T(8,128)(2,1)}, bf16[4,256,64]{2,1,0:T(8,128)(2,1)}, u32[]{:S(2)}, u32[]{:S(2)}) collective-permute-start(bf16[4,256,64]{2,1,0:T(8,128)(2,1)} %bitcast.19), channel_id=1, source_target_pairs={{0,6},{2,8},{4,10},{6,12},{8,14},{10,16},{12,18},{14,20},{16,22},{... | collective-permute-start | bytes 393224 | tf_op jit(solution)/shard_map/ppermute | solution.py:153
  27.5 3.4 %collective-permute-start.2 = (bf16[4,256,64]{2,1,0:T(8,128)(2,1)}, bf16[4,256,64]{2,1,0:T(8,128)(2,1)}, u32[]{:S(2)}, u32[]{:S(2)}) collective-permute-start(bf16[4,256,64]{2,1,0:T(8,128)(2,1)} %bitcast.19), channel_id=1, source_target_pairs={{0,4},{2,6},{4,8},{6,10},{8,12},{10,14},{12,16},{14,18},{16,20},{1... | collective-permute-start | bytes 393224 | tf_op jit(solution)/shard_map/ppermute | solution.py:153
  30.9 2.6 %collective-permute-start.3 = (bf16[4,256,64]{2,1,0:T(8,128)(2,1)}, bf16[4,256,64]{2,1,0:T(8,128)(2,1)}, u32[]{:S(2)}, u32[]{:S(2)}) collective-permute-start(bf16[4,256,64]{2,1,0:T(8,128)(2,1)} %bitcast.19), channel_id=1, source_target_pairs={{0,2},{2,4},{4,6},{6,8},{8,10},{10,12},{12,14},{14,16},{16,18},{18... | collective-permute-start | bytes 393224 | tf_op jit(solution)/shard_map/ppermute | solution.py:153
  36.9 4.1 %fusion.8 = f32[256,1024]{0,1:T(8,128)S(1)} fusion(bf16[2048,1024]{1,0:T(8,128)(2,1)} %param.13, f32[2048]{0:T(1024)} %copy-done.13, f32[256]{0:T(256)} %copy-done.17, bf16[256,2048]{1,0:T(8,128)(2,1)S(1)} %copy-done.2), kind=kOutput, calls=%fused_computation.21 | convolution fusion | flops 1075838976 | bytes 6300672 | tf_op jit(solution)/shard_map/dot_general | solution.py:216
  54.3 9.4 %shard_map.120 = (f32[2,2048,1]{2,1,0:T(8,128)}, f32[2,2048,1]{2,1,0:T(8,128)}, f32[2,2048,64]{2,1,0:T(8,128)}) custom-call(s32[8]{0:T(128)} %reshape.323.table, bf16[2,2048,64]{2,1,0:T(8,128)(2,1)} %bitcast.59, s32[2048,1]{1,0:T(8,128)} %broadcast_in_dim_reshape.13.rr_ref, s32[2048,1]{1,0:T(8,128)} %broadcast_in_dim_reshape.14.rp_ref, ...), custom_call_target="tpu_custom_call" | custom-call | tf_op jit(solution)/shard_map/pallas_call | solution.py:278
  63.7 11.7 %all-gather.2.cloned.1.call-done = bf16[4,4,2048,64]{2,3,0,1:T(8,128)(2,1)} async-done(((bf16[4,4,128,64]{2,3,0,1:T(8,128)(2,1)}), bf16[4,4,2048,64]{2,3,0,1:T(8,128)(2,1)}) %all-gather.2.cloned.1.call-update) | async-done | bytes 4194320 | tf_op jit(solution)/shard_map/all_gather | solution.py:183
  75.4 28.1 %shard_map.121 = bf16[2,2048,64]{2,1,0:T(8,128)(2,1)} custom-call(s32[8]{0:T(128)} %reshape.323.table, bf16[2,2048,64]{2,1,0:T(8,128)(2,1)} %bitcast.60, s32[2048,1]{1,0:T(8,128)} %broadcast_in_dim_reshape.12.rg_ref, bf16[4,4,64,2048]{3,2,1,0:T(8,128)(2,1)} %bitcast.57, bf16[4,4,64,2048]{3,2,1,0:T(8,128)(2,1)} %bitcast.58, ...), custom_call_target="tpu_custom_call" | custom-call | tf_op jit(solution)/shard_map/pallas_call | solution.py:296
  103.5 2.5 %copy.42 = bf16[2,256,8,64]{1,3,2,0:T(8,128)(2,1)} copy(bf16[2,256,8,64]{3,2,1,0:T(8,128)(2,1)} %bitcast.61) | data formatting | bytes 1048576 | tf_op jit(solution)/shard_map/reshape | solution.py:317
  106.0 3.4 %fusion.4 = bf16[256,1024]{1,0:T(8,128)(2,1)} fusion(bf16[256,1024]{0,1:T(8,128)(2,1)} %bitcast.62, bf16[1024,2048]{1,0:T(8,128)(2,1)} %param.15, s32[]{:T(128)S(6)} %select_n.107), kind=kOutput, calls=%fused_computation.11 | convolution fusion | flops 537133056 | bytes 3145732 | tf_op jit(solution)/shard_map/dot_general | solution.py:322
  110.8 1.6 convert_element_type.55
  112.4 11.4 %collective-permute-done.4 = bf16[256,1024]{1,0:T(8,128)(2,1)} collective-permute-done((bf16[256,1024]{1,0:T(8,128)(2,1)}, bf16[256,1024]{1,0:T(8,128)(2,1)}, u32[]{:S(2)}, u32[]{:S(2)}) %collective-permute-start.4) | collective-permute-done | bytes 524320 | tf_op jit(solution)/shard_map/ppermute | solution.py:327
  123.8 3.0 %add_convert_fusion = bf16[256,1024]{1,0:T(8,128)(2,1)S(1)} fusion(bf16[256,1024]{1,0:T(8,128)(2,1)} %collective-permute-done.4, f32[256,2048]{1,0:T(8,128)} %convert_element_type.55, s32[]{:T(128)S(6)} %select_n.94, bf16[256,1024]{0,1:T(8,128)(2,1)} %bitcast.63, bf16[1024,2048]{1,0:T(8,128)(2,1)} %param.15), kind=kOutput, calls=%fused_computation.14 | convolution fusion | flops 537919488 | bytes 4719616 | tf_op jit(solution)/shard_map/dot_general | solution.py:328
  128.5 4.2 %collective-permute-done.6 = bf16[32,1024]{1,0:T(8,128)(2,1)S(1)} collective-permute-done((bf16[32,1024]{1,0:T(8,128)(2,1)S(1)}, bf16[32,1024]{1,0:T(8,128)(2,1)S(1)}, u32[]{:S(2)}, u32[]{:S(2)}) %collective-permute-start.6) | collective-permute-done | bytes 65568 | tf_op jit(solution)/shard_map/ppermute | solution.py:144
  132.8 8.0 %collective-permute-start.7 = (bf16[32,1024]{1,0:T(8,128)(2,1)S(1)}, bf16[32,1024]{1,0:T(8,128)(2,1)S(1)}, u32[]{:S(2)}, u32[]{:S(2)}) collective-permute-start(bf16[32,1024]{1,0:T(8,128)(2,1)S(1)} %add.230), channel_id=1, source_target_pairs={{0,8},{2,10},{4,12},{6,14},{8,0},{10,2},{12,4},{14,6},{16,24},{18,... | collective-permute-start | bytes 196616 | tf_op jit(solution)/shard_map/ppermute | solution.py:144
  140.8 2.2 %collective-permute-done.7 = bf16[32,1024]{1,0:T(8,128)(2,1)S(1)} collective-permute-done((bf16[32,1024]{1,0:T(8,128)(2,1)S(1)}, bf16[32,1024]{1,0:T(8,128)(2,1)S(1)}, u32[]{:S(2)}, u32[]{:S(2)}) %collective-permute-start.7) | collective-permute-done | bytes 65568 | tf_op jit(solution)/shard_map/ppermute | solution.py:144
  143.1 2.0 %collective-permute-start.8 = (bf16[32,1024]{1,0:T(8,128)(2,1)S(1)}, bf16[32,1024]{1,0:T(8,128)(2,1)S(1)}, u32[]{:S(2)}, u32[]{:S(2)}) collective-permute-start(bf16[32,1024]{1,0:T(8,128)(2,1)S(1)} %add.231), channel_id=1, source_target_pairs={{0,16},{2,18},{4,20},{6,22},{8,24},{10,26},{12,28},{14,30},{16,0},... | collective-permute-start | bytes 196616 | tf_op jit(solution)/shard_map/ppermute | solution.py:144
  145.1 3.2 %collective-permute-done.8 = bf16[32,1024]{1,0:T(8,128)(2,1)S(1)} collective-permute-done((bf16[32,1024]{1,0:T(8,128)(2,1)S(1)}, bf16[32,1024]{1,0:T(8,128)(2,1)S(1)}, u32[]{:S(2)}, u32[]{:S(2)}) %collective-permute-start.8) | collective-permute-done | bytes 65568 | tf_op jit(solution)/shard_map/ppermute | solution.py:144
  148.3 4.9 %all_gather.7 = bf16[32,2048]{1,0:T(8,128)(2,1)S(1)} all-gather(bf16[32,1024]{1,0:T(8,128)(2,1)S(1)} %add.232), channel_id=1, replica_groups=mesh['seq'=16,'mp'=2] {'mp'}, dimensions={1}, use_global_device_ids=true | all-gather | bytes 196608 | tf_op jit(solution)/shard_map/all_gather | solution.py:348
  156.3 3.4 %collective-permute-done.10 = f32[32]{0:T(128)S(1)} collective-permute-done((f32[32]{0:T(128)S(1)}, f32[32]{0:T(128)S(1)}, u32[]{:S(2)}, u32[]{:S(2)}) %collective-permute-start.10) | collective-permute-done | bytes 160 | tf_op jit(solution)/shard_map/ppermute | solution.py:144
  159.7 2.0 %collective-permute-start.11 = (f32[32]{0:T(128)S(1)}, f32[32]{0:T(128)S(1)}, u32[]{:S(2)}, u32[]{:S(2)}) collective-permute-start(f32[32]{0:T(128)S(1)} %max.27), channel_id=1, source_target_pairs={{0,8},{2,10},{4,12},{6,14},{8,0},{10,2},{12,4},{14,6},{16,24},{18,... | collective-permute-start | bytes 392 | tf_op jit(solution)/shard_map/ppermute | solution.py:144
  161.7 1.5 collective-permute-done.11
  163.2 2.1 %collective-permute-start.12 = (f32[32]{0:T(128)S(1)}, f32[32]{0:T(128)S(1)}, u32[]{:S(2)}, u32[]{:S(2)}) collective-permute-start(f32[32]{0:T(128)S(1)} %max.28), channel_id=1, source_target_pairs={{0,16},{2,18},{4,20},{6,22},{8,24},{10,26},{12,28},{14,30},{16,0},... | collective-permute-start | bytes 392 | tf_op jit(solution)/shard_map/ppermute | solution.py:144
  165.3 2.3 %collective-permute-done.12 = f32[32]{0:T(128)S(1)} collective-permute-done((f32[32]{0:T(128)S(1)}, f32[32]{0:T(128)S(1)}, u32[]{:S(2)}, u32[]{:S(2)}) %collective-permute-start.12) | collective-permute-done | bytes 160 | tf_op jit(solution)/shard_map/ppermute | solution.py:144
  (129 shorter events, 38.0 us)
Async XLA Ops:
  7.2 68.2 %all-gather.2.cloned.1.call-start = ((), (), s32[]{:S(2)}) async-start(), calls=%async_computation | async-start | bytes 4456448 | tf_op jit(solution)/shard_map/all_gather | solution.py:183
  15.8 25.1 %copy-start.6 = (bf16[256,256]{1,0:T(8,128)(2,1)}, bf16[256,256]{1,0:T(8,128)(2,1)S(1)}, u32[]{:S(2)}) copy-start(bf16[256,256]{1,0:T(8,128)(2,1)S(1)} %copy.36) | copy-start | bytes 393220
  18.5 29.8 %collective-permute-start = (bf16[4,256,64]{2,1,0:T(8,128)(2,1)}, bf16[4,256,64]{2,1,0:T(8,128)(2,1)}, u32[]{:S(2)}, u32[]{:S(2)}) collective-permute-start(bf16[4,256,64]{2,1,0:T(8,128)(2,1)} %bitcast.19), channel_id=1, source_target_pairs={{0,8},{2,10},{4,12},{6,14},{8,16},{10,18},{12,20},{14,22},{16,24},... | collective-permute-start | bytes 393224 | tf_op jit(solution)/shard_map/ppermute | solution.py:153
  24.2 25.1 %collective-permute-start.1 = (bf16[4,256,64]{2,1,0:T(8,128)(2,1)}, bf16[4,256,64]{2,1,0:T(8,128)(2,1)}, u32[]{:S(2)}, u32[]{:S(2)}) collective-permute-start(bf16[4,256,64]{2,1,0:T(8,128)(2,1)} %bitcast.19), channel_id=1, source_target_pairs={{0,6},{2,8},{4,10},{6,12},{8,14},{10,16},{12,18},{14,20},{16,22},{... | collective-permute-start | bytes 393224 | tf_op jit(solution)/shard_map/ppermute | solution.py:153
  27.5 22.8 %collective-permute-start.2 = (bf16[4,256,64]{2,1,0:T(8,128)(2,1)}, bf16[4,256,64]{2,1,0:T(8,128)(2,1)}, u32[]{:S(2)}, u32[]{:S(2)}) collective-permute-start(bf16[4,256,64]{2,1,0:T(8,128)(2,1)} %bitcast.19), channel_id=1, source_target_pairs={{0,4},{2,6},{4,8},{6,10},{8,12},{10,14},{12,16},{14,18},{16,20},{1... | collective-permute-start | bytes 393224 | tf_op jit(solution)/shard_map/ppermute | solution.py:153
  30.9 20.4 %collective-permute-start.3 = (bf16[4,256,64]{2,1,0:T(8,128)(2,1)}, bf16[4,256,64]{2,1,0:T(8,128)(2,1)}, u32[]{:S(2)}, u32[]{:S(2)}) collective-permute-start(bf16[4,256,64]{2,1,0:T(8,128)(2,1)} %bitcast.19), channel_id=1, source_target_pairs={{0,2},{2,4},{4,6},{6,8},{8,10},{10,12},{12,14},{14,16},{16,18},{18... | collective-permute-start | bytes 393224 | tf_op jit(solution)/shard_map/ppermute | solution.py:153
  36.9 4.1 %copy-start.10 = (f32[256,32]{0,1:T(8,128)S(1)}, f32[256,32]{0,1:T(8,128)}, u32[]{:S(2)}) copy-start(f32[256,32]{0,1:T(8,128)} %copy-done.9) | copy-start | bytes 98308
  36.9 4.1 %copy-start.12 = (f32[256,32]{0,1:T(8,128)S(1)}, f32[256,32]{0,1:T(8,128)}, u32[]{:S(2)}) copy-start(f32[256,32]{0,1:T(8,128)} %copy-done.11) | copy-start | bytes 98308
  106.0 4.8 %copy-start.3 = (bf16[256,2048]{1,0:T(8,128)(2,1)S(1)}, bf16[256,2048]{1,0:T(8,128)(2,1)}, u32[]{:S(2)}) copy-start(bf16[256,2048]{1,0:T(8,128)(2,1)} %param.9) | copy-start | bytes 3145732
  109.4 14.4 %collective-permute-start.4 = (bf16[256,1024]{1,0:T(8,128)(2,1)}, bf16[256,1024]{1,0:T(8,128)(2,1)}, u32[]{:S(2)}, u32[]{:S(2)}) collective-permute-start(bf16[256,1024]{1,0:T(8,128)(2,1)} %fusion.4), channel_id=1, source_target_pairs={{0,1},{1,0},{2,3},{3,2},{4,5},{5,4},{6,7},{7,6},{8,9},{9,8},{10,11... | collective-permute-start | bytes 1572872 | tf_op jit(solution)/shard_map/ppermute | solution.py:327
  112.4 14.4 %copy-start.16 = (s32[32]{0:T(128)S(1)}, s32[32]{0:T(128)}, u32[]{:S(2)}) copy-start(s32[32]{0:T(128)} %get-tuple-element.18) | copy-start | bytes 388
  112.4 32.7 %copy-start.14 = (bf16[2048]{0:T(1024)(128)(2,1)S(1)}, bf16[2048]{0:T(1024)(128)(2,1)}, u32[]{:S(2)}) copy-start(bf16[2048]{0:T(1024)(128)(2,1)} %param.16) | copy-start | bytes 12292
  123.8 29.7 %copy-start.4 = (bf16[2048,1000]{0,1:T(8,128)(2,1)S(1)}, bf16[2048,1000]{0,1:T(8,128)(2,1)}, u32[]{:S(2)}) copy-start(bf16[2048,1000]{0,1:T(8,128)(2,1)} %param.17) | copy-start | bytes 12288004
  126.8 28.1 %copy-start.5 = (bf16[256,1024]{1,0:T(8,128)(2,1)}, bf16[256,1024]{1,0:T(8,128)(2,1)S(1)}, u32[]{:S(2)}) copy-start(bf16[256,1024]{1,0:T(8,128)(2,1)S(1)} %add_convert_fusion) | copy-start | bytes 1572868
  127.1 1.3 collective-permute-start.5
  128.4 4.3 %collective-permute-start.6 = (bf16[32,1024]{1,0:T(8,128)(2,1)S(1)}, bf16[32,1024]{1,0:T(8,128)(2,1)S(1)}, u32[]{:S(2)}, u32[]{:S(2)}) collective-permute-start(bf16[32,1024]{1,0:T(8,128)(2,1)S(1)} %add.229), channel_id=1, source_target_pairs={{0,4},{2,6},{4,0},{6,2},{8,12},{10,14},{12,8},{14,10},{16,20},{18,... | collective-permute-start | bytes 196616 | tf_op jit(solution)/shard_map/ppermute | solution.py:144
  132.8 10.3 %collective-permute-start.7 = (bf16[32,1024]{1,0:T(8,128)(2,1)S(1)}, bf16[32,1024]{1,0:T(8,128)(2,1)S(1)}, u32[]{:S(2)}, u32[]{:S(2)}) collective-permute-start(bf16[32,1024]{1,0:T(8,128)(2,1)S(1)} %add.230), channel_id=1, source_target_pairs={{0,8},{2,10},{4,12},{6,14},{8,0},{10,2},{12,4},{14,6},{16,24},{18,... | collective-permute-start | bytes 196616 | tf_op jit(solution)/shard_map/ppermute | solution.py:144
  143.1 5.2 %collective-permute-start.8 = (bf16[32,1024]{1,0:T(8,128)(2,1)S(1)}, bf16[32,1024]{1,0:T(8,128)(2,1)S(1)}, u32[]{:S(2)}, u32[]{:S(2)}) collective-permute-start(bf16[32,1024]{1,0:T(8,128)(2,1)S(1)} %add.231), channel_id=1, source_target_pairs={{0,16},{2,18},{4,20},{6,22},{8,24},{10,26},{12,28},{14,30},{16,0},... | collective-permute-start | bytes 196616 | tf_op jit(solution)/shard_map/ppermute | solution.py:144
  153.5 15.6 %copy-start.7 = (bf16[256,256]{1,0:T(8,128)(2,1)S(1)}, bf16[256,256]{1,0:T(8,128)(2,1)}, u32[]{:S(2)}) copy-start(bf16[256,256]{1,0:T(8,128)(2,1)} %copy-done.6) | copy-start | bytes 393220
  154.9 1.2 collective-permute-start.9
  156.1 3.5 %collective-permute-start.10 = (f32[32]{0:T(128)S(1)}, f32[32]{0:T(128)S(1)}, u32[]{:S(2)}, u32[]{:S(2)}) collective-permute-start(f32[32]{0:T(128)S(1)} %max.26), channel_id=1, source_target_pairs={{0,4},{2,6},{4,0},{6,2},{8,12},{10,14},{12,8},{14,10},{16,20},{18,... | collective-permute-start | bytes 392 | tf_op jit(solution)/shard_map/ppermute | solution.py:144
  159.7 3.5 %collective-permute-start.11 = (f32[32]{0:T(128)S(1)}, f32[32]{0:T(128)S(1)}, u32[]{:S(2)}, u32[]{:S(2)}) collective-permute-start(f32[32]{0:T(128)S(1)} %max.27), channel_id=1, source_target_pairs={{0,8},{2,10},{4,12},{6,14},{8,0},{10,2},{12,4},{14,6},{16,24},{18,... | collective-permute-start | bytes 392 | tf_op jit(solution)/shard_map/ppermute | solution.py:144
  163.2 4.4 %collective-permute-start.12 = (f32[32]{0:T(128)S(1)}, f32[32]{0:T(128)S(1)}, u32[]{:S(2)}, u32[]{:S(2)}) collective-permute-start(f32[32]{0:T(128)S(1)} %max.28), channel_id=1, source_target_pairs={{0,16},{2,18},{4,20},{6,22},{8,24},{10,26},{12,28},{14,30},{16,0},... | collective-permute-start | bytes 392 | tf_op jit(solution)/shard_map/ppermute | solution.py:144
  167.7 3.5 %collective-permute-start.13 = (f32[32]{0:T(128)S(1)}, f32[32]{0:T(128)S(1)}, u32[]{:S(2)}, u32[]{:S(2)}) collective-permute-start(f32[32]{0:T(128)S(1)} %max.29), channel_id=1, source_target_pairs={{0,1},{1,0},{2,3},{3,2},{4,5},{5,4},{6,7},{7,6},{8,9},{9,8},{10,11... | collective-permute-start | bytes 392 | tf_op jit(solution)/shard_map/ppermute | solution.py:144
  (9 other events, 13.7 us)
Sparse Core Ops, SparseCore 0:
  10.8 64.6 all-gather.1
